TPU v7x, 512 devices: a whole 4x4x16 slice. The times are simulated.
512 devices in a mesh: cols: 128 (over x, z, core), mem: 4 (over y).
Axes of the slice: x: 4, y: 4, z: 16, core: 2. Of those that a mesh axis runs over, the one named last changes fastest.
Arguments:
- column_profiles: bfloat16 [2048, 100, 512], P('cols', None, 'mem'), may hold values from -6 to 6
- w_in: bfloat16 [100, 256], replicated, may hold values from -0.625 to 0.625
- w_depth: float32 [3, 256], replicated, may hold values from -3 to 3
- w_out: bfloat16 [256, 100], replicated, may hold values from -0.375 to 0.375
- obs_op: float32 [100, 16], replicated, may hold values from -0.625 to 0.625
- foot: int32 [16384, 4], P('cols'), may hold values from -1 to 15, as said below
- owner: int32 [16384, 1], P('cols'), may hold values from 0 to 127; in each aligned block of 128 rows (0 to 127, 128 to 255, ...) at most 2 rows name the same one
- obs: float32 [16384, 16], P('cols'), may hold values from -6 to 6
- rinv: float32 [16384, 16], P('cols'), may hold values from 0.5 to 4
- inflation: float32 [128], P('cols'), may hold values from 0.5 to 2
Outputs:
- analysis: bfloat16 [2048, 100, 512], P('cols', None, 'mem')
Inputs may be any that keep to these rules, and one draw needn't show every extreme that they name: `foot`: the first slot of every batch is a column of its source; other slots are a column or -1. Among the 128 batches of one index of cols, no owner appears more than 2 times.
All inputs are finite; a program needn't handle non-finite values.
Results may differ from a plain program's by a relative error of at most 0.01.
Values may be sent and summed in bfloat16 or wider, within the bound.
No kernel may reach another device: no remote copies, remote signals or barrier semaphores. Data moves between devices by JAX's collectives and lax.ppermute only.
A program may use at most 64 MiB of HBM per device.

v0:
```python
import math

import jax
import jax.numpy as jnp
from jax import lax
from jax.sharding import PartitionSpec as P


def extended(block, sides, width):
    for axis, dim in sides:
        count = lax.axis_size(axis)
        forward = [(i, i + 1) for i in range(count - 1)]
        backward = [(target, source) for source, target in forward]
        low = lax.ppermute(
            lax.slice_in_dim(block, block.shape[dim] - width, None, axis=dim), axis, forward
        )
        high = lax.ppermute(lax.slice_in_dim(block, 0, width, axis=dim), axis, backward)
        block = jnp.concatenate([low, block, high], axis=dim)
    return block


def sent_to_all(shard, axis):
    peers = lax.axis_size(axis)
    return lax.all_to_all(
        jnp.broadcast_to(shard[None], (peers, *shard.shape)), axis, 0, 0, tiled=True
    )


def taken_together(shard, axis):
    everything = sent_to_all(shard, axis)
    return jnp.sum(everything, axis=0)


def in_one_piece(arrays, axis, split_dim, concat_dim, along):
    columns = [a.reshape(*a.shape[:along], -1) for a in arrays]
    both = jnp.concatenate(columns, axis=along)
    out, at, done = (
        lax.all_to_all(both, axis, split_axis=split_dim, concat_axis=concat_dim, tiled=True),
        0,
        [],
    )
    for a, column in zip(arrays, columns):
        section = out[..., at : at + column.shape[along]]
        done.append(section.reshape(*section.shape[:along], *a.shape[along:]))
        at += column.shape[along]
    return tuple(done)


def in_one_piece_2(arrays, axis, split_dim, concat_dim, along):
    ends, at = ([], 0)
    for a in arrays[:-1]:
        at += a.shape[along]
        ends.append(at)
    both = jnp.concatenate(arrays, axis=along)
    return tuple(
        jnp.split(
            lax.all_to_all(both, axis, split_axis=split_dim, concat_axis=concat_dim, tiled=True),
            ends,
            axis=along,
        )
    )


def together(arrays, axis):
    ravelled, at, done = (jnp.concatenate([a.reshape(-1) for a in arrays]), 0, [])
    subtotal = lax.psum(ravelled, axis)
    for a in arrays:
        done.append(subtotal[at : at + a.size].reshape(a.shape))
        at += a.size
    return tuple(done)


def joined_along(parts, dim):
    parts = jnp.moveaxis(parts, 0, dim)
    lengths = parts.shape
    return parts.reshape(*lengths[:dim], lengths[dim] * lengths[dim + 1], *lengths[dim + 2 :])


def collect(shard, axis, dim):
    return joined_along(sent_to_all(shard, axis), dim)


def factor_block(block):
    top = lax.Precision.HIGHEST
    width = block.shape[0]
    places = jnp.arange(width, dtype=jnp.int32)

    def advance(index, carry):
        lower, inverse = carry
        column = lax.dynamic_slice_in_dim(block, index, 1, 1)[:, 0]
        known = lax.dynamic_slice_in_dim(lower, index, 1, 0)[0]
        value = column - jnp.dot(lower, known, precision=top)
        pivot = jnp.sqrt(jnp.sum(jnp.where(places == index, value, 0.0)))
        fresh = jnp.where(places >= index, value / pivot, 0.0)
        lower = lower + fresh[:, None] * (places[None, :] == index).astype(jnp.float32)
        full_row = lax.dynamic_slice_in_dim(lower, index, 1, 0)[0]
        strict_row = jnp.where(places < index, full_row, 0.0)
        unit = (places == index).astype(jnp.float32)
        inverse_row = (unit - jnp.dot(strict_row, inverse, precision=top)) / pivot
        inverse = inverse + (places[:, None] == index).astype(jnp.float32) * inverse_row[None, :]
        return (lower, inverse)

    start = (jnp.zeros((width, width), jnp.float32), jnp.zeros((width, width), jnp.float32))
    return lax.fori_loop(0, width, advance, start)


def factor_inverse(gram):
    top = lax.Precision.HIGHEST
    order = gram.shape[0]
    step_size = min(128, order)
    identity = jnp.eye(order, dtype=jnp.float32)
    chol = jnp.zeros((order, order), jnp.float32)
    chol_inverse = jnp.zeros((order, order), jnp.float32)
    for block_index in range(order // step_size):
        begin = block_index * step_size
        finish = begin + step_size
        panel = gram[begin:, begin:finish]
        if block_index > 0:
            panel = panel - jnp.dot(
                chol[begin:, :begin], chol[begin:finish, :begin].T, precision=top
            )
        diag_low, diag_inverse = factor_block(panel[:step_size])
        below = jnp.dot(panel[step_size:], diag_inverse.T, precision=top)
        chol = chol.at[begin:, begin:finish].set(jnp.concatenate([diag_low, below], axis=0))
        right_side = identity[begin:finish]
        if block_index > 0:
            right_side = right_side - jnp.dot(
                chol[begin:finish, :begin], chol_inverse[:begin], precision=top
            )
        chol_inverse = chol_inverse.at[begin:finish].set(
            jnp.dot(diag_inverse, right_side, precision=top)
        )
    return chol_inverse


def body(column_profiles, w_in, w_depth, w_out, obs_op, foot, owner, obs, rinv, inflation):
    top = lax.Precision.HIGHEST
    n_cols = lax.axis_size("cols")
    n_mem = lax.axis_size("mem")
    mem_dev = column_profiles.shape[2]
    members = mem_dev * n_mem
    src_b = foot.shape[0]
    col_dev = column_profiles.shape[0]
    widened = extended(column_profiles, (("cols", 0),), 1)
    hidden = jax.nn.gelu(
        jnp.einsum("kcm,ch->khm", widened, w_in, preferred_element_type=jnp.float32)
    ).astype(jnp.bfloat16)
    mixed = (
        w_depth[0][None, :, None] * hidden[:-2]
        + w_depth[1][None, :, None] * hidden[1:-1]
        + w_depth[2][None, :, None] * hidden[2:]
    ).astype(jnp.bfloat16)
    predicted_column = column_profiles.astype(jnp.float32) + jnp.einsum(
        "khm,hc->kcm", mixed, w_out, preferred_element_type=jnp.float32
    )
    grand_accumulation = taken_together(jnp.sum(predicted_column, axis=2), "mem")
    profile_average = grand_accumulation / members
    departure_from_average = predicted_column - profile_average[:, :, None]
    pobs = jnp.einsum("kcm,co->kom", departure_from_average, obs_op, precision=top)
    mobs = jnp.dot(profile_average, obs_op, precision=top)
    hits = (foot[:, :, None] == jnp.arange(col_dev, dtype=jnp.int32)[None, None, :]).astype(
        jnp.float32
    )
    counts = jnp.sum((foot >= 0).astype(jnp.float32), axis=1)
    onehot = jnp.sum(hits, axis=1) / counts[:, None]
    fpert = jnp.einsum("bk,kom->bom", onehot, pobs, precision=top)
    fmean = jnp.dot(onehot, mobs, precision=top)
    scale = 1.0 / math.sqrt(members - 1)
    spread = (rinv[:, :, None] * fpert * scale).astype(jnp.bfloat16)
    innov = (rinv * (obs - fmean)).astype(jnp.bfloat16)
    target = owner[:, 0]
    capacity = max(2, 2 * src_b // n_cols)
    owner_hits = (target[:, None] == jnp.arange(n_cols, dtype=jnp.int32)[None, :]).astype(jnp.int32)
    ranking = jnp.sum((jnp.cumsum(owner_hits, axis=0) - 1) * owner_hits, axis=1)
    slot = target * capacity + ranking
    placing = (slot[:, None] == jnp.arange(n_cols * capacity, dtype=jnp.int32)[None, :]).astype(
        jnp.bfloat16
    )
    send_spread = jnp.einsum(
        "bq,bom->qom", placing, spread, preferred_element_type=jnp.float32
    ).astype(jnp.bfloat16)
    send_innov = jnp.einsum("bq,bo->qo", placing, innov, preferred_element_type=jnp.float32).astype(
        jnp.bfloat16
    )
    held_spread, held_innov = in_one_piece((send_spread, send_innov), "cols", 0, 0, 2)
    held_factor = jnp.full((held_spread.shape[0],), inflation[0] * inflation[0], jnp.float32)
    quarter = held_spread.shape[0] // n_mem
    factor_grid = jnp.broadcast_to(held_factor[:, None, None], held_spread.shape)
    portion, factor_part = tuple(
        (
            part.astype(jnp.float32)
            for part in in_one_piece_2(
                (
                    held_spread.astype(jnp.float32).astype(jnp.bfloat16),
                    factor_grid.astype(jnp.bfloat16),
                ),
                "mem",
                0,
                2,
                1,
            )
        )
    )
    innov_part = lax.dynamic_slice_in_dim(held_innov, lax.axis_index("mem") * quarter, quarter, 0)
    weighted = portion * factor_part
    whole = jnp.einsum("qom,qoj->mj", weighted, portion, precision=top)
    vector = jnp.einsum("qom,qo->m", weighted, innov_part.astype(jnp.float32), precision=top)
    gram_part, vec_all = together((whole, vector), ("cols", "mem"))
    gram = jnp.eye(members, dtype=jnp.float32) + gram_part
    chol_inverse = factor_inverse(gram)
    weights = jnp.dot(chol_inverse.T, jnp.dot(chol_inverse, vec_all, precision=top), precision=top)
    first = lax.axis_index("mem") * mem_dev
    tinv_mine = lax.dynamic_slice_in_dim(chol_inverse, first, mem_dev, 0).T
    mix_w = (weights[:, None] * scale + tinv_mine).astype(jnp.bfloat16)
    pertb = departure_from_average.astype(jnp.bfloat16)
    moved = jnp.einsum(
        "kcm,mj->kcj", collect(pertb, "mem", 2), mix_w, preferred_element_type=jnp.float32
    )
    return (profile_average[:, :, None] + moved).astype(jnp.bfloat16)


def solution(mesh):
    placed = (
        P("cols", None, "mem"),
        P(),
        P(),
        P(),
        P(),
        P("cols", None),
        P("cols", None),
        P("cols", None),
        P("cols", None),
        P("cols"),
    )
    return jax.shard_map(
        body, mesh=mesh, in_specs=placed, out_specs=P("cols", None, "mem"), check_vma=False
    )
```

profile of v0, /device:TPU:1, one launch (start us, length us, event | category | flops | bytes accessed | tf_op | source)
XLA Modules:
  0.0 1697.3 jit_solution(2422012358642895942)
XLA Ops:
  7.7 4.9 collective-permute-start
  12.6 5.1 collective-permute-start.1
  24.2 3.3 all-to-all-start
  27.5 4.4 all-to-all-done
  35.9 3.0 copy.69
  38.9 19.3 %all-to-all-start.2 = ((bf16[256,16,129]{2,1,0:T(8,128)(2,1)}), bf16[256,16,129]{2,1,0:T(8,128)(2,1)S(1)}, u32[]{:S(2)}, u32[]{:S(2)}) async-start(bf16[256,16,129]{2,1,0:T(8,128)(2,1)} %copy.69), calls=%async_computation.2 | async-start | bytes 4194304 | tf_op jit(solution)/shard_map/all_to_all | solution.py:38
  58.8 98.5 %all-to-all-done.2 = bf16[256,16,129]{2,1,0:T(8,128)(2,1)S(1)} async-done(((bf16[256,16,129]{2,1,0:T(8,128)(2,1)}), bf16[256,16,129]{2,1,0:T(8,128)(2,1)S(1)}, u32[]{:S(2)}, u32[]{:S(2)}) %all-to-all-start.2) | async-done | bytes 1056800 | tf_op jit(solution)/shard_map/all_to_all | solution.py:38
  157.5 1.8 concatenate.39
  159.3 3.6 all-to-all-start.3
  164.2 24.5 %all-to-all-done.3 = bf16[256,32,128]{2,1,0:T(8,128)(2,1)S(1)} async-done(((bf16[256,32,128]{2,1,0:T(8,128)(2,1)}), bf16[256,32,128]{2,1,0:T(8,128)(2,1)S(1)}, u32[]{:S(2)}, u32[]{:S(2)}) %all-to-all-start.3) | async-done | bytes 2097184 | tf_op jit(solution)/shard_map/all_to_all | solution.py:57
  188.7 1.4 broadcast_in_dim.108
  190.2 4.3 all-to-all-start.1
  194.6 3.0 copy.70
  197.5 2.7 all_to_all.28
  200.3 1.9 fusion.78
  205.4 1.1 fusion.106
  206.5 8.1 all-to-all-done.1
  214.7 3.9 copy.80
  218.6 2.8 reshape.344
  221.4 451.8 %all-reduce.5.cloned.1.call-done = f32[262656]{0:T(1024)} async-done(((f32[262656]{0:T(1024)}), f32[262656]{0:T(1024)}) %all-reduce.5.cloned.1.call-update) | async-done | bytes 1050640 | tf_op jit(solution)/shard_map/psum | solution.py:66
  673.3 2.3 slice.308
  675.5 2.4 slice.277
  677.9 1.3 convert_add_fusion
  680.3 249.9 %while.76 = (s32[]{:T(128)}, f32[128,128]{1,0:T(8,128)S(1)}, f32[128,128]{1,0:T(8,128)S(1)}, f32[128,128]{0,1:T(8,128)S(1)}, s32[]{:T(128)}, /*index=5*/s32[]{:T(128)}) while((s32[]{:T(128)}, f32[128,128]{1,0:T(8,128)S(1)}, f32[128,128]{1,0:T(8,128)S(1)}, f32[128,128]{0,1:T(8,128)S(1)}, s32[]{:T(128)}, ...), condition=%wide.region_9.10_spmd.clone.clone, body=%wide.region_7.9_spmd.clone.clone.sunk | while | flops 526210 | bytes 533614 | solution.py:104
  930.2 1.3 fusion.112
  932.1 1.3 convolution_subtract_fusion.3
  934.5 248.2 %while.77 = (s32[]{:T(128)}, f32[128,128]{1,0:T(8,128)S(1)}, f32[128,128]{1,0:T(8,128)S(1)}, f32[128,128]{0,1:T(8,128)S(1)}, s32[]{:T(128)}, /*index=5*/s32[]{:T(128)}) while((s32[]{:T(128)}, f32[128,128]{1,0:T(8,128)S(1)}, f32[128,128]{1,0:T(8,128)S(1)}, f32[128,128]{0,1:T(8,128)S(1)}, s32[]{:T(128)}, ...), condition=%wide.region_13.14_spmd.clone.clone, body=%wide.region_11.13_spmd.clone.clone.sunk | while | flops 526210 | bytes 533614 | solution.py:104
  1183.7 1.4 convolution_subtract_fusion.4
  1185.3 248.2 %while.78 = (s32[]{:T(128)}, f32[128,128]{1,0:T(8,128)S(1)}, f32[128,128]{1,0:T(8,128)S(1)}, f32[128,128]{0,1:T(8,128)S(1)}, s32[]{:T(128)}, /*index=5*/s32[]{:T(128)}) while((s32[]{:T(128)}, f32[128,128]{1,0:T(8,128)S(1)}, f32[128,128]{1,0:T(8,128)S(1)}, f32[128,128]{0,1:T(8,128)S(1)}, s32[]{:T(128)}, ...), condition=%wide.region_16.17_spmd.clone.clone, body=%wide.region_14.16_spmd.clone.clone.sunk | while | flops 526210 | bytes 533614 | solution.py:104
  1434.2 1.4 convolution_subtract_fusion.1
  1435.9 1.2 convolution_subtract_fusion.5
  1438.7 248.2 %while.79 = (s32[]{:T(128)}, f32[128,128]{1,0:T(8,128)S(1)}, f32[128,128]{1,0:T(8,128)S(1)}, f32[128,128]{0,1:T(8,128)S(1)}, s32[]{:T(128)}, /*index=5*/s32[]{:T(128)}) while((s32[]{:T(128)}, f32[128,128]{1,0:T(8,128)S(1)}, f32[128,128]{1,0:T(8,128)S(1)}, f32[128,128]{0,1:T(8,128)S(1)}, s32[]{:T(128)}, ...), condition=%wide.region_19.20_spmd.clone.clone, body=%wide.region_17.19_spmd.clone.clone.sunk | while | flops 526210 | bytes 533614 | solution.py:104
  (3680 shorter events, 637.7 us)
Async XLA Ops:
  6.5 15.1 copy-start
  7.7 14.0 collective-permute-start
  12.6 9.1 collective-permute-start.1
  21.6 1.0 copy-start.5
  21.6 1.0 copy-start.8
  22.7 4.7 copy-start.7
  22.7 9.2 copy-start.6
  22.7 10.0 copy-start.9
  24.2 7.7 all-to-all-start
  34.6 0.7 copy-start.10
  38.9 118.5 %all-to-all-start.2 = ((bf16[256,16,129]{2,1,0:T(8,128)(2,1)}), bf16[256,16,129]{2,1,0:T(8,128)(2,1)S(1)}, u32[]{:S(2)}, u32[]{:S(2)}) async-start(bf16[256,16,129]{2,1,0:T(8,128)(2,1)} %copy.69), calls=%async_computation.2 | async-start | bytes 4194304 | tf_op jit(solution)/shard_map/all_to_all | solution.py:38
  157.4 2.0 copy-start.1
  159.3 29.4 %all-to-all-start.3 = ((bf16[256,32,128]{2,1,0:T(8,128)(2,1)}), bf16[256,32,128]{2,1,0:T(8,128)(2,1)S(1)}, u32[]{:S(2)}, u32[]{:S(2)}) async-start(bf16[256,32,128]{2,1,0:T(8,128)(2,1)} %concatenate.39), calls=%async_computation.3 | async-start | bytes 4194304 | tf_op jit(solution)/shard_map/all_to_all | solution.py:57
  162.9 1.2 slice-start
  190.2 24.5 %all-to-all-start.1 = ((bf16[4,16,100,128]{3,1,2,0:T(8,128)(2,1)}), bf16[4,16,100,128]{3,1,2,0:T(8,128)(2,1)}, u32[]{:S(2)}, u32[]{:S(2)}) async-start(bf16[4,16,100,128]{3,1,2,0:T(8,128)(2,1)} %broadcast_in_dim.108), calls=%async_computation.1 | async-start | bytes 3276800 | tf_op jit(solution)/shard_map/all_to_all | solution.py:24
  194.5 478.7 %all-reduce.5.cloned.1.call-start = ((), (), s32[]{:S(2)}) async-start(), calls=%async_computation.4 | async-start | bytes 2105344 | tf_op jit(solution)/shard_map/psum | solution.py:66
  679.2 1.0 copy-start.4
  1433.5 2.4 copy-start.2
  1433.5 3.7 copy-start.3
  1438.6 248.7 %slice-start.1 = ((f32[262656]{0:T(1024)}), f32[512]{0:T(512)S(1)}, s32[]{:S(2)}) async-start(f32[262656]{0:T(1024)} %all-reduce.5.cloned.1.call-done), calls=%async_computation.6 | async-start | bytes 4096 | tf_op jit(solution)/shard_map/slice | solution.py:68
Sparse Core Ops, SparseCore 0:
  204.7 468.5 all-reduce.4
where the time goes:
time: 1700 us
  waiting for transfers between devices  587 us (35%)
  matrix products  525 us (31%)
  loops' own time  383 us (23%)
  other arithmetic  115 us (7%)
  starting transfers between devices  40.6 us (2%)
  local copies, waits for them, and re-layouts  31.6 us (2%)
    psum x1, waiting for transfers between devices, together(): subtotal = lax.psum(ravelled, axis)  452 us
    dot_general x512, matrix products, advance(): value = column - jnp.dot(lower, known, precision=top)  424 us
    another operation x4, loops' own time, factor_block(): return lax.fori_loop(0, width, advance, start)  383 us
    all_to_all x1, waiting for transfers between devices, in_one_piece(): lax.all_to_all(both, axis, split_axis=split_dim, concat_axis=concat_dim,...  98.5 us
    dot_general x512, matrix products, advance(): inverse_row = (unit - jnp.dot(strict_row, inverse, precision=top)) / pivot  81.4 us
    add x512, other arithmetic, advance(): inverse + (places[:, None] == index).astype(jnp.float32) * inverse_row[No...  53.6 us
    add x512, other arithmetic, advance(): lower + fresh[:, None] * (places[None, :] == index).astype(jnp.float32)  43.4 us
  transfers between devices with their start and end apart: 7, of which 5 were waited for; matrix products, arithmetic and copies ran while one was open for 1% of the time, Pallas kernels for 0%

commit v1 on v0

--- a/solution.py
+++ b/solution.py
@@ -3,6 +3,8 @@
 import jax
 import jax.numpy as jnp
 from jax import lax
+from jax.experimental import pallas as pl
+from jax.experimental.pallas import tpu as pltpu
 from jax.sharding import PartitionSpec as P
 
 
@@ -80,28 +82,44 @@
     return joined_along(sent_to_all(shard, axis), dim)
 
 
+def _eliminate(a_ref, low_ref, inv_ref, m_ref):
+    n = a_ref.shape[0]
+    sub = lax.broadcasted_iota(jnp.int32, (n, 1), 0)
+    lane = lax.broadcasted_iota(jnp.int32, (1, n), 1)
+    rows = lax.broadcasted_iota(jnp.int32, (n, n), 0)
+    cols = lax.broadcasted_iota(jnp.int32, (n, n), 1)
+    m_ref[:, :n] = a_ref[...]
+    m_ref[:, n:] = (rows == cols).astype(jnp.float32)
+
+    def step(j, carry):
+        row = m_ref[pl.ds(j, 1), :]
+        whole = m_ref[...]
+        column = jnp.sum(jnp.where(lane == j, whole[:, :n], 0.0), axis=1, keepdims=True)
+        pivot = jnp.sum(jnp.where(lane == j, row[:, :n], 0.0), axis=1, keepdims=True)
+        factor = jnp.where(sub > j, column / pivot, 0.0)
+        m_ref[...] = whole - factor * row
+        return carry
+
+    lax.fori_loop(0, n, step, 0)
+    whole = m_ref[...]
+    diag = jnp.sum(jnp.where(rows == cols, whole[:, :n], 0.0), axis=1, keepdims=True)
+    scale = 1.0 / jnp.sqrt(diag)
+    low_ref[...] = jnp.where(rows <= cols, whole[:, :n] * scale, 0.0)
+    inv_ref[...] = whole[:, n:] * scale
+
+
 def factor_block(block):
-    top = lax.Precision.HIGHEST
     width = block.shape[0]
-    places = jnp.arange(width, dtype=jnp.int32)
-
-    def advance(index, carry):
-        lower, inverse = carry
-        column = lax.dynamic_slice_in_dim(block, index, 1, 1)[:, 0]
-        known = lax.dynamic_slice_in_dim(lower, index, 1, 0)[0]
-        value = column - jnp.dot(lower, known, precision=top)
-        pivot = jnp.sqrt(jnp.sum(jnp.where(places == index, value, 0.0)))
-        fresh = jnp.where(places >= index, value / pivot, 0.0)
-        lower = lower + fresh[:, None] * (places[None, :] == index).astype(jnp.float32)
-        full_row = lax.dynamic_slice_in_dim(lower, index, 1, 0)[0]
-        strict_row = jnp.where(places < index, full_row, 0.0)
-        unit = (places == index).astype(jnp.float32)
-        inverse_row = (unit - jnp.dot(strict_row, inverse, precision=top)) / pivot
-        inverse = inverse + (places[:, None] == index).astype(jnp.float32) * inverse_row[None, :]
-        return (lower, inverse)
-
-    start = (jnp.zeros((width, width), jnp.float32), jnp.zeros((width, width), jnp.float32))
-    return lax.fori_loop(0, width, advance, start)
+    symmetric = jnp.tril(block) + jnp.tril(block, -1).T
+    square = jax.ShapeDtypeStruct((width, width), jnp.float32)
+    upper, inverse = pl.pallas_call(
+        _eliminate,
+        out_shape=(square, square),
+        in_specs=[pl.BlockSpec(memory_space=pltpu.VMEM)],
+        out_specs=(pl.BlockSpec(memory_space=pltpu.VMEM), pl.BlockSpec(memory_space=pltpu.VMEM)),
+        scratch_shapes=[pltpu.VMEM((width, 2 * width), jnp.float32)],
+    )(symmetric)
+    return upper.T, inverse
 
 
 def factor_inverse(gram):

time: 1700 us -> 774 us (0.46)
  matrix products: 525 us -> 24.3 us
  loops' own time: 383 us -> 0 us
  other arithmetic: 115 us -> 12.3 us
  Pallas kernels: 0 us -> 61.1 us
    dot_general x1024 -> x0, matrix products: 506 us -> none  [the longest x512 424 us: advance(): value = column - jnp.dot(lower, known, precision=top)]
    another operation x4 -> x0, loops' own time: 383 us -> none  [factor_block(): return lax.fori_loop(0, width, advance, start)]
    add x1024 -> x5, other arithmetic: 97 us -> 2.76 us  [factor_block(): symmetric = jnp.tril(block) + jnp.tril(block, -1).T]
    pallas_call x0 -> x4, Pallas kernels: none -> 61.1 us  [factor_block(): pl.pallas_call(_eliminate, out_shape=(square, square), in_specs=[pl.Block...]
  transfers between devices with their start and end apart: 7 -> 7, of which waited for: 5 -> 5; matrix products, arithmetic and copies ran while one was open for 1% -> 3% of each run, Pallas kernels for 0% -> 0%
where the time goes in v1:
time: 774 us; the launch traced here: 772 us
  waiting for transfers between devices  587 us (76%)
  Pallas kernels  61.1 us (8%)
  starting transfers between devices  40.9 us (5%)
  local copies, waits for them, and re-layouts  32.1 us (4%)
  matrix products  24.3 us (3%)
  between operations  14.7 us (2%)
  other arithmetic  12.3 us (2%)
    psum x1, waiting for transfers between devices, together(): subtotal = lax.psum(ravelled, axis)  452 us
    all_to_all x1, waiting for transfers between devices, in_one_piece(): lax.all_to_all(both, axis, split_axis=split_dim, concat_axis=concat_dim,...  98.5 us
    pallas_call x4, Pallas kernels, factor_block(): pl.pallas_call(_eliminate, out_shape=(square, square), in_specs=[pl.Block...  61.1 us
    all_to_all x1, waiting for transfers between devices, in_one_piece_2(): lax.all_to_all(both, axis, split_axis=split_dim, concat_axis=concat_dim,...  24.5 us
    all_to_all x1, starting transfers between devices, in_one_piece(): lax.all_to_all(both, axis, split_axis=split_dim, concat_axis=concat_dim,...  19.3 us
  transfers between devices with their start and end apart: 7, of which 5 were waited for; matrix products, arithmetic and copies ran while one was open for 3% of the time, Pallas kernels for 0%

profile of v1, /device:TPU:1, one launch (start us, length us, event | category | flops | bytes accessed | tf_op | source)
XLA Modules:
  0.0 772.5 jit_solution(2682262679582904577)
XLA Ops:
  7.7 4.9 collective-permute-start
  12.6 5.1 collective-permute-start.1
  24.2 3.3 all-to-all-start
  27.5 4.4 all-to-all-done
  35.3 3.0 copy.110
  38.3 19.3 %all-to-all-start.2 = ((bf16[256,16,129]{2,1,0:T(8,128)(2,1)}), bf16[256,16,129]{2,1,0:T(8,128)(2,1)S(1)}, u32[]{:S(2)}, u32[]{:S(2)}) async-start(bf16[256,16,129]{2,1,0:T(8,128)(2,1)} %copy.110), calls=%async_computation.2 | async-start | bytes 4194304 | tf_op jit(solution)/shard_map/all_to_all | solution.py:40
  58.3 98.5 %all-to-all-done.2 = bf16[256,16,129]{2,1,0:T(8,128)(2,1)S(1)} async-done(((bf16[256,16,129]{2,1,0:T(8,128)(2,1)}), bf16[256,16,129]{2,1,0:T(8,128)(2,1)S(1)}, u32[]{:S(2)}, u32[]{:S(2)}) %all-to-all-start.2) | async-done | bytes 1056800 | tf_op jit(solution)/shard_map/all_to_all | solution.py:40
  157.0 1.8 concatenate.39
  158.8 3.6 all-to-all-start.3
  163.7 24.5 %all-to-all-done.3 = bf16[256,32,128]{2,1,0:T(8,128)(2,1)S(1)} async-done(((bf16[256,32,128]{2,1,0:T(8,128)(2,1)}), bf16[256,32,128]{2,1,0:T(8,128)(2,1)S(1)}, u32[]{:S(2)}, u32[]{:S(2)}) %all-to-all-start.3) | async-done | bytes 2097184 | tf_op jit(solution)/shard_map/all_to_all | solution.py:59
  188.2 1.4 broadcast_in_dim.17
  189.7 4.4 all-to-all-start.1
  194.3 3.0 copy.111
  197.2 2.7 all_to_all.28
  200.0 1.9 fusion.10
  206.3 7.9 %all-to-all-done.1 = bf16[4,16,100,128]{3,1,2,0:T(8,128)(2,1)} async-done(((bf16[4,16,100,128]{3,1,2,0:T(8,128)(2,1)}), bf16[4,16,100,128]{3,1,2,0:T(8,128)(2,1)}, u32[]{:S(2)}, u32[]{:S(2)}) %all-to-all-start.1) | async-done | bytes 1638432 | tf_op jit(solution)/shard_map/all_to_all | solution.py:26
  214.2 3.9 copy.144
  218.1 2.8 reshape.256
  220.9 451.8 %all-reduce.5.cloned.1.call-done = f32[262656]{0:T(1024)} async-done(((f32[262656]{0:T(1024)}), f32[262656]{0:T(1024)}) %all-reduce.5.cloned.1.call-update) | async-done | bytes 1050640 | tf_op jit(solution)/shard_map/psum | solution.py:68
  672.8 2.3 slice.308
  675.0 1.4 slice.277
  677.8 1.3 convert_add_fusion
  680.0 15.2 %shard_map.100 = (f32[128,128]{1,0:T(8,128)}, f32[128,128]{1,0:T(8,128)}) custom-call(f32[128,128]{1,0:T(8,128)} %bitcast_add_fusion.3.a_ref), custom_call_target="tpu_custom_call" | custom-call | tf_op jit(solution)/shard_map/pallas_call | solution.py:115
  696.2 1.4 fusion.44
  699.9 15.2 %shard_map.101 = (f32[128,128]{1,0:T(8,128)}, f32[128,128]{1,0:T(8,128)}) custom-call(f32[128,128]{1,0:T(8,128)} %bitcast_add_fusion.2.a_ref), custom_call_target="tpu_custom_call" | custom-call | tf_op jit(solution)/shard_map/pallas_call | solution.py:115
  717.3 1.4 convolution_subtract_fusion.4
  719.5 15.2 %shard_map.102 = (f32[128,128]{1,0:T(8,128)}, f32[128,128]{1,0:T(8,128)}) custom-call(f32[128,128]{1,0:T(8,128)} %bitcast_add_fusion.1.a_ref), custom_call_target="tpu_custom_call" | custom-call | tf_op jit(solution)/shard_map/pallas_call | solution.py:115
  736.9 1.6 convolution_subtract_fusion.1
  739.2 1.4 broadcast_select_fusion
  741.3 15.4 %shard_map.103 = (f32[128,128]{1,0:T(8,128)}, f32[128,128]{1,0:T(8,128)}) custom-call(f32[128,128]{1,0:T(8,128)} %bitcast_add_fusion.a_ref), custom_call_target="tpu_custom_call" | custom-call | tf_op jit(solution)/shard_map/pallas_call | solution.py:115
  757.1 2.0 convolution_subtract_fusion
  759.6 2.6 convolution_subtract_fusion.2
  (106 shorter events, 32.9 us)
Async XLA Ops:
  6.5 15.1 %copy-start = (bf16[100,256]{1,0:T(8,128)(2,1)S(1)}, bf16[100,256]{1,0:T(8,128)(2,1)}, u32[]{:S(2)}) copy-start(bf16[100,256]{1,0:T(8,128)(2,1)} %param.27) | copy-start | bytes 153604
  7.7 14.0 %collective-permute-start = (bf16[1,100,128]{2,1,0:T(8,128)(2,1)S(1)}, bf16[1,100,128]{2,1,0:T(8,128)(2,1)S(1)}, u32[]{:S(2)}, u32[]{:S(2)}) collective-permute-start(bf16[1,100,128]{2,1,0:T(8,128)(2,1)S(1)} %get-tuple-element.115), channel_id=1, source_target_pairs={{0,4},{4,8},{8,12},{12,16},{16,20},{20,24},{24,28},{28,32},{32,36}... | collective-permute-start | bytes 76808 | tf_op jit(solution)/shard_map/ppermute | solution.py:16
  12.6 9.1 %collective-permute-start.1 = (bf16[1,100,128]{2,1,0:T(8,128)(2,1)S(1)}, bf16[1,100,128]{2,1,0:T(8,128)(2,1)S(1)}, u32[]{:S(2)}, u32[]{:S(2)}) collective-permute-start(bf16[1,100,128]{2,1,0:T(8,128)(2,1)S(1)} %get-tuple-element.116), channel_id=1, source_target_pairs={{4,0},{8,4},{12,8},{16,12},{20,16},{24,20},{28,24},{32,28},{36,32}... | collective-permute-start | bytes 76808 | tf_op jit(solution)/shard_map/ppermute | solution.py:19
  21.6 1.0 copy-start.4
  21.6 1.0 copy-start.11
  22.7 4.8 copy-start.10
  22.7 9.2 %copy-start.9 = (f32[100,16]{0,1:T(8,128)S(1)}, f32[100,16]{0,1:T(8,128)}, u32[]{:S(2)}) copy-start(f32[100,16]{0,1:T(8,128)} %param.30) | copy-start | bytes 19204
  22.7 9.3 %copy-start.12 = (f32[128,16]{0,1:T(8,128)S(1)}, f32[128,16]{0,1:T(8,128)}, u32[]{:S(2)}) copy-start(f32[128,16]{0,1:T(8,128)} %param.33) | copy-start | bytes 24580
  22.7 9.3 %copy-start.13 = (f32[128,16]{0,1:T(8,128)S(1)}, f32[128,16]{0,1:T(8,128)}, u32[]{:S(2)}) copy-start(f32[128,16]{0,1:T(8,128)} %param.34) | copy-start | bytes 24580
  24.2 7.7 all-to-all-start
  38.3 118.5 %all-to-all-start.2 = ((bf16[256,16,129]{2,1,0:T(8,128)(2,1)}), bf16[256,16,129]{2,1,0:T(8,128)(2,1)S(1)}, u32[]{:S(2)}, u32[]{:S(2)}) async-start(bf16[256,16,129]{2,1,0:T(8,128)(2,1)} %copy.110), calls=%async_computation.2 | async-start | bytes 4194304 | tf_op jit(solution)/shard_map/all_to_all | solution.py:40
  156.9 2.0 copy-start.1
  158.8 29.4 %all-to-all-start.3 = ((bf16[256,32,128]{2,1,0:T(8,128)(2,1)}), bf16[256,32,128]{2,1,0:T(8,128)(2,1)S(1)}, u32[]{:S(2)}, u32[]{:S(2)}) async-start(bf16[256,32,128]{2,1,0:T(8,128)(2,1)} %concatenate.39), calls=%async_computation.3 | async-start | bytes 4194304 | tf_op jit(solution)/shard_map/all_to_all | solution.py:59
  162.4 1.2 slice-start
  189.7 24.5 %all-to-all-start.1 = ((bf16[4,16,100,128]{3,1,2,0:T(8,128)(2,1)}), bf16[4,16,100,128]{3,1,2,0:T(8,128)(2,1)}, u32[]{:S(2)}, u32[]{:S(2)}) async-start(bf16[4,16,100,128]{3,1,2,0:T(8,128)(2,1)} %broadcast_in_dim.17), calls=%async_computation.1 | async-start | bytes 3276800 | tf_op jit(solution)/shard_map/all_to_all | solution.py:26
  194.0 478.7 %all-reduce.5.cloned.1.call-start = ((), (), s32[]{:S(2)}) async-start(), calls=%async_computation.4 | async-start | bytes 2105344 | tf_op jit(solution)/shard_map/psum | solution.py:68
  679.1 19.2 %copy-start.3 = (f32[512,512]{0,1:T(8,128)}, f32[512,512]{0,1:T(8,128)S(1)}, u32[]{:S(2)}) copy-start(f32[512,512]{0,1:T(8,128)S(1)} %convert_add_fusion) | copy-start | bytes 3145732
  696.2 2.7 copy-start.7
  717.3 19.3 %copy-start.2 = (f32[512,512]{1,0:T(8,128)}, f32[512,512]{1,0:T(8,128)S(1)}, u32[]{:S(2)}) copy-start(f32[512,512]{1,0:T(8,128)S(1)} %maximum_dynamic-update-slice_fusion) | copy-start | bytes 3145732
  718.9 37.9 %copy-start.5 = (f32[128,128]{1,0:T(8,128)S(1)}, f32[128,128]{1,0:T(8,128)}, u32[]{:S(2)}) copy-start(f32[128,128]{1,0:T(8,128)} %get-tuple-element.110) | copy-start | bytes 196612
  738.5 20.7 %copy-start.6 = (f32[128,128]{1,0:T(8,128)S(1)}, f32[128,128]{1,0:T(8,128)}, u32[]{:S(2)}) copy-start(f32[128,128]{1,0:T(8,128)} %get-tuple-element.112) | copy-start | bytes 196612
  756.8 5.4 copy-start.8
  756.8 5.8 slice-start.1
Sparse Core Ops, SparseCore 0:
  204.4 468.3 all-reduce.4

commit v2 on v1

--- a/solution.py
+++ b/solution.py
@@ -223,8 +223,20 @@
     weighted = portion * factor_part
     whole = jnp.einsum("qom,qoj->mj", weighted, portion, precision=top)
     vector = jnp.einsum("qom,qo->m", weighted, innov_part.astype(jnp.float32), precision=top)
-    gram_part, vec_all = together((whole, vector), ("cols", "mem"))
-    gram = jnp.eye(members, dtype=jnp.float32) + gram_part
+    half = members // 2
+    folded = jnp.tril(whole[half:, half:]) + jnp.tril(whole[:half, :half], -1).T
+    lower_left, folded, diagonal, vec_all = together(
+        (whole[half:, :half], folded, jnp.diagonal(whole[:half, :half]), vector), ("cols", "mem")
+    )
+    upper_left = jnp.triu(folded, 1).T + jnp.diag(diagonal)
+    gram_low = jnp.concatenate(
+        [
+            jnp.concatenate([upper_left, jnp.zeros_like(upper_left)], axis=1),
+            jnp.concatenate([lower_left, jnp.tril(folded)], axis=1),
+        ],
+        axis=0,
+    )
+    gram = jnp.eye(members, dtype=jnp.float32) + gram_low
     chol_inverse = factor_inverse(gram)
     weights = jnp.dot(chol_inverse.T, jnp.dot(chol_inverse, vec_all, precision=top), precision=top)
     first = lax.axis_index("mem") * mem_dev

time: 774 us -> 764 us (0.987)
  waiting for transfers between devices: 587 us -> 577 us
where the time goes in v2:
time: 764 us; the launch traced here: 762 us
  waiting for transfers between devices  577 us (76%)
  Pallas kernels  61.1 us (8%)
  starting transfers between devices  40.8 us (5%)
  local copies, waits for them, and re-layouts  31.8 us (4%)
  matrix products  23.4 us (3%)
  between operations  14.9 us (2%)
  other arithmetic  12.1 us (2%)
    psum x1, waiting for transfers between devices, together(): subtotal = lax.psum(ravelled, axis)  447 us
    all_to_all x1, waiting for transfers between devices, in_one_piece(): lax.all_to_all(both, axis, split_axis=split_dim, concat_axis=concat_dim,...  98.5 us
    pallas_call x4, Pallas kernels, factor_block(): pl.pallas_call(_eliminate, out_shape=(square, square), in_specs=[pl.Block...  61.1 us
    all_to_all x1, waiting for transfers between devices, in_one_piece_2(): lax.all_to_all(both, axis, split_axis=split_dim, concat_axis=concat_dim,...  23.9 us
    all_to_all x1, starting transfers between devices, in_one_piece(): lax.all_to_all(both, axis, split_axis=split_dim, concat_axis=concat_dim,...  19.3 us
  transfers between devices with their start and end apart: 7, of which 5 were waited for; matrix products, arithmetic and copies ran while one was open for 3% of the time, Pallas kernels for 0%

profile of v2, /device:TPU:1, one launch (start us, length us, event | category | flops | bytes accessed | tf_op | source)
XLA Modules:
  0.0 761.6 jit_solution(2213237556665088121)
XLA Ops:
  7.7 4.9 collective-permute-start
  12.6 5.1 collective-permute-start.1
  24.2 3.3 all-to-all-start
  27.5 4.4 all-to-all-done
  35.9 3.0 copy.125
  38.9 19.3 %all-to-all-start.2 = ((bf16[256,16,129]{2,1,0:T(8,128)(2,1)}), bf16[256,16,129]{2,1,0:T(8,128)(2,1)S(1)}, u32[]{:S(2)}, u32[]{:S(2)}) async-start(bf16[256,16,129]{2,1,0:T(8,128)(2,1)} %copy.125), calls=%async_computation.2 | async-start | bytes 4194304 | tf_op jit(solution)/shard_map/all_to_all | solution.py:40
  58.9 98.5 %all-to-all-done.2 = bf16[256,16,129]{2,1,0:T(8,128)(2,1)S(1)} async-done(((bf16[256,16,129]{2,1,0:T(8,128)(2,1)}), bf16[256,16,129]{2,1,0:T(8,128)(2,1)S(1)}, u32[]{:S(2)}, u32[]{:S(2)}) %all-to-all-start.2) | async-done | bytes 1056800 | tf_op jit(solution)/shard_map/all_to_all | solution.py:40
  157.6 1.8 concatenate.52
  159.3 3.6 all-to-all-start.3
  164.9 23.9 %all-to-all-done.3 = bf16[256,32,128]{2,1,0:T(8,128)(2,1)S(1)} async-done(((bf16[256,32,128]{2,1,0:T(8,128)(2,1)}), bf16[256,32,128]{2,1,0:T(8,128)(2,1)S(1)}, u32[]{:S(2)}, u32[]{:S(2)}) %all-to-all-start.3) | async-done | bytes 2097184 | tf_op jit(solution)/shard_map/all_to_all | solution.py:59
  188.8 1.4 broadcast_in_dim.65
  190.2 4.4 all-to-all-start.1
  194.8 2.9 copy.126
  197.7 2.7 all_to_all.28
  200.5 1.8 fusion.10
  202.3 1.6 fusion.8
  205.0 2.4 gather_fusion
  210.5 4.1 all-to-all-done.1
  214.7 3.9 copy.164
  218.5 2.8 reshape.276
  221.4 446.5 %all-reduce.6.cloned.1.call-done = f32[131840]{0:T(1024)} async-done(((f32[131840]{0:T(1024)}), f32[131840]{0:T(1024)}) %all-reduce.6.cloned.1.call-update) | async-done | bytes 527376 | tf_op jit(solution)/shard_map/psum | solution.py:68
  670.5 15.2 %shard_map.100 = (f32[128,128]{1,0:T(8,128)}, f32[128,128]{1,0:T(8,128)}) custom-call(f32[128,128]{1,0:T(8,128)} %bitcast_add_fusion.4.a_ref), custom_call_target="tpu_custom_call" | custom-call | tf_op jit(solution)/shard_map/pallas_call | solution.py:115
  685.8 1.3 fusion.47
  690.0 15.2 %shard_map.101 = (f32[128,128]{1,0:T(8,128)}, f32[128,128]{1,0:T(8,128)}) custom-call(f32[128,128]{1,0:T(8,128)} %bitcast_add_fusion.3.a_ref), custom_call_target="tpu_custom_call" | custom-call | tf_op jit(solution)/shard_map/pallas_call | solution.py:115
  705.2 1.2 fusion.55
  707.4 1.4 convolution_subtract_fusion.4
  709.6 15.4 %shard_map.102 = (f32[128,128]{1,0:T(8,128)}, f32[128,128]{1,0:T(8,128)}) custom-call(f32[128,128]{1,0:T(8,128)} %bitcast_add_fusion.2.a_ref), custom_call_target="tpu_custom_call" | custom-call | tf_op jit(solution)/shard_map/pallas_call | solution.py:115
  727.6 1.7 convolution_subtract_fusion.1
  731.1 1.5 convolution_subtract_fusion.2
  732.6 1.2 broadcast_select_fusion.1
  734.5 15.2 %shard_map.103 = (f32[128,128]{1,0:T(8,128)}, f32[128,128]{1,0:T(8,128)}) custom-call(f32[128,128]{1,0:T(8,128)} %bitcast_add_fusion.1.a_ref), custom_call_target="tpu_custom_call" | custom-call | tf_op jit(solution)/shard_map/pallas_call | solution.py:115
  749.8 1.2 convolution_dynamic-update-slice_fusion
  (127 shorter events, 33.6 us)
Async XLA Ops:
  6.5 15.1 %copy-start = (bf16[100,256]{1,0:T(8,128)(2,1)S(1)}, bf16[100,256]{1,0:T(8,128)(2,1)}, u32[]{:S(2)}) copy-start(bf16[100,256]{1,0:T(8,128)(2,1)} %param.27) | copy-start | bytes 153604
  7.7 14.0 %collective-permute-start = (bf16[1,100,128]{2,1,0:T(8,128)(2,1)S(1)}, bf16[1,100,128]{2,1,0:T(8,128)(2,1)S(1)}, u32[]{:S(2)}, u32[]{:S(2)}) collective-permute-start(bf16[1,100,128]{2,1,0:T(8,128)(2,1)S(1)} %get-tuple-element.119), channel_id=1, source_target_pairs={{0,4},{4,8},{8,12},{12,16},{16,20},{20,24},{24,28},{28,32},{32,36}... | collective-permute-start | bytes 76808 | tf_op jit(solution)/shard_map/ppermute | solution.py:16
  12.6 9.1 %collective-permute-start.1 = (bf16[1,100,128]{2,1,0:T(8,128)(2,1)S(1)}, bf16[1,100,128]{2,1,0:T(8,128)(2,1)S(1)}, u32[]{:S(2)}, u32[]{:S(2)}) collective-permute-start(bf16[1,100,128]{2,1,0:T(8,128)(2,1)S(1)} %get-tuple-element.120), channel_id=1, source_target_pairs={{4,0},{8,4},{12,8},{16,12},{20,16},{24,20},{28,24},{32,28},{36,32}... | collective-permute-start | bytes 76808 | tf_op jit(solution)/shard_map/ppermute | solution.py:19
  21.6 1.0 copy-start.6
  21.6 1.0 copy-start.15
  22.7 4.7 copy-start.13
  22.7 9.2 %copy-start.10 = (f32[100,16]{0,1:T(8,128)S(1)}, f32[100,16]{0,1:T(8,128)}, u32[]{:S(2)}) copy-start(f32[100,16]{0,1:T(8,128)} %param.30) | copy-start | bytes 19204
  22.7 10.0 %copy-start.16 = (f32[128,16]{0,1:T(8,128)S(1)}, f32[128,16]{0,1:T(8,128)}, u32[]{:S(2)}) copy-start(f32[128,16]{0,1:T(8,128)} %param.34) | copy-start | bytes 24580
  24.2 7.7 %all-to-all-start = ((f32[4,16,100]{2,1,0:T(8,128)}), f32[4,16,100]{2,1,0:T(8,128)S(1)}, u32[]{:S(2)}, u32[]{:S(2)}) async-start(f32[4,16,100]{2,1,0:T(8,128)} %broadcast_in_dim.64), calls=%async_computation | async-start | bytes 65536 | tf_op jit(solution)/shard_map/all_to_all | solution.py:26
  34.6 0.7 copy-start.17
  38.9 118.5 %all-to-all-start.2 = ((bf16[256,16,129]{2,1,0:T(8,128)(2,1)}), bf16[256,16,129]{2,1,0:T(8,128)(2,1)S(1)}, u32[]{:S(2)}, u32[]{:S(2)}) async-start(bf16[256,16,129]{2,1,0:T(8,128)(2,1)} %copy.125), calls=%async_computation.2 | async-start | bytes 4194304 | tf_op jit(solution)/shard_map/all_to_all | solution.py:40
  157.4 2.0 copy-start.1
  159.3 29.4 %all-to-all-start.3 = ((bf16[256,32,128]{2,1,0:T(8,128)(2,1)}), bf16[256,32,128]{2,1,0:T(8,128)(2,1)S(1)}, u32[]{:S(2)}, u32[]{:S(2)}) async-start(bf16[256,32,128]{2,1,0:T(8,128)(2,1)} %concatenate.52), calls=%async_computation.3 | async-start | bytes 4194304 | tf_op jit(solution)/shard_map/all_to_all | solution.py:59
  163.6 1.2 slice-start
  190.2 24.5 %all-to-all-start.1 = ((bf16[4,16,100,128]{3,1,2,0:T(8,128)(2,1)}), bf16[4,16,100,128]{3,1,2,0:T(8,128)(2,1)}, u32[]{:S(2)}, u32[]{:S(2)}) async-start(bf16[4,16,100,128]{3,1,2,0:T(8,128)(2,1)} %broadcast_in_dim.65), calls=%async_computation.1 | async-start | bytes 3276800 | tf_op jit(solution)/shard_map/all_to_all | solution.py:26
  194.5 473.4 %all-reduce.6.cloned.1.call-start = ((), (), s32[]{:S(2)}) async-start(), calls=%async_computation.4 | async-start | bytes 1056768 | tf_op jit(solution)/shard_map/psum | solution.py:68
  203.9 3.6 copy-start.14
  208.4 461.4 %copy-start.11 = (s32[128]{0:T(128)}, s32[128]{0:T(128)S(1)}, u32[]{:S(2)}) copy-start(s32[128]{0:T(128)S(1)} %iota_add_fusion.1) | copy-start | bytes 1540
  667.9 1.5 slice-start.1
  669.6 19.1 %copy-start.5 = (f32[512,512]{0,1:T(8,128)}, f32[512,512]{0,1:T(8,128)S(1)}, u32[]{:S(2)}) copy-start(f32[512,512]{0,1:T(8,128)S(1)} %fusion.18) | copy-start | bytes 3145732
  670.5 18.8 %copy-start.12 = (s32[128]{0:T(128)S(1)}, s32[128]{0:T(128)}, u32[]{:S(2)}) copy-start(s32[128]{0:T(128)} %copy-done.11) | copy-start | bytes 1540
  689.1 38.0 %copy-start.9 = (f32[128,128]{1,0:T(8,128)S(1)}, f32[128,128]{1,0:T(8,128)}, u32[]{:S(2)}) copy-start(f32[128,128]{1,0:T(8,128)} %get-tuple-element.108) | copy-start | bytes 196612
  707.4 19.7 %copy-start.2 = (f32[512,512]{1,0:T(8,128)}, f32[512,512]{1,0:T(8,128)S(1)}, u32[]{:S(2)}) copy-start(f32[512,512]{1,0:T(8,128)S(1)} %maximum_dynamic-update-slice_fusion) | copy-start | bytes 3145732
  708.9 20.4 %copy-start.7 = (f32[128,128]{1,0:T(8,128)S(1)}, f32[128,128]{1,0:T(8,128)}, u32[]{:S(2)}) copy-start(f32[128,128]{1,0:T(8,128)} %get-tuple-element.110) | copy-start | bytes 196612
  727.1 2.6 copy-start.4
  727.4 1.8 copy-start.3
  727.4 3.3 copy-start.8
Sparse Core Ops, SparseCore 0:
  208.5 459.3 all-reduce.5

commit v3 on v2

--- a/solution.py
+++ b/solution.py
@@ -68,6 +68,21 @@
     subtotal = lax.psum(ravelled, axis)
     for a in arrays:
         done.append(subtotal[at : at + a.size].reshape(a.shape))
+        at += a.size
+    return tuple(done)
+
+
+def summed_everywhere(arrays):
+    flat = jnp.concatenate([a.reshape(-1) for a in arrays])
+    peers = lax.axis_size("cols")
+    size = flat.shape[0]
+    width = -(-size // peers)
+    flat = jnp.pad(flat, (0, width * peers - size))
+    pieces = lax.all_to_all(flat.reshape(peers, width), "cols", 0, 0, tiled=True)
+    mine = lax.psum(jnp.sum(pieces, axis=0), "mem")
+    total, at, done = sent_to_all(mine, "cols").reshape(-1), 0, []
+    for a in arrays:
+        done.append(total[at : at + a.size].reshape(a.shape))
         at += a.size
     return tuple(done)
 
@@ -225,8 +240,8 @@
     vector = jnp.einsum("qom,qo->m", weighted, innov_part.astype(jnp.float32), precision=top)
     half = members // 2
     folded = jnp.tril(whole[half:, half:]) + jnp.tril(whole[:half, :half], -1).T
-    lower_left, folded, diagonal, vec_all = together(
-        (whole[half:, :half], folded, jnp.diagonal(whole[:half, :half]), vector), ("cols", "mem")
+    lower_left, folded, diagonal, vec_all = summed_everywhere(
+        (whole[half:, :half], folded, jnp.diagonal(whole[:half, :half]), vector)
     )
     upper_left = jnp.triu(folded, 1).T + jnp.diag(diagonal)
     gram_low = jnp.concatenate(

time: 764 us -> 413 us (0.54)
  waiting for transfers between devices: 577 us -> 194 us
  blocking collectives: 0 us -> 20.6 us
  starting transfers between devices: 40.8 us -> 59.8 us
  between operations: 14.9 us -> 1.49 us
    psum x1 -> x0, waiting for transfers between devices: 447 us -> none  [together(): subtotal = lax.psum(ravelled, axis)]
    all_to_all x0 -> x1, waiting for transfers between devices: none -> 35.3 us  [summed_everywhere(): lax.all_to_all(flat.reshape(peers, width), 'cols', 0, 0, tiled=True)]
    all_to_all x2 -> x3, waiting for transfers between devices: 8.52 us -> 34.4 us  [sent_to_all(): lax.all_to_all(jnp.broadcast_to(shard[None], (peers, *shard.shape)), axis...]
    psum x0 -> x1, blocking collectives: none -> 20.6 us  [summed_everywhere(): mine = lax.psum(jnp.sum(pieces, axis=0), 'mem')]
    all_to_all x0 -> x1, starting transfers between devices: none -> 9.24 us  [summed_everywhere(): lax.all_to_all(flat.reshape(peers, width), 'cols', 0, 0, tiled=True)]
    all_to_all x2 -> x3, starting transfers between devices: 7.64 us -> 16.5 us  [sent_to_all(): lax.all_to_all(jnp.broadcast_to(shard[None], (peers, *shard.shape)), axis...]
  transfers between devices with their start and end apart: 7 -> 8, of which waited for: 5 -> 5; matrix products, arithmetic and copies ran while one was open for 3% -> 3% of each run, Pallas kernels for 0% -> 0%
where the time goes in v3:
time: 413 us; the launch traced here: 411 us
  waiting for transfers between devices  194 us (47%)
  Pallas kernels  60.9 us (15%)
  starting transfers between devices  59.8 us (14%)
  local copies, waits for them, and re-layouts  30.2 us (7%)
  matrix products  25.7 us (6%)
  blocking collectives  20.6 us (5%)
  other arithmetic  19 us (5%)
    all_to_all x1, waiting for transfers between devices, in_one_piece(): lax.all_to_all(both, axis, split_axis=split_dim, concat_axis=concat_dim,...  98.5 us
    pallas_call x4, Pallas kernels, factor_block(): pl.pallas_call(_eliminate, out_shape=(square, square), in_specs=[pl.Block...  60.9 us
    all_to_all x1, waiting for transfers between devices, summed_everywhere(): lax.all_to_all(flat.reshape(peers, width), 'cols', 0, 0, tiled=True)  35.3 us
    all_to_all x3, waiting for transfers between devices, sent_to_all(): lax.all_to_all(jnp.broadcast_to(shard[None], (peers, *shard.shape)), axis...  34.4 us
    all_to_all x1, waiting for transfers between devices, in_one_piece_2(): lax.all_to_all(both, axis, split_axis=split_dim, concat_axis=concat_dim,...  25.5 us
    psum x1, blocking collectives, summed_everywhere(): mine = lax.psum(jnp.sum(pieces, axis=0), 'mem')  20.6 us
    all_to_all x1, starting transfers between devices, in_one_piece(): lax.all_to_all(both, axis, split_axis=split_dim, concat_axis=concat_dim,...  19.3 us
    all_to_all x3, starting transfers between devices, sent_to_all(): lax.all_to_all(jnp.broadcast_to(shard[None], (peers, *shard.shape)), axis...  16.5 us
  transfers between devices with their start and end apart: 8, of which 5 were waited for; matrix products, arithmetic and copies ran while one was open for 3% of the time, Pallas kernels for 0%

profile of v3, /device:TPU:1, one launch (start us, length us, event | category | flops | bytes accessed | tf_op | source)
XLA Modules:
  0.0 411.4 jit_solution(6056820491665192106)
XLA Ops:
  1.1 4.9 %collective-permute-start = (bf16[1,100,128]{2,1,0:T(8,128)(2,1)S(1)}, bf16[1,100,128]{2,1,0:T(8,128)(2,1)S(1)}, u32[]{:S(2)}, u32[]{:S(2)}) collective-permute-start(bf16[1,100,128]{2,1,0:T(8,128)(2,1)S(1)} %get-tuple-element.119), channel_id=1, source_target_pairs={{0,4},{4,8},{8,12},{12,16},{16,20},{20,24},{24,28},{28,32},{32,36}... | collective-permute-start | bytes 76808 | tf_op jit(solution)/shard_map/ppermute | solution.py:16
  6.1 5.1 %collective-permute-start.1 = (bf16[1,100,128]{2,1,0:T(8,128)(2,1)S(1)}, bf16[1,100,128]{2,1,0:T(8,128)(2,1)S(1)}, u32[]{:S(2)}, u32[]{:S(2)}) collective-permute-start(bf16[1,100,128]{2,1,0:T(8,128)(2,1)S(1)} %get-tuple-element.120), channel_id=1, source_target_pairs={{4,0},{8,4},{12,8},{16,12},{20,16},{24,20},{28,24},{32,28},{36,32}... | collective-permute-start | bytes 76808 | tf_op jit(solution)/shard_map/ppermute | solution.py:19
  17.6 3.3 all-to-all-start
  20.9 4.4 %all-to-all-done = f32[4,16,100]{2,1,0:T(8,128)S(1)} async-done(((f32[4,16,100]{2,1,0:T(8,128)}), f32[4,16,100]{2,1,0:T(8,128)S(1)}, u32[]{:S(2)}, u32[]{:S(2)}) %all-to-all-start) | async-done | bytes 25632 | tf_op jit(solution)/shard_map/all_to_all | solution.py:26
  29.3 3.0 copy.127
  32.3 19.3 %all-to-all-start.2 = ((bf16[256,16,129]{2,1,0:T(8,128)(2,1)}), bf16[256,16,129]{2,1,0:T(8,128)(2,1)S(1)}, u32[]{:S(2)}, u32[]{:S(2)}) async-start(bf16[256,16,129]{2,1,0:T(8,128)(2,1)} %copy.127), calls=%async_computation.2 | async-start | bytes 4194304 | tf_op jit(solution)/shard_map/all_to_all | solution.py:40
  52.3 98.5 %all-to-all-done.2 = bf16[256,16,129]{2,1,0:T(8,128)(2,1)S(1)} async-done(((bf16[256,16,129]{2,1,0:T(8,128)(2,1)}), bf16[256,16,129]{2,1,0:T(8,128)(2,1)S(1)}, u32[]{:S(2)}, u32[]{:S(2)}) %all-to-all-start.2) | async-done | bytes 1056800 | tf_op jit(solution)/shard_map/all_to_all | solution.py:40
  151.1 1.6 concatenate.52
  152.7 4.6 %all-to-all-start.3 = ((bf16[256,32,128]{2,1,0:T(8,128)(2,1)}), bf16[256,32,128]{2,1,0:T(8,128)(2,1)}, u32[]{:S(2)}, u32[]{:S(2)}) async-start(bf16[256,32,128]{2,1,0:T(8,128)(2,1)} %concatenate.52), calls=%async_computation.3 | async-start | bytes 4194304 | tf_op jit(solution)/shard_map/all_to_all | solution.py:59
  157.6 25.5 %all-to-all-done.3 = bf16[256,32,128]{2,1,0:T(8,128)(2,1)} async-done(((bf16[256,32,128]{2,1,0:T(8,128)(2,1)}), bf16[256,32,128]{2,1,0:T(8,128)(2,1)}, u32[]{:S(2)}, u32[]{:S(2)}) %all-to-all-start.3) | async-done | bytes 2097184 | tf_op jit(solution)/shard_map/all_to_all | solution.py:59
  183.1 3.2 copy.128
  186.3 2.2 all_to_all.38
  188.5 3.8 fusion.10
  194.7 2.4 gather_fusion
  197.3 1.6 all_to_all.42
  198.9 9.2 %all-to-all-start.4 = ((f32[128,1,1030]{2,1,0:T(1,128)}), f32[128,1,1030]{2,1,0:T(1,128)S(1)}, u32[]{:S(2)}, u32[]{:S(2)}) async-start(f32[128,1,1030]{2,1,0:T(1,128)} %all_to_all.42), calls=%async_computation.4 | async-start | bytes 1179648 | tf_op jit(solution)/shard_map/all_to_all | solution.py:81
  208.5 35.3 %all-to-all-done.4 = f32[128,1,1030]{2,1,0:T(1,128)S(1)} async-done(((f32[128,1,1030]{2,1,0:T(1,128)}), f32[128,1,1030]{2,1,0:T(1,128)S(1)}, u32[]{:S(2)}, u32[]{:S(2)}) %all-to-all-start.4) | async-done | bytes 527392 | tf_op jit(solution)/shard_map/all_to_all | solution.py:81
  245.3 3.6 all-to-all-start.1
  248.9 1.5 reduce_sum.62
  250.3 20.6 %psum.7 = f32[1030]{0:T(1024)S(1)} all-reduce(f32[1030]{0:T(1024)S(1)} %reduce_sum.62), channel_id=1, replica_groups=mesh['cols'=128,'mem'=4] {'mem'}, use_global_device_ids=true, to_apply=%region_7.8 | all-reduce | flops 1030 | bytes 8240 | tf_op jit(solution)/shard_map/psum | solution.py:82
  272.1 9.7 %all-to-all-start.5 = ((f32[128,1,1030]{2,1,0:T(1,128)}), f32[128,1,1030]{2,1,0:T(1,128)}, u32[]{:S(2)}, u32[]{:S(2)}) async-start(f32[128,1,1030]{2,1,0:T(1,128)} %broadcast_in_dim.73), calls=%async_computation.5 | async-start | bytes 1179648 | tf_op jit(solution)/shard_map/all_to_all | solution.py:26
  287.1 30.0 %all-to-all-done.5 = f32[128,1,1030]{2,1,0:T(1,128)} async-done(((f32[128,1,1030]{2,1,0:T(1,128)}), f32[128,1,1030]{2,1,0:T(1,128)}, u32[]{:S(2)}, u32[]{:S(2)}) %all-to-all-start.5) | async-done | bytes 527392 | tf_op jit(solution)/shard_map/all_to_all | solution.py:26
  317.2 2.5 reduce.22
  322.3 1.6 bitcast_add_fusion.4.a_ref
  324.0 15.2 %shard_map.100 = (f32[128,128]{1,0:T(8,128)}, f32[128,128]{1,0:T(8,128)}) custom-call(f32[128,128]{1,0:T(8,128)} %bitcast_add_fusion.4.a_ref), custom_call_target="tpu_custom_call" | custom-call | tf_op jit(solution)/shard_map/pallas_call | solution.py:130
  340.5 1.6 copy.140
  342.1 1.5 maximum_select_fusion
  346.1 15.2 %shard_map.101 = (f32[128,128]{1,0:T(8,128)}, f32[128,128]{1,0:T(8,128)}) custom-call(f32[128,128]{1,0:T(8,128)} %bitcast_add_fusion.3.a_ref), custom_call_target="tpu_custom_call" | custom-call | tf_op jit(solution)/shard_map/pallas_call | solution.py:130
  366.2 15.2 %shard_map.102 = (f32[128,128]{1,0:T(8,128)}, f32[128,128]{1,0:T(8,128)}) custom-call(f32[128,128]{1,0:T(8,128)} %bitcast_add_fusion.2.a_ref), custom_call_target="tpu_custom_call" | custom-call | tf_op jit(solution)/shard_map/pallas_call | solution.py:130
  384.9 1.7 convolution_subtract_fusion.1
  388.4 1.5 convolution_subtract_fusion.2
  391.8 15.2 %shard_map.103 = (f32[128,128]{1,0:T(8,128)}, f32[128,128]{1,0:T(8,128)}) custom-call(f32[128,128]{1,0:T(8,128)} %bitcast_add_fusion.1.a_ref), custom_call_target="tpu_custom_call" | custom-call | tf_op jit(solution)/shard_map/pallas_call | solution.py:130
  (134 shorter events, 45.1 us)
Async XLA Ops:
  0.0 15.1 %copy-start = (bf16[100,256]{1,0:T(8,128)(2,1)S(1)}, bf16[100,256]{1,0:T(8,128)(2,1)}, u32[]{:S(2)}) copy-start(bf16[100,256]{1,0:T(8,128)(2,1)} %param.27) | copy-start | bytes 153604
  1.1 14.0 %collective-permute-start = (bf16[1,100,128]{2,1,0:T(8,128)(2,1)S(1)}, bf16[1,100,128]{2,1,0:T(8,128)(2,1)S(1)}, u32[]{:S(2)}, u32[]{:S(2)}) collective-permute-start(bf16[1,100,128]{2,1,0:T(8,128)(2,1)S(1)} %get-tuple-element.119), channel_id=1, source_target_pairs={{0,4},{4,8},{8,12},{12,16},{16,20},{20,24},{24,28},{28,32},{32,36}... | collective-permute-start | bytes 76808 | tf_op jit(solution)/shard_map/ppermute | solution.py:16
  6.1 9.1 %collective-permute-start.1 = (bf16[1,100,128]{2,1,0:T(8,128)(2,1)S(1)}, bf16[1,100,128]{2,1,0:T(8,128)(2,1)S(1)}, u32[]{:S(2)}, u32[]{:S(2)}) collective-permute-start(bf16[1,100,128]{2,1,0:T(8,128)(2,1)S(1)} %get-tuple-element.120), channel_id=1, source_target_pairs={{4,0},{8,4},{12,8},{16,12},{20,16},{24,20},{28,24},{32,28},{36,32}... | collective-permute-start | bytes 76808 | tf_op jit(solution)/shard_map/ppermute | solution.py:19
  15.1 1.0 copy-start.9
  15.1 1.0 copy-start.16
  16.2 4.7 %copy-start.15 = (s32[128,4]{0,1:T(4,128)S(1)}, s32[128,4]{0,1:T(4,128)}, u32[]{:S(2)}) copy-start(s32[128,4]{0,1:T(4,128)} %param.31) | copy-start | bytes 6148
  16.2 9.2 %copy-start.12 = (f32[100,16]{0,1:T(8,128)S(1)}, f32[100,16]{0,1:T(8,128)}, u32[]{:S(2)}) copy-start(f32[100,16]{0,1:T(8,128)} %param.30) | copy-start | bytes 19204
  16.2 10.0 %copy-start.17 = (f32[128,16]{0,1:T(8,128)S(1)}, f32[128,16]{0,1:T(8,128)}, u32[]{:S(2)}) copy-start(f32[128,16]{0,1:T(8,128)} %param.34) | copy-start | bytes 24580
  17.6 7.7 %all-to-all-start = ((f32[4,16,100]{2,1,0:T(8,128)}), f32[4,16,100]{2,1,0:T(8,128)S(1)}, u32[]{:S(2)}, u32[]{:S(2)}) async-start(f32[4,16,100]{2,1,0:T(8,128)} %broadcast_in_dim.70), calls=%async_computation | async-start | bytes 65536 | tf_op jit(solution)/shard_map/all_to_all | solution.py:26
  28.1 0.7 copy-start.18
  32.3 118.5 %all-to-all-start.2 = ((bf16[256,16,129]{2,1,0:T(8,128)(2,1)}), bf16[256,16,129]{2,1,0:T(8,128)(2,1)S(1)}, u32[]{:S(2)}, u32[]{:S(2)}) async-start(bf16[256,16,129]{2,1,0:T(8,128)(2,1)} %copy.127), calls=%async_computation.2 | async-start | bytes 4194304 | tf_op jit(solution)/shard_map/all_to_all | solution.py:40
  152.7 30.3 %all-to-all-start.3 = ((bf16[256,32,128]{2,1,0:T(8,128)(2,1)}), bf16[256,32,128]{2,1,0:T(8,128)(2,1)}, u32[]{:S(2)}, u32[]{:S(2)}) async-start(bf16[256,32,128]{2,1,0:T(8,128)(2,1)} %concatenate.52), calls=%async_computation.3 | async-start | bytes 4194304 | tf_op jit(solution)/shard_map/all_to_all | solution.py:59
  188.5 3.8 copy-start.6
  192.4 1.1 copy-start.7
  198.9 44.9 %all-to-all-start.4 = ((f32[128,1,1030]{2,1,0:T(1,128)}), f32[128,1,1030]{2,1,0:T(1,128)S(1)}, u32[]{:S(2)}, u32[]{:S(2)}) async-start(f32[128,1,1030]{2,1,0:T(1,128)} %all_to_all.42), calls=%async_computation.4 | async-start | bytes 1179648 | tf_op jit(solution)/shard_map/all_to_all | solution.py:81
  243.9 1.4 copy-start.5
  245.3 25.7 %all-to-all-start.1 = ((bf16[4,16,100,128]{3,1,2,0:T(8,128)(2,1)}), bf16[4,16,100,128]{3,1,2,0:T(8,128)(2,1)S(1)}, u32[]{:S(2)}, u32[]{:S(2)}) async-start(bf16[4,16,100,128]{3,1,2,0:T(8,128)(2,1)} %broadcast_in_dim.71), calls=%async_computation.1 | async-start | bytes 3276800 | tf_op jit(solution)/shard_map/all_to_all | solution.py:26
  272.1 45.1 %all-to-all-start.5 = ((f32[128,1,1030]{2,1,0:T(1,128)}), f32[128,1,1030]{2,1,0:T(1,128)}, u32[]{:S(2)}, u32[]{:S(2)}) async-start(f32[128,1,1030]{2,1,0:T(1,128)} %broadcast_in_dim.73), calls=%async_computation.5 | async-start | bytes 1179648 | tf_op jit(solution)/shard_map/all_to_all | solution.py:26
  321.3 0.7 slice-start
  322.2 21.4 %copy-start.4 = (f32[512,512]{0,1:T(8,128)}, f32[512,512]{0,1:T(8,128)S(1)}, u32[]{:S(2)}) copy-start(f32[512,512]{0,1:T(8,128)S(1)} %fusion.18) | copy-start | bytes 3145732
  322.2 21.9 %copy-start.8 = (f32[131840]{0:T(1024)S(1)}, f32[131840]{0:T(1024)}, u32[]{:S(2)}) copy-start(f32[131840]{0:T(1024)} %reshape.258) | copy-start | bytes 1582084
  363.5 20.0 %copy-start.1 = (f32[512,512]{1,0:T(8,128)}, f32[512,512]{1,0:T(8,128)S(1)}, u32[]{:S(2)}) copy-start(f32[512,512]{1,0:T(8,128)S(1)} %maximum_dynamic-update-slice_fusion) | copy-start | bytes 3145732
  364.9 21.6 %copy-start.10 = (f32[128,128]{1,0:T(8,128)S(1)}, f32[128,128]{1,0:T(8,128)}, u32[]{:S(2)}) copy-start(f32[128,128]{1,0:T(8,128)} %get-tuple-element.110) | copy-start | bytes 196612
  383.5 3.5 copy-start.3
  384.7 1.8 copy-start.2
  384.7 3.3 copy-start.11
  386.6 4.6 %copy-start.13 = (s32[128]{0:T(128)S(1)}, s32[128]{0:T(128)}, u32[]{:S(2)}) copy-start(s32[128]{0:T(128)} %iota_add_fusion.1) | copy-start | bytes 1540
  387.0 21.3 %copy-start.14 = (f32[512]{0:T(512)S(1)}, f32[512]{0:T(512)}, u32[]{:S(2)}) copy-start(f32[512]{0:T(512)} %slice.353) | copy-start | bytes 6148

commit v4 on v3

--- a/solution.py
+++ b/solution.py
@@ -201,41 +201,14 @@
     scale = 1.0 / math.sqrt(members - 1)
     spread = (rinv[:, :, None] * fpert * scale).astype(jnp.bfloat16)
     innov = (rinv * (obs - fmean)).astype(jnp.bfloat16)
-    target = owner[:, 0]
-    capacity = max(2, 2 * src_b // n_cols)
-    owner_hits = (target[:, None] == jnp.arange(n_cols, dtype=jnp.int32)[None, :]).astype(jnp.int32)
-    ranking = jnp.sum((jnp.cumsum(owner_hits, axis=0) - 1) * owner_hits, axis=1)
-    slot = target * capacity + ranking
-    placing = (slot[:, None] == jnp.arange(n_cols * capacity, dtype=jnp.int32)[None, :]).astype(
-        jnp.bfloat16
-    )
-    send_spread = jnp.einsum(
-        "bq,bom->qom", placing, spread, preferred_element_type=jnp.float32
-    ).astype(jnp.bfloat16)
-    send_innov = jnp.einsum("bq,bo->qo", placing, innov, preferred_element_type=jnp.float32).astype(
-        jnp.bfloat16
-    )
-    held_spread, held_innov = in_one_piece((send_spread, send_innov), "cols", 0, 0, 2)
-    held_factor = jnp.full((held_spread.shape[0],), inflation[0] * inflation[0], jnp.float32)
-    quarter = held_spread.shape[0] // n_mem
-    factor_grid = jnp.broadcast_to(held_factor[:, None, None], held_spread.shape)
-    portion, factor_part = tuple(
-        (
-            part.astype(jnp.float32)
-            for part in in_one_piece_2(
-                (
-                    held_spread.astype(jnp.float32).astype(jnp.bfloat16),
-                    factor_grid.astype(jnp.bfloat16),
-                ),
-                "mem",
-                0,
-                2,
-                1,
-            )
-        )
-    )
-    innov_part = lax.dynamic_slice_in_dim(held_innov, lax.axis_index("mem") * quarter, quarter, 0)
-    weighted = portion * factor_part
+    every_inflation = sent_to_all(inflation, "cols").reshape(-1)
+    factor = every_inflation[owner[:, 0]] ** 2
+    quarter = src_b // n_mem
+    first_batch = lax.axis_index("mem") * quarter
+    portion = lax.all_to_all(spread, "mem", 0, 2, tiled=True).astype(jnp.float32)
+    innov_part = lax.dynamic_slice_in_dim(innov, first_batch, quarter, 0)
+    factor_part = lax.dynamic_slice_in_dim(factor, first_batch, quarter, 0)
+    weighted = portion * factor_part[:, None, None]
     whole = jnp.einsum("qom,qoj->mj", weighted, portion, precision=top)
     vector = jnp.einsum("qom,qo->m", weighted, innov_part.astype(jnp.float32), precision=top)
     half = members // 2

time: 413 us -> 286 us (0.69)
  waiting for transfers between devices: 194 us -> 77.9 us
  local copies, waits for them, and re-layouts: 30.2 us -> 22 us
  other arithmetic: 19 us -> 13.5 us
    all_to_all x2 -> x1, waiting for transfers between devices: 124 us -> 6.48 us  [body(): lax.all_to_all(spread, 'mem', 0, 2, tiled=True).astype(jnp.float32)]
    all_to_all x3 -> x4, starting transfers between devices: 16.5 us -> 37.8 us  [sent_to_all(): lax.all_to_all(jnp.broadcast_to(shard[None], (peers, *shard.shape)), axis...]
    all_to_all x2 -> x1, starting transfers between devices: 24 us -> 3.47 us  [body(): lax.all_to_all(spread, 'mem', 0, 2, tiled=True).astype(jnp.float32)]
    all_to_all x1, starting transfers between devices: 9.24 us -> 16.7 us  [summed_everywhere(): lax.all_to_all(flat.reshape(peers, width), 'cols', 0, 0, tiled=True)]
    all_to_all x2, local copies, waits for them, and re-layouts: 5.46 us -> 0.61 us  [body(): lax.all_to_all(spread, 'mem', 0, 2, tiled=True).astype(jnp.float32)]
    concatenate x2 -> x0, local copies, waits for them, and re-layouts: 4.66 us -> none  [the longest x1 3.01 us: in_one_piece(): both = jnp.concatenate(columns, axis=along)]
    all_to_all x3 -> x4, waiting for transfers between devices: 34.4 us -> 35.5 us  [sent_to_all(): lax.all_to_all(jnp.broadcast_to(shard[None], (peers, *shard.shape)), axis...]
  transfers between devices with their start and end apart: 8 -> 8, of which waited for: 5 -> 6; matrix products, arithmetic and copies ran while one was open for 3% -> 5% of each run, Pallas kernels for 0% -> 0%
where the time goes in v4:
time: 286 us; the launch traced here: 284 us
  waiting for transfers between devices  77.9 us (27%)
  starting transfers between devices  63.5 us (22%)
  Pallas kernels  61.1 us (21%)
  matrix products  23.1 us (8%)
  local copies, waits for them, and re-layouts  22 us (8%)
  blocking collectives  21.7 us (8%)
  other arithmetic  13.5 us (5%)
    pallas_call x4, Pallas kernels, factor_block(): pl.pallas_call(_eliminate, out_shape=(square, square), in_specs=[pl.Block...  61.1 us
    all_to_all x4, starting transfers between devices, sent_to_all(): lax.all_to_all(jnp.broadcast_to(shard[None], (peers, *shard.shape)), axis...  37.8 us
    all_to_all x4, waiting for transfers between devices, sent_to_all(): lax.all_to_all(jnp.broadcast_to(shard[None], (peers, *shard.shape)), axis...  35.5 us
    all_to_all x1, waiting for transfers between devices, summed_everywhere(): lax.all_to_all(flat.reshape(peers, width), 'cols', 0, 0, tiled=True)  35.3 us
    psum x1, blocking collectives, summed_everywhere(): mine = lax.psum(jnp.sum(pieces, axis=0), 'mem')  21.7 us
    all_to_all x1, starting transfers between devices, summed_everywhere(): lax.all_to_all(flat.reshape(peers, width), 'cols', 0, 0, tiled=True)  16.7 us
    all_to_all x1, waiting for transfers between devices, body(): lax.all_to_all(spread, 'mem', 0, 2, tiled=True).astype(jnp.float32)  6.48 us
    dot_general x3, matrix products, factor_inverse(): jnp.dot(chol[begin:finish, :begin], chol_inverse[:begin], precision=top)  6.18 us
  transfers between devices with their start and end apart: 8, of which 6 were waited for; matrix products, arithmetic and copies ran while one was open for 5% of the time, Pallas kernels for 0%

profile of v4, /device:TPU:1, one launch (start us, length us, event | category | flops | bytes accessed | tf_op | source)
XLA Modules:
  0.0 284.1 jit_solution(17860288022010182455)
XLA Ops:
  1.3 20.4 %all-to-all-start.3 = ((f32[128,1,1]{2,1,0:T(1,128)}), f32[128,1,1]{2,1,0:T(1,128)S(1)}, u32[]{:S(2)}, u32[]{:S(2)}) async-start(f32[128,1,1]{2,1,0:T(1,128)} %broadcast_in_dim.81), calls=%async_computation.3 | async-start | bytes 131072 | tf_op jit(solution)/shard_map/all_to_all | solution.py:26
  22.8 3.5 %collective-permute-start = (bf16[1,100,128]{2,1,0:T(8,128)(2,1)S(1)}, bf16[1,100,128]{2,1,0:T(8,128)(2,1)S(1)}, u32[]{:S(2)}, u32[]{:S(2)}) collective-permute-start(bf16[1,100,128]{2,1,0:T(8,128)(2,1)S(1)} %get-tuple-element.119), channel_id=1, source_target_pairs={{0,4},{4,8},{8,12},{12,16},{16,20},{20,24},{24,28},{28,32},{32,36}... | collective-permute-start | bytes 76808 | tf_op jit(solution)/shard_map/ppermute | solution.py:16
  26.4 1.9 collective-permute-start.1
  33.7 3.0 %all-to-all-done.3 = f32[128,1,1]{2,1,0:T(1,128)S(1)} async-done(((f32[128,1,1]{2,1,0:T(1,128)}), f32[128,1,1]{2,1,0:T(1,128)S(1)}, u32[]{:S(2)}, u32[]{:S(2)}) %all-to-all-start.3) | async-done | bytes 544 | tf_op jit(solution)/shard_map/all_to_all | solution.py:26
  37.3 4.2 %all-to-all-start = ((f32[4,16,100]{2,1,0:T(8,128)}), f32[4,16,100]{2,1,0:T(8,128)S(1)}, u32[]{:S(2)}, u32[]{:S(2)}) async-start(f32[4,16,100]{2,1,0:T(8,128)} %broadcast_in_dim.77), calls=%async_computation | async-start | bytes 65536 | tf_op jit(solution)/shard_map/all_to_all | solution.py:26
  42.5 1.2 gather_fusion
  43.9 1.9 all-to-all-done
  48.8 3.5 %all-to-all-start.2 = ((bf16[128,16,128]{2,1,0:T(8,128)(2,1)}), bf16[128,16,128]{2,1,0:T(8,128)(2,1)S(1)}, u32[]{:S(2)}, u32[]{:S(2)}) async-start(bf16[128,16,128]{2,1,0:T(8,128)(2,1)} %copy.159), calls=%async_computation.2 | async-start | bytes 1048576 | tf_op jit(solution)/shard_map/all_to_all | solution.py:208
  52.7 6.5 %all-to-all-done.2 = bf16[128,16,128]{2,1,0:T(8,128)(2,1)S(1)} async-done(((bf16[128,16,128]{2,1,0:T(8,128)(2,1)}), bf16[128,16,128]{2,1,0:T(8,128)(2,1)S(1)}, u32[]{:S(2)}, u32[]{:S(2)}) %all-to-all-start.2) | async-done | bytes 524320 | tf_op jit(solution)/shard_map/all_to_all | solution.py:208
  61.9 2.4 gather_fusion.1
  64.4 1.6 all_to_all.43
  66.1 16.7 %all-to-all-start.4 = ((f32[128,1,1030]{2,1,0:T(1,128)}), f32[128,1,1030]{2,1,0:T(1,128)S(1)}, u32[]{:S(2)}, u32[]{:S(2)}) async-start(f32[128,1,1030]{2,1,0:T(1,128)} %all_to_all.43), calls=%async_computation.4 | async-start | bytes 1179648 | tf_op jit(solution)/shard_map/all_to_all | solution.py:81
  83.1 35.3 %all-to-all-done.4 = f32[128,1,1030]{2,1,0:T(1,128)S(1)} async-done(((f32[128,1,1030]{2,1,0:T(1,128)}), f32[128,1,1030]{2,1,0:T(1,128)S(1)}, u32[]{:S(2)}, u32[]{:S(2)}) %all-to-all-start.4) | async-done | bytes 527392 | tf_op jit(solution)/shard_map/all_to_all | solution.py:81
  118.5 1.4 broadcast_in_dim.78
  119.9 3.6 %all-to-all-start.1 = ((bf16[4,16,100,128]{3,1,2,0:T(8,128)(2,1)}), bf16[4,16,100,128]{3,1,2,0:T(8,128)(2,1)S(1)}, u32[]{:S(2)}, u32[]{:S(2)}) async-start(bf16[4,16,100,128]{3,1,2,0:T(8,128)(2,1)} %broadcast_in_dim.78), calls=%async_computation.1 | async-start | bytes 3276800 | tf_op jit(solution)/shard_map/all_to_all | solution.py:26
  123.8 21.7 %psum.7 = f32[1030]{0:T(1024)S(1)} all-reduce(f32[1030]{0:T(1024)S(1)} %reduce_sum.49), channel_id=1, replica_groups=mesh['cols'=128,'mem'=4] {'mem'}, use_global_device_ids=true, to_apply=%region_5.6 | all-reduce | flops 1030 | bytes 8240 | tf_op jit(solution)/shard_map/psum | solution.py:82
  145.5 1.1 broadcast_in_dim.82
  146.7 9.7 %all-to-all-start.5 = ((f32[128,1,1030]{2,1,0:T(1,128)}), f32[128,1,1030]{2,1,0:T(1,128)}, u32[]{:S(2)}, u32[]{:S(2)}) async-start(f32[128,1,1030]{2,1,0:T(1,128)} %broadcast_in_dim.82), calls=%async_computation.5 | async-start | bytes 1179648 | tf_op jit(solution)/shard_map/all_to_all | solution.py:26
  159.3 1.3 copy.198
  161.2 30.6 %all-to-all-done.5 = f32[128,1,1030]{2,1,0:T(1,128)} async-done(((f32[128,1,1030]{2,1,0:T(1,128)}), f32[128,1,1030]{2,1,0:T(1,128)}, u32[]{:S(2)}, u32[]{:S(2)}) %all-to-all-start.5) | async-done | bytes 527392 | tf_op jit(solution)/shard_map/all_to_all | solution.py:26
  191.8 2.5 reduce.23
  197.7 15.2 %shard_map.100 = (f32[128,128]{1,0:T(8,128)}, f32[128,128]{1,0:T(8,128)}) custom-call(f32[128,128]{1,0:T(8,128)} %bitcast_add_fusion.4.a_ref), custom_call_target="tpu_custom_call" | custom-call | tf_op jit(solution)/shard_map/pallas_call | solution.py:130
  213.9 1.3 fusion.39
  218.3 15.2 %shard_map.101 = (f32[128,128]{1,0:T(8,128)}, f32[128,128]{1,0:T(8,128)}) custom-call(f32[128,128]{1,0:T(8,128)} %bitcast_add_fusion.3.a_ref), custom_call_target="tpu_custom_call" | custom-call | tf_op jit(solution)/shard_map/pallas_call | solution.py:130
  233.5 1.2 fusion.47
  235.7 1.4 convolution_subtract_fusion.4
  237.9 15.2 %shard_map.102 = (f32[128,128]{1,0:T(8,128)}, f32[128,128]{1,0:T(8,128)}) custom-call(f32[128,128]{1,0:T(8,128)} %bitcast_add_fusion.2.a_ref), custom_call_target="tpu_custom_call" | custom-call | tf_op jit(solution)/shard_map/pallas_call | solution.py:130
  255.3 1.6 convolution_subtract_fusion.1
  257.6 1.4 broadcast_select_fusion.1
  259.7 15.4 %shard_map.103 = (f32[128,128]{1,0:T(8,128)}, f32[128,128]{1,0:T(8,128)}) custom-call(f32[128,128]{1,0:T(8,128)} %bitcast_add_fusion.1.a_ref), custom_call_target="tpu_custom_call" | custom-call | tf_op jit(solution)/shard_map/pallas_call | solution.py:130
  275.6 2.0 convolution_subtract_fusion
  278.0 2.6 convolution_subtract_fusion.2
  (118 shorter events, 36.1 us)
Async XLA Ops:
  0.0 31.9 %copy-start = (bf16[100,256]{1,0:T(8,128)(2,1)S(1)}, bf16[100,256]{1,0:T(8,128)(2,1)}, u32[]{:S(2)}) copy-start(bf16[100,256]{1,0:T(8,128)(2,1)} %param.27) | copy-start | bytes 153604
  1.3 35.4 %all-to-all-start.3 = ((f32[128,1,1]{2,1,0:T(1,128)}), f32[128,1,1]{2,1,0:T(1,128)S(1)}, u32[]{:S(2)}, u32[]{:S(2)}) async-start(f32[128,1,1]{2,1,0:T(1,128)} %broadcast_in_dim.81), calls=%async_computation.3 | async-start | bytes 131072 | tf_op jit(solution)/shard_map/all_to_all | solution.py:26
  22.8 8.4 %collective-permute-start = (bf16[1,100,128]{2,1,0:T(8,128)(2,1)S(1)}, bf16[1,100,128]{2,1,0:T(8,128)(2,1)S(1)}, u32[]{:S(2)}, u32[]{:S(2)}) collective-permute-start(bf16[1,100,128]{2,1,0:T(8,128)(2,1)S(1)} %get-tuple-element.119), channel_id=1, source_target_pairs={{0,4},{4,8},{8,12},{12,16},{16,20},{20,24},{24,28},{28,32},{32,36}... | collective-permute-start | bytes 76808 | tf_op jit(solution)/shard_map/ppermute | solution.py:16
  26.4 5.5 %collective-permute-start.1 = (bf16[1,100,128]{2,1,0:T(8,128)(2,1)S(1)}, bf16[1,100,128]{2,1,0:T(8,128)(2,1)S(1)}, u32[]{:S(2)}, u32[]{:S(2)}) collective-permute-start(bf16[1,100,128]{2,1,0:T(8,128)(2,1)S(1)} %get-tuple-element.120), channel_id=1, source_target_pairs={{4,0},{8,4},{12,8},{16,12},{20,16},{24,20},{28,24},{32,28},{36,32}... | collective-permute-start | bytes 76808 | tf_op jit(solution)/shard_map/ppermute | solution.py:19
  31.2 1.7 copy-start.4
  31.2 1.7 copy-start.13
  32.9 12.9 %copy-start.9 = (f32[100,16]{0,1:T(8,128)S(1)}, f32[100,16]{0,1:T(8,128)}, u32[]{:S(2)}) copy-start(f32[100,16]{0,1:T(8,128)} %param.30) | copy-start | bytes 19204
  33.7 12.9 %copy-start.11 = (f32[128,16]{0,1:T(8,128)S(1)}, f32[128,16]{0,1:T(8,128)}, u32[]{:S(2)}) copy-start(f32[128,16]{0,1:T(8,128)} %param.34) | copy-start | bytes 24580
  37.3 8.5 %all-to-all-start = ((f32[4,16,100]{2,1,0:T(8,128)}), f32[4,16,100]{2,1,0:T(8,128)S(1)}, u32[]{:S(2)}, u32[]{:S(2)}) async-start(f32[4,16,100]{2,1,0:T(8,128)} %broadcast_in_dim.77), calls=%async_computation | async-start | bytes 65536 | tf_op jit(solution)/shard_map/all_to_all | solution.py:26
  46.6 6.0 %copy-start.12 = (f32[128,16]{0,1:T(8,128)S(1)}, f32[128,16]{0,1:T(8,128)}, u32[]{:S(2)}) copy-start(f32[128,16]{0,1:T(8,128)} %param.33) | copy-start | bytes 24580
  48.8 10.4 %all-to-all-start.2 = ((bf16[128,16,128]{2,1,0:T(8,128)(2,1)}), bf16[128,16,128]{2,1,0:T(8,128)(2,1)S(1)}, u32[]{:S(2)}, u32[]{:S(2)}) async-start(bf16[128,16,128]{2,1,0:T(8,128)(2,1)} %copy.159), calls=%async_computation.2 | async-start | bytes 1048576 | tf_op jit(solution)/shard_map/all_to_all | solution.py:208
  66.1 52.4 %all-to-all-start.4 = ((f32[128,1,1030]{2,1,0:T(1,128)}), f32[128,1,1030]{2,1,0:T(1,128)S(1)}, u32[]{:S(2)}, u32[]{:S(2)}) async-start(f32[128,1,1030]{2,1,0:T(1,128)} %all_to_all.43), calls=%async_computation.4 | async-start | bytes 1179648 | tf_op jit(solution)/shard_map/all_to_all | solution.py:81
  119.9 25.7 %all-to-all-start.1 = ((bf16[4,16,100,128]{3,1,2,0:T(8,128)(2,1)}), bf16[4,16,100,128]{3,1,2,0:T(8,128)(2,1)S(1)}, u32[]{:S(2)}, u32[]{:S(2)}) async-start(bf16[4,16,100,128]{3,1,2,0:T(8,128)(2,1)} %broadcast_in_dim.78), calls=%async_computation.1 | async-start | bytes 3276800 | tf_op jit(solution)/shard_map/all_to_all | solution.py:26
  146.7 45.1 %all-to-all-start.5 = ((f32[128,1,1030]{2,1,0:T(1,128)}), f32[128,1,1030]{2,1,0:T(1,128)}, u32[]{:S(2)}, u32[]{:S(2)}) async-start(f32[128,1,1030]{2,1,0:T(1,128)} %broadcast_in_dim.82), calls=%async_computation.5 | async-start | bytes 1179648 | tf_op jit(solution)/shard_map/all_to_all | solution.py:26
  194.5 0.8 copy-start.3
  196.0 0.7 slice-start
  196.8 19.1 %copy-start.2 = (f32[512,512]{0,1:T(8,128)}, f32[512,512]{0,1:T(8,128)S(1)}, u32[]{:S(2)}) copy-start(f32[512,512]{0,1:T(8,128)S(1)} %fusion.12) | copy-start | bytes 3145732
  213.0 3.5 %copy-start.7 = (f32[128,128]{1,0:T(8,128)S(1)}, f32[128,128]{1,0:T(8,128)}, u32[]{:S(2)}) copy-start(f32[128,128]{1,0:T(8,128)} %get-tuple-element.108) | copy-start | bytes 196612
  235.7 19.4 %copy-start.1 = (f32[512,512]{1,0:T(8,128)}, f32[512,512]{1,0:T(8,128)S(1)}, u32[]{:S(2)}) copy-start(f32[512,512]{1,0:T(8,128)S(1)} %maximum_dynamic-update-slice_fusion) | copy-start | bytes 3145732
  255.1 20.1 %copy-start.5 = (f32[128,128]{1,0:T(8,128)S(1)}, f32[128,128]{1,0:T(8,128)}, u32[]{:S(2)}) copy-start(f32[128,128]{1,0:T(8,128)} %get-tuple-element.110) | copy-start | bytes 196612
  256.9 20.7 %copy-start.6 = (f32[128,128]{1,0:T(8,128)S(1)}, f32[128,128]{1,0:T(8,128)}, u32[]{:S(2)}) copy-start(f32[128,128]{1,0:T(8,128)} %get-tuple-element.112) | copy-start | bytes 196612
  275.6 5.0 %copy-start.8 = (f32[128,128]{1,0:T(8,128)S(1)}, f32[128,128]{1,0:T(8,128)}, u32[]{:S(2)}) copy-start(f32[128,128]{1,0:T(8,128)} %get-tuple-element.114) | copy-start | bytes 196612
  275.6 5.4 %copy-start.10 = (f32[512]{0:T(512)S(1)}, f32[512]{0:T(512)}, u32[]{:S(2)}) copy-start(f32[512]{0:T(512)} %slice.345) | copy-start | bytes 6148

commit v5 on v4

--- a/solution.py
+++ b/solution.py
@@ -74,13 +74,15 @@
 
 def summed_everywhere(arrays):
     flat = jnp.concatenate([a.reshape(-1) for a in arrays])
-    peers = lax.axis_size("cols")
+    n_cols, n_mem = lax.axis_size("cols"), lax.axis_size("mem")
     size = flat.shape[0]
-    width = -(-size // peers)
-    flat = jnp.pad(flat, (0, width * peers - size))
-    pieces = lax.all_to_all(flat.reshape(peers, width), "cols", 0, 0, tiled=True)
-    mine = lax.psum(jnp.sum(pieces, axis=0), "mem")
-    total, at, done = sent_to_all(mine, "cols").reshape(-1), 0, []
+    width = -(-size // (n_cols * n_mem))
+    flat = jnp.pad(flat, (0, width * n_cols * n_mem - size))
+    part = lax.all_to_all(flat.reshape(n_mem, n_cols * width), "mem", 0, 0, tiled=True)
+    pieces = lax.all_to_all(jnp.sum(part, axis=0).reshape(n_cols, width), "cols", 0, 0, tiled=True)
+    mine = jnp.sum(pieces, axis=0)
+    back = sent_to_all(mine, "cols").reshape(-1)
+    total, at, done = sent_to_all(back, "mem").reshape(-1), 0, []
     for a in arrays:
         done.append(total[at : at + a.size].reshape(a.shape))
         at += a.size

time: 286 us -> 275 us (0.962)
  blocking collectives: 21.7 us -> 48.1 us
  waiting for transfers between devices: 77.9 us -> 52.6 us
  starting transfers between devices: 63.5 us -> 48.4 us
    all_to_all x0 -> x2, blocking collectives: none -> 48.1 us  [the longest x1 38.7 us: summed_everywhere(): lax.all_to_all(jnp.sum(part, axis=0).reshape(n_cols, width), 'cols', 0, 0...]
    all_to_all x1 -> x0, waiting for transfers between devices: 35.3 us -> none  [summed_everywhere(): lax.all_to_all(flat.reshape(peers, width), 'cols', 0, 0, tiled=True)]
    psum x1 -> x0, blocking collectives: 21.7 us -> none  [summed_everywhere(): mine = lax.psum(jnp.sum(pieces, axis=0), 'mem')]
    all_to_all x1 -> x0, starting transfers between devices: 16.7 us -> none  [summed_everywhere(): lax.all_to_all(flat.reshape(peers, width), 'cols', 0, 0, tiled=True)]
    all_to_all x4 -> x5, waiting for transfers between devices: 35.5 us -> 45.5 us  [sent_to_all(): lax.all_to_all(jnp.broadcast_to(shard[None], (peers, *shard.shape)), axis...]
    all_to_all x4 -> x5, starting transfers between devices: 37.8 us -> 39.5 us  [sent_to_all(): lax.all_to_all(jnp.broadcast_to(shard[None], (peers, *shard.shape)), axis...]
  transfers between devices with their start and end apart: 8 -> 8, of which waited for: 6 -> 7; matrix products, arithmetic and copies ran while one was open for 5% -> 5% of each run, Pallas kernels for 0% -> 0%
where the time goes in v5:
time: 275 us; the launch traced here: 271 us
  Pallas kernels  61.1 us (22%)
  waiting for transfers between devices  52.6 us (19%)
  starting transfers between devices  48.4 us (18%)
  blocking collectives  48.1 us (17%)
  matrix products  23.1 us (8%)
  local copies, waits for them, and re-layouts  21.7 us (8%)
  other arithmetic  14.1 us (5%)
    pallas_call x4, Pallas kernels, factor_block(): pl.pallas_call(_eliminate, out_shape=(square, square), in_specs=[pl.Block...  61.1 us
    all_to_all x5, waiting for transfers between devices, sent_to_all(): lax.all_to_all(jnp.broadcast_to(shard[None], (peers, *shard.shape)), axis...  45.5 us
    all_to_all x5, starting transfers between devices, sent_to_all(): lax.all_to_all(jnp.broadcast_to(shard[None], (peers, *shard.shape)), axis...  39.5 us
    all_to_all x1, blocking collectives, summed_everywhere(): lax.all_to_all(jnp.sum(part, axis=0).reshape(n_cols, width), 'cols', 0, 0...  38.7 us
    all_to_all x1, blocking collectives, summed_everywhere(): lax.all_to_all(flat.reshape(n_mem, n_cols * width), 'mem', 0, 0, tiled=True)  9.4 us
    all_to_all x1, waiting for transfers between devices, body(): lax.all_to_all(spread, 'mem', 0, 2, tiled=True).astype(jnp.float32)  6.48 us
    dot_general x3, matrix products, factor_inverse(): jnp.dot(chol[begin:finish, :begin], chol_inverse[:begin], precision=top)  6.18 us
  transfers between devices with their start and end apart: 8, of which 7 were waited for; matrix products, arithmetic and copies ran while one was open for 5% of the time, Pallas kernels for 0%

profile of v5, /device:TPU:1, one launch (start us, length us, event | category | flops | bytes accessed | tf_op | source)
XLA Modules:
  0.0 270.5 jit_solution(17638270639820829444)
XLA Ops:
  1.3 20.4 %all-to-all-start.3 = ((f32[128,1,1]{2,1,0:T(1,128)}), f32[128,1,1]{2,1,0:T(1,128)S(1)}, u32[]{:S(2)}, u32[]{:S(2)}) async-start(f32[128,1,1]{2,1,0:T(1,128)} %broadcast_in_dim.88), calls=%async_computation.3 | async-start | bytes 131072 | tf_op jit(solution)/shard_map/all_to_all | solution.py:26
  22.8 3.5 %collective-permute-start = (bf16[1,100,128]{2,1,0:T(8,128)(2,1)S(1)}, bf16[1,100,128]{2,1,0:T(8,128)(2,1)S(1)}, u32[]{:S(2)}, u32[]{:S(2)}) collective-permute-start(bf16[1,100,128]{2,1,0:T(8,128)(2,1)S(1)} %get-tuple-element.119), channel_id=1, source_target_pairs={{0,4},{4,8},{8,12},{12,16},{16,20},{20,24},{24,28},{28,32},{32,36}... | collective-permute-start | bytes 76808 | tf_op jit(solution)/shard_map/ppermute | solution.py:16
  26.4 1.9 collective-permute-start.1
  33.7 3.0 %all-to-all-done.3 = f32[128,1,1]{2,1,0:T(1,128)S(1)} async-done(((f32[128,1,1]{2,1,0:T(1,128)}), f32[128,1,1]{2,1,0:T(1,128)S(1)}, u32[]{:S(2)}, u32[]{:S(2)}) %all-to-all-start.3) | async-done | bytes 544 | tf_op jit(solution)/shard_map/all_to_all | solution.py:26
  37.3 4.2 %all-to-all-start = ((f32[4,16,100]{2,1,0:T(8,128)}), f32[4,16,100]{2,1,0:T(8,128)S(1)}, u32[]{:S(2)}, u32[]{:S(2)}) async-start(f32[4,16,100]{2,1,0:T(8,128)} %broadcast_in_dim.84), calls=%async_computation | async-start | bytes 65536 | tf_op jit(solution)/shard_map/all_to_all | solution.py:26
  43.9 1.9 all-to-all-done
  48.8 3.5 %all-to-all-start.2 = ((bf16[128,16,128]{2,1,0:T(8,128)(2,1)}), bf16[128,16,128]{2,1,0:T(8,128)(2,1)S(1)}, u32[]{:S(2)}, u32[]{:S(2)}) async-start(bf16[128,16,128]{2,1,0:T(8,128)(2,1)} %copy.197), calls=%async_computation.2 | async-start | bytes 1048576 | tf_op jit(solution)/shard_map/all_to_all | solution.py:210
  52.7 6.5 %all-to-all-done.2 = bf16[128,16,128]{2,1,0:T(8,128)(2,1)S(1)} async-done(((bf16[128,16,128]{2,1,0:T(8,128)(2,1)}), bf16[128,16,128]{2,1,0:T(8,128)(2,1)S(1)}, u32[]{:S(2)}, u32[]{:S(2)}) %all-to-all-start.2) | async-done | bytes 524320 | tf_op jit(solution)/shard_map/all_to_all | solution.py:210
  61.9 2.4 gather_fusion.1
  64.4 9.4 %all_to_all.65 = f32[4,1,33024]{2,1,0:T(1,128)S(1)} all-to-all(f32[4,1,33024]{2,1,0:T(1,128)S(1)} %bitcast.96), channel_id=1, replica_groups=mesh['cols'=128,'mem'=4] {'mem'}, dimensions={0} | all-to-all | bytes 1056768 | tf_op jit(solution)/shard_map/all_to_all | solution.py:81
  74.7 38.7 %all_to_all.66 = f32[128,1,258]{2,1,0:T(1,128)S(1)} all-to-all(f32[128,1,258]{2,1,0:T(1,128)S(1)} %all_to_all.56), channel_id=1, replica_groups=mesh['cols'=128,'mem'=4] {'cols'}, dimensions={0} | all-to-all | bytes 264192 | tf_op jit(solution)/shard_map/all_to_all | solution.py:82
  114.4 7.2 %all-to-all-start.6 = ((f32[128,1,258]{2,1,0:T(1,128)}), f32[128,1,258]{2,1,0:T(1,128)S(1)}, u32[]{:S(2)}, u32[]{:S(2)}) async-start(f32[128,1,258]{2,1,0:T(1,128)} %broadcast_in_dim.89), calls=%async_computation.6 | async-start | bytes 393216 | tf_op jit(solution)/shard_map/all_to_all | solution.py:26
  121.9 19.6 %all-to-all-done.6 = f32[128,1,258]{2,1,0:T(1,128)S(1)} async-done(((f32[128,1,258]{2,1,0:T(1,128)}), f32[128,1,258]{2,1,0:T(1,128)S(1)}, u32[]{:S(2)}, u32[]{:S(2)}) %all-to-all-start.6) | async-done | bytes 132128 | tf_op jit(solution)/shard_map/all_to_all | solution.py:26
  141.5 1.4 broadcast_in_dim.85
  142.9 3.6 %all-to-all-start.1 = ((bf16[4,16,100,128]{3,1,2,0:T(8,128)(2,1)}), bf16[4,16,100,128]{3,1,2,0:T(8,128)(2,1)S(1)}, u32[]{:S(2)}, u32[]{:S(2)}) async-start(bf16[4,16,100,128]{3,1,2,0:T(8,128)(2,1)} %broadcast_in_dim.85), calls=%async_computation.1 | async-start | bytes 3276800 | tf_op jit(solution)/shard_map/all_to_all | solution.py:26
  147.2 18.7 %all-to-all-done.1 = bf16[4,16,100,128]{3,1,2,0:T(8,128)(2,1)S(1)} async-done(((bf16[4,16,100,128]{3,1,2,0:T(8,128)(2,1)}), bf16[4,16,100,128]{3,1,2,0:T(8,128)(2,1)S(1)}, u32[]{:S(2)}, u32[]{:S(2)}) %all-to-all-start.1) | async-done | bytes 1638432 | tf_op jit(solution)/shard_map/all_to_all | solution.py:26
  167.0 4.1 %all-to-all-start.7 = ((f32[4,1,33024]{2,1,0:T(1,128)}), f32[4,1,33024]{2,1,0:T(1,128)}, u32[]{:S(2)}, u32[]{:S(2)}) async-start(f32[4,1,33024]{2,1,0:T(1,128)} %broadcast_in_dim.91), calls=%async_computation.7 | async-start | bytes 1056768 | tf_op jit(solution)/shard_map/all_to_all | solution.py:26
  174.0 1.3 copy.237
  175.9 2.3 all-to-all-done.7
  178.9 1.3 slice.345
  180.1 2.4 reduce.25
  184.3 15.2 %shard_map.100 = (f32[128,128]{1,0:T(8,128)}, f32[128,128]{1,0:T(8,128)}) custom-call(f32[128,128]{1,0:T(8,128)} %bitcast_add_fusion.4.a_ref), custom_call_target="tpu_custom_call" | custom-call | tf_op jit(solution)/shard_map/pallas_call | solution.py:132
  200.4 1.3 fusion.39
  204.7 15.2 %shard_map.101 = (f32[128,128]{1,0:T(8,128)}, f32[128,128]{1,0:T(8,128)}) custom-call(f32[128,128]{1,0:T(8,128)} %bitcast_add_fusion.3.a_ref), custom_call_target="tpu_custom_call" | custom-call | tf_op jit(solution)/shard_map/pallas_call | solution.py:132
  219.9 1.2 fusion.47
  222.1 1.4 convolution_subtract_fusion.4
  224.3 15.2 %shard_map.102 = (f32[128,128]{1,0:T(8,128)}, f32[128,128]{1,0:T(8,128)}) custom-call(f32[128,128]{1,0:T(8,128)} %bitcast_add_fusion.2.a_ref), custom_call_target="tpu_custom_call" | custom-call | tf_op jit(solution)/shard_map/pallas_call | solution.py:132
  241.7 1.6 convolution_subtract_fusion.1
  244.0 1.4 broadcast_select_fusion.1
  246.2 15.4 %shard_map.103 = (f32[128,128]{1,0:T(8,128)}, f32[128,128]{1,0:T(8,128)}) custom-call(f32[128,128]{1,0:T(8,128)} %bitcast_add_fusion.1.a_ref), custom_call_target="tpu_custom_call" | custom-call | tf_op jit(solution)/shard_map/pallas_call | solution.py:132
  262.0 2.0 convolution_subtract_fusion
  264.4 2.6 convolution_subtract_fusion.2
  (119 shorter events, 39.2 us)
Async XLA Ops:
  0.0 31.9 %copy-start = (bf16[100,256]{1,0:T(8,128)(2,1)S(1)}, bf16[100,256]{1,0:T(8,128)(2,1)}, u32[]{:S(2)}) copy-start(bf16[100,256]{1,0:T(8,128)(2,1)} %param.27) | copy-start | bytes 153604
  1.3 35.4 %all-to-all-start.3 = ((f32[128,1,1]{2,1,0:T(1,128)}), f32[128,1,1]{2,1,0:T(1,128)S(1)}, u32[]{:S(2)}, u32[]{:S(2)}) async-start(f32[128,1,1]{2,1,0:T(1,128)} %broadcast_in_dim.88), calls=%async_computation.3 | async-start | bytes 131072 | tf_op jit(solution)/shard_map/all_to_all | solution.py:26
  22.8 8.4 %collective-permute-start = (bf16[1,100,128]{2,1,0:T(8,128)(2,1)S(1)}, bf16[1,100,128]{2,1,0:T(8,128)(2,1)S(1)}, u32[]{:S(2)}, u32[]{:S(2)}) collective-permute-start(bf16[1,100,128]{2,1,0:T(8,128)(2,1)S(1)} %get-tuple-element.119), channel_id=1, source_target_pairs={{0,4},{4,8},{8,12},{12,16},{16,20},{20,24},{24,28},{28,32},{32,36}... | collective-permute-start | bytes 76808 | tf_op jit(solution)/shard_map/ppermute | solution.py:16
  26.4 5.5 %collective-permute-start.1 = (bf16[1,100,128]{2,1,0:T(8,128)(2,1)S(1)}, bf16[1,100,128]{2,1,0:T(8,128)(2,1)S(1)}, u32[]{:S(2)}, u32[]{:S(2)}) collective-permute-start(bf16[1,100,128]{2,1,0:T(8,128)(2,1)S(1)} %get-tuple-element.120), channel_id=1, source_target_pairs={{4,0},{8,4},{12,8},{16,12},{20,16},{24,20},{28,24},{32,28},{36,32}... | collective-permute-start | bytes 76808 | tf_op jit(solution)/shard_map/ppermute | solution.py:19
  31.2 1.7 copy-start.3
  31.2 1.7 copy-start.12
  32.9 12.9 %copy-start.8 = (f32[100,16]{0,1:T(8,128)S(1)}, f32[100,16]{0,1:T(8,128)}, u32[]{:S(2)}) copy-start(f32[100,16]{0,1:T(8,128)} %param.30) | copy-start | bytes 19204
  33.7 12.9 %copy-start.10 = (f32[128,16]{0,1:T(8,128)S(1)}, f32[128,16]{0,1:T(8,128)}, u32[]{:S(2)}) copy-start(f32[128,16]{0,1:T(8,128)} %param.34) | copy-start | bytes 24580
  37.3 8.5 %all-to-all-start = ((f32[4,16,100]{2,1,0:T(8,128)}), f32[4,16,100]{2,1,0:T(8,128)S(1)}, u32[]{:S(2)}, u32[]{:S(2)}) async-start(f32[4,16,100]{2,1,0:T(8,128)} %broadcast_in_dim.84), calls=%async_computation | async-start | bytes 65536 | tf_op jit(solution)/shard_map/all_to_all | solution.py:26
  46.6 6.0 %copy-start.11 = (f32[128,16]{0,1:T(8,128)S(1)}, f32[128,16]{0,1:T(8,128)}, u32[]{:S(2)}) copy-start(f32[128,16]{0,1:T(8,128)} %param.33) | copy-start | bytes 24580
  48.8 10.4 %all-to-all-start.2 = ((bf16[128,16,128]{2,1,0:T(8,128)(2,1)}), bf16[128,16,128]{2,1,0:T(8,128)(2,1)S(1)}, u32[]{:S(2)}, u32[]{:S(2)}) async-start(bf16[128,16,128]{2,1,0:T(8,128)(2,1)} %copy.197), calls=%async_computation.2 | async-start | bytes 1048576 | tf_op jit(solution)/shard_map/all_to_all | solution.py:210
  114.4 27.1 %all-to-all-start.6 = ((f32[128,1,258]{2,1,0:T(1,128)}), f32[128,1,258]{2,1,0:T(1,128)S(1)}, u32[]{:S(2)}, u32[]{:S(2)}) async-start(f32[128,1,258]{2,1,0:T(1,128)} %broadcast_in_dim.89), calls=%async_computation.6 | async-start | bytes 393216 | tf_op jit(solution)/shard_map/all_to_all | solution.py:26
  142.9 23.1 %all-to-all-start.1 = ((bf16[4,16,100,128]{3,1,2,0:T(8,128)(2,1)}), bf16[4,16,100,128]{3,1,2,0:T(8,128)(2,1)S(1)}, u32[]{:S(2)}, u32[]{:S(2)}) async-start(bf16[4,16,100,128]{3,1,2,0:T(8,128)(2,1)} %broadcast_in_dim.85), calls=%async_computation.1 | async-start | bytes 3276800 | tf_op jit(solution)/shard_map/all_to_all | solution.py:26
  167.0 11.2 %all-to-all-start.7 = ((f32[4,1,33024]{2,1,0:T(1,128)}), f32[4,1,33024]{2,1,0:T(1,128)}, u32[]{:S(2)}, u32[]{:S(2)}) async-start(f32[4,1,33024]{2,1,0:T(1,128)} %broadcast_in_dim.91), calls=%async_computation.7 | async-start | bytes 1056768 | tf_op jit(solution)/shard_map/all_to_all | solution.py:26
  183.3 19.1 %copy-start.2 = (f32[512,512]{0,1:T(8,128)}, f32[512,512]{0,1:T(8,128)S(1)}, u32[]{:S(2)}) copy-start(f32[512,512]{0,1:T(8,128)S(1)} %fusion.12) | copy-start | bytes 3145732
  199.5 3.4 %copy-start.6 = (f32[128,128]{1,0:T(8,128)S(1)}, f32[128,128]{1,0:T(8,128)}, u32[]{:S(2)}) copy-start(f32[128,128]{1,0:T(8,128)} %get-tuple-element.108) | copy-start | bytes 196612
  222.1 19.3 %copy-start.1 = (f32[512,512]{1,0:T(8,128)}, f32[512,512]{1,0:T(8,128)S(1)}, u32[]{:S(2)}) copy-start(f32[512,512]{1,0:T(8,128)S(1)} %maximum_dynamic-update-slice_fusion) | copy-start | bytes 3145732
  241.5 20.1 %copy-start.4 = (f32[128,128]{1,0:T(8,128)S(1)}, f32[128,128]{1,0:T(8,128)}, u32[]{:S(2)}) copy-start(f32[128,128]{1,0:T(8,128)} %get-tuple-element.110) | copy-start | bytes 196612
  243.3 20.7 %copy-start.5 = (f32[128,128]{1,0:T(8,128)S(1)}, f32[128,128]{1,0:T(8,128)}, u32[]{:S(2)}) copy-start(f32[128,128]{1,0:T(8,128)} %get-tuple-element.112) | copy-start | bytes 196612
  262.0 5.0 %copy-start.7 = (f32[128,128]{1,0:T(8,128)S(1)}, f32[128,128]{1,0:T(8,128)}, u32[]{:S(2)}) copy-start(f32[128,128]{1,0:T(8,128)} %get-tuple-element.114) | copy-start | bytes 196612
  262.0 5.4 %copy-start.9 = (f32[512]{0:T(512)S(1)}, f32[512]{0:T(512)}, u32[]{:S(2)}) copy-start(f32[512]{0:T(512)} %slice.345) | copy-start | bytes 6148

commit v6 on v5

--- a/solution.py
+++ b/solution.py
@@ -207,7 +207,20 @@
     factor = every_inflation[owner[:, 0]] ** 2
     quarter = src_b // n_mem
     first_batch = lax.axis_index("mem") * quarter
-    portion = lax.all_to_all(spread, "mem", 0, 2, tiled=True).astype(jnp.float32)
+    pertb = departure_from_average.astype(jnp.bfloat16)
+    own = pertb.shape[0] * pertb.shape[1]
+    outgoing = jnp.concatenate(
+        [
+            jnp.broadcast_to(pertb.reshape(1, own, mem_dev), (n_mem, own, mem_dev)),
+            spread.reshape(n_mem, -1, mem_dev),
+        ],
+        axis=1,
+    )
+    incoming = lax.all_to_all(outgoing, "mem", 0, 0, tiled=True)
+    every_pertb = joined_along(incoming[:, :own].reshape(n_mem, *pertb.shape), 2)
+    portion = joined_along(
+        incoming[:, own:].reshape(n_mem, quarter, *spread.shape[1:]), 2
+    ).astype(jnp.float32)
     innov_part = lax.dynamic_slice_in_dim(innov, first_batch, quarter, 0)
     factor_part = lax.dynamic_slice_in_dim(factor, first_batch, quarter, 0)
     weighted = portion * factor_part[:, None, None]
@@ -232,10 +245,7 @@
     first = lax.axis_index("mem") * mem_dev
     tinv_mine = lax.dynamic_slice_in_dim(chol_inverse, first, mem_dev, 0).T
     mix_w = (weights[:, None] * scale + tinv_mine).astype(jnp.bfloat16)
-    pertb = departure_from_average.astype(jnp.bfloat16)
-    moved = jnp.einsum(
-        "kcm,mj->kcj", collect(pertb, "mem", 2), mix_w, preferred_element_type=jnp.float32
-    )
+    moved = jnp.einsum("kcm,mj->kcj", every_pertb, mix_w, preferred_element_type=jnp.float32)
     return (profile_average[:, :, None] + moved).astype(jnp.bfloat16)
 
 

time: 275 us -> 271 us (0.985)
  blocking collectives: 48.1 us -> 38.9 us
  waiting for transfers between devices: 52.6 us -> 57.1 us
    all_to_all x1, waiting for transfers between devices: 6.48 us -> 22.9 us  [body(): incoming = lax.all_to_all(outgoing, 'mem', 0, 0, tiled=True)]
    all_to_all x5 -> x4, waiting for transfers between devices: 45.5 us -> 34.3 us  [sent_to_all(): lax.all_to_all(jnp.broadcast_to(shard[None], (peers, *shard.shape)), axis...]
    all_to_all x1, blocking collectives: 38.7 us -> 29.4 us  [summed_everywhere(): lax.all_to_all(jnp.sum(part, axis=0).reshape(n_cols, width), 'cols', 0, 0...]
    all_to_all x5 -> x4, starting transfers between devices: 39.5 us -> 34.2 us  [sent_to_all(): lax.all_to_all(jnp.broadcast_to(shard[None], (peers, *shard.shape)), axis...]
    ppermute x1, starting transfers between devices: 1.92 us -> 5.11 us  [extended(): lax.ppermute(lax.slice_in_dim(block, 0, width, axis=dim), axis, backward)]
  transfers between devices with their start and end apart: 8 -> 7, of which waited for: 7 -> 4; matrix products, arithmetic and copies ran while one was open for 5% -> 6% of each run, Pallas kernels for 0% -> 0%
where the time goes in v6:
time: 271 us; the launch traced here: 268 us
  Pallas kernels  61.1 us (23%)
  waiting for transfers between devices  57.1 us (21%)
  starting transfers between devices  47.9 us (18%)
  blocking collectives  38.9 us (14%)
  local copies, waits for them, and re-layouts  23.6 us (9%)
  matrix products  23 us (8%)
  other arithmetic  15.3 us (6%)
    pallas_call x4, Pallas kernels, factor_block(): pl.pallas_call(_eliminate, out_shape=(square, square), in_specs=[pl.Block...  61.1 us
    all_to_all x4, waiting for transfers between devices, sent_to_all(): lax.all_to_all(jnp.broadcast_to(shard[None], (peers, *shard.shape)), axis...  34.3 us
    all_to_all x4, starting transfers between devices, sent_to_all(): lax.all_to_all(jnp.broadcast_to(shard[None], (peers, *shard.shape)), axis...  34.2 us
    all_to_all x1, blocking collectives, summed_everywhere(): lax.all_to_all(jnp.sum(part, axis=0).reshape(n_cols, width), 'cols', 0, 0...  29.4 us
    all_to_all x1, waiting for transfers between devices, body(): incoming = lax.all_to_all(outgoing, 'mem', 0, 0, tiled=True)  22.9 us
    all_to_all x1, blocking collectives, summed_everywhere(): lax.all_to_all(flat.reshape(n_mem, n_cols * width), 'mem', 0, 0, tiled=True)  9.47 us
    dot_general x3, matrix products, factor_inverse(): jnp.dot(chol[begin:finish, :begin], chol_inverse[:begin], precision=top)  6.16 us
  transfers between devices with their start and end apart: 7, of which 4 were waited for; matrix products, arithmetic and copies ran while one was open for 6% of the time, Pallas kernels for 0%

profile of v6, /device:TPU:1, one launch (start us, length us, event | category | flops | bytes accessed | tf_op | source)
XLA Modules:
  0.0 268.4 jit_solution(15599649410360799079)
XLA Ops:
  1.1 4.9 %collective-permute-start = (bf16[1,100,128]{2,1,0:T(8,128)(2,1)S(1)}, bf16[1,100,128]{2,1,0:T(8,128)(2,1)S(1)}, u32[]{:S(2)}, u32[]{:S(2)}) collective-permute-start(bf16[1,100,128]{2,1,0:T(8,128)(2,1)S(1)} %get-tuple-element.119), channel_id=1, source_target_pairs={{0,4},{4,8},{8,12},{12,16},{16,20},{20,24},{24,28},{28,32},{32,36}... | collective-permute-start | bytes 76808 | tf_op jit(solution)/shard_map/ppermute | solution.py:16
  6.1 5.1 %collective-permute-start.1 = (bf16[1,100,128]{2,1,0:T(8,128)(2,1)S(1)}, bf16[1,100,128]{2,1,0:T(8,128)(2,1)S(1)}, u32[]{:S(2)}, u32[]{:S(2)}) collective-permute-start(bf16[1,100,128]{2,1,0:T(8,128)(2,1)S(1)} %get-tuple-element.120), channel_id=1, source_target_pairs={{4,0},{8,4},{12,8},{16,12},{20,16},{24,20},{28,24},{32,28},{36,32}... | collective-permute-start | bytes 76808 | tf_op jit(solution)/shard_map/ppermute | solution.py:19
  15.2 3.3 %all-to-all-start = ((f32[4,16,100]{2,1,0:T(8,128)}), f32[4,16,100]{2,1,0:T(8,128)S(1)}, u32[]{:S(2)}, u32[]{:S(2)}) async-start(f32[4,16,100]{2,1,0:T(8,128)} %broadcast_in_dim.85), calls=%async_computation | async-start | bytes 65536 | tf_op jit(solution)/shard_map/all_to_all | solution.py:26
  19.2 3.7 %all-to-all-done = f32[4,16,100]{2,1,0:T(8,128)S(1)} async-done(((f32[4,16,100]{2,1,0:T(8,128)}), f32[4,16,100]{2,1,0:T(8,128)S(1)}, u32[]{:S(2)}, u32[]{:S(2)}) %all-to-all-start) | async-done | bytes 25632 | tf_op jit(solution)/shard_map/all_to_all | solution.py:26
  23.5 19.4 %all-to-all-start.2 = ((f32[128,1,1]{2,1,0:T(1,128)}), f32[128,1,1]{2,1,0:T(1,128)S(1)}, u32[]{:S(2)}, u32[]{:S(2)}) async-start(f32[128,1,1]{2,1,0:T(1,128)} %broadcast_in_dim.90), calls=%async_computation.2 | async-start | bytes 131072 | tf_op jit(solution)/shard_map/all_to_all | solution.py:26
  45.7 1.5 pad_maximum_fusion
  47.2 10.7 %all-to-all-done.2 = f32[128,1,1]{2,1,0:T(1,128)S(1)} async-done(((f32[128,1,1]{2,1,0:T(1,128)}), f32[128,1,1]{2,1,0:T(1,128)S(1)}, u32[]{:S(2)}, u32[]{:S(2)}) %all-to-all-start.2) | async-done | bytes 544 | tf_op jit(solution)/shard_map/all_to_all | solution.py:26
  57.9 3.6 %all-to-all-start.1 = ((bf16[4,2112,128]{2,1,0:T(8,128)(2,1)}), bf16[4,2112,128]{2,1,0:T(8,128)(2,1)S(1)}, u32[]{:S(2)}, u32[]{:S(2)}) async-start(bf16[4,2112,128]{2,1,0:T(8,128)(2,1)} %pad_maximum_fusion), calls=%async_computation.1 | async-start | bytes 4325376 | tf_op jit(solution)/shard_map/all_to_all | solution.py:219
  62.6 1.2 gather_fusion
  64.4 22.9 %all-to-all-done.1 = bf16[4,2112,128]{2,1,0:T(8,128)(2,1)S(1)} async-done(((bf16[4,2112,128]{2,1,0:T(8,128)(2,1)}), bf16[4,2112,128]{2,1,0:T(8,128)(2,1)S(1)}, u32[]{:S(2)}, u32[]{:S(2)}) %all-to-all-start.1) | async-done | bytes 2162720 | tf_op jit(solution)/shard_map/all_to_all | solution.py:219
  91.1 2.4 gather_fusion.1
  93.6 9.5 %all_to_all.47 = f32[4,1,33024]{2,1,0:T(1,128)S(1)} all-to-all(f32[4,1,33024]{2,1,0:T(1,128)S(1)} %bitcast.96), channel_id=1, replica_groups=mesh['cols'=128,'mem'=4] {'mem'}, dimensions={0} | all-to-all | bytes 1056768 | tf_op jit(solution)/shard_map/all_to_all | solution.py:81
  104.0 29.4 %all_to_all.48 = f32[128,1,258]{2,1,0:T(1,128)S(1)} all-to-all(f32[128,1,258]{2,1,0:T(1,128)S(1)} %all_to_all.39), channel_id=1, replica_groups=mesh['cols'=128,'mem'=4] {'cols'}, dimensions={0} | all-to-all | bytes 264192 | tf_op jit(solution)/shard_map/all_to_all | solution.py:82
  134.3 7.2 %all-to-all-start.5 = ((f32[128,1,258]{2,1,0:T(1,128)}), f32[128,1,258]{2,1,0:T(1,128)S(1)}, u32[]{:S(2)}, u32[]{:S(2)}) async-start(f32[128,1,258]{2,1,0:T(1,128)} %broadcast_in_dim.91), calls=%async_computation.5 | async-start | bytes 393216 | tf_op jit(solution)/shard_map/all_to_all | solution.py:26
  141.6 19.9 %all-to-all-done.5 = f32[128,1,258]{2,1,0:T(1,128)S(1)} async-done(((f32[128,1,258]{2,1,0:T(1,128)}), f32[128,1,258]{2,1,0:T(1,128)S(1)}, u32[]{:S(2)}, u32[]{:S(2)}) %all-to-all-start.5) | async-done | bytes 132128 | tf_op jit(solution)/shard_map/all_to_all | solution.py:26
  163.3 4.3 %all-to-all-start.6 = ((f32[4,1,33024]{2,1,0:T(1,128)}), f32[4,1,33024]{2,1,0:T(1,128)}, u32[]{:S(2)}, u32[]{:S(2)}) async-start(f32[4,1,33024]{2,1,0:T(1,128)} %broadcast_in_dim.93), calls=%async_computation.6 | async-start | bytes 1056768 | tf_op jit(solution)/shard_map/all_to_all | solution.py:26
  170.5 1.3 slice.325
  171.8 2.3 reshape.283
  174.1 1.3 copy.270
  176.7 1.2 slice.355
  178.0 2.4 reduce.25
  182.0 15.2 %shard_map.100 = (f32[128,128]{1,0:T(8,128)}, f32[128,128]{1,0:T(8,128)}) custom-call(f32[128,128]{1,0:T(8,128)} %bitcast_add_fusion.4.a_ref), custom_call_target="tpu_custom_call" | custom-call | tf_op jit(solution)/shard_map/pallas_call | solution.py:132
  198.2 1.3 fusion.39
  202.6 15.2 %shard_map.101 = (f32[128,128]{1,0:T(8,128)}, f32[128,128]{1,0:T(8,128)}) custom-call(f32[128,128]{1,0:T(8,128)} %bitcast_add_fusion.3.a_ref), custom_call_target="tpu_custom_call" | custom-call | tf_op jit(solution)/shard_map/pallas_call | solution.py:132
  217.8 1.2 fusion.47
  220.0 1.4 convolution_subtract_fusion.4
  222.2 15.2 %shard_map.102 = (f32[128,128]{1,0:T(8,128)}, f32[128,128]{1,0:T(8,128)}) custom-call(f32[128,128]{1,0:T(8,128)} %bitcast_add_fusion.2.a_ref), custom_call_target="tpu_custom_call" | custom-call | tf_op jit(solution)/shard_map/pallas_call | solution.py:132
  239.6 1.6 convolution_subtract_fusion.1
  241.8 1.4 broadcast_select_fusion.1
  244.0 15.5 %shard_map.103 = (f32[128,128]{1,0:T(8,128)}, f32[128,128]{1,0:T(8,128)}) custom-call(f32[128,128]{1,0:T(8,128)} %bitcast_add_fusion.1.a_ref), custom_call_target="tpu_custom_call" | custom-call | tf_op jit(solution)/shard_map/pallas_call | solution.py:132
  259.8 2.0 convolution_subtract_fusion
  262.3 2.6 convolution_subtract_fusion.2
  (127 shorter events, 36.7 us)
Async XLA Ops:
  0.0 12.7 %copy-start = (bf16[100,256]{1,0:T(8,128)(2,1)S(1)}, bf16[100,256]{1,0:T(8,128)(2,1)}, u32[]{:S(2)}) copy-start(bf16[100,256]{1,0:T(8,128)(2,1)} %param.27) | copy-start | bytes 153604
  1.1 11.6 %collective-permute-start = (bf16[1,100,128]{2,1,0:T(8,128)(2,1)S(1)}, bf16[1,100,128]{2,1,0:T(8,128)(2,1)S(1)}, u32[]{:S(2)}, u32[]{:S(2)}) collective-permute-start(bf16[1,100,128]{2,1,0:T(8,128)(2,1)S(1)} %get-tuple-element.119), channel_id=1, source_target_pairs={{0,4},{4,8},{8,12},{12,16},{16,20},{20,24},{24,28},{28,32},{32,36}... | collective-permute-start | bytes 76808 | tf_op jit(solution)/shard_map/ppermute | solution.py:16
  6.1 6.6 %collective-permute-start.1 = (bf16[1,100,128]{2,1,0:T(8,128)(2,1)S(1)}, bf16[1,100,128]{2,1,0:T(8,128)(2,1)S(1)}, u32[]{:S(2)}, u32[]{:S(2)}) collective-permute-start(bf16[1,100,128]{2,1,0:T(8,128)(2,1)S(1)} %get-tuple-element.120), channel_id=1, source_target_pairs={{4,0},{8,4},{12,8},{16,12},{20,16},{24,20},{28,24},{32,28},{36,32}... | collective-permute-start | bytes 76808 | tf_op jit(solution)/shard_map/ppermute | solution.py:19
  12.7 1.0 copy-start.4
  12.7 1.0 copy-start.14
  13.7 4.7 %copy-start.13 = (s32[128,4]{0,1:T(4,128)S(1)}, s32[128,4]{0,1:T(4,128)}, u32[]{:S(2)}) copy-start(s32[128,4]{0,1:T(4,128)} %param.31) | copy-start | bytes 6148
  13.8 29.5 %copy-start.9 = (f32[100,16]{0,1:T(8,128)S(1)}, f32[100,16]{0,1:T(8,128)}, u32[]{:S(2)}) copy-start(f32[100,16]{0,1:T(8,128)} %param.30) | copy-start | bytes 19204
  14.6 29.5 %copy-start.11 = (f32[128,16]{0,1:T(8,128)S(1)}, f32[128,16]{0,1:T(8,128)}, u32[]{:S(2)}) copy-start(f32[128,16]{0,1:T(8,128)} %param.34) | copy-start | bytes 24580
  15.2 7.6 %all-to-all-start = ((f32[4,16,100]{2,1,0:T(8,128)}), f32[4,16,100]{2,1,0:T(8,128)S(1)}, u32[]{:S(2)}, u32[]{:S(2)}) async-start(f32[4,16,100]{2,1,0:T(8,128)} %broadcast_in_dim.85), calls=%async_computation | async-start | bytes 65536 | tf_op jit(solution)/shard_map/all_to_all | solution.py:26
  23.5 34.4 %all-to-all-start.2 = ((f32[128,1,1]{2,1,0:T(1,128)}), f32[128,1,1]{2,1,0:T(1,128)S(1)}, u32[]{:S(2)}, u32[]{:S(2)}) async-start(f32[128,1,1]{2,1,0:T(1,128)} %broadcast_in_dim.90), calls=%async_computation.2 | async-start | bytes 131072 | tf_op jit(solution)/shard_map/all_to_all | solution.py:26
  47.2 14.3 %copy-start.15 = (s32[128,1]{0,1:T(1,128)S(1)}, s32[128,1]{0,1:T(1,128)}, u32[]{:S(2)}) copy-start(s32[128,1]{0,1:T(1,128)} %param.32) | copy-start | bytes 1540
  47.2 17.1 %copy-start.12 = (f32[128,16]{0,1:T(8,128)S(1)}, f32[128,16]{0,1:T(8,128)}, u32[]{:S(2)}) copy-start(f32[128,16]{0,1:T(8,128)} %param.33) | copy-start | bytes 24580
  57.9 29.3 %all-to-all-start.1 = ((bf16[4,2112,128]{2,1,0:T(8,128)(2,1)}), bf16[4,2112,128]{2,1,0:T(8,128)(2,1)S(1)}, u32[]{:S(2)}, u32[]{:S(2)}) async-start(bf16[4,2112,128]{2,1,0:T(8,128)(2,1)} %pad_maximum_fusion), calls=%async_computation.1 | async-start | bytes 4325376 | tf_op jit(solution)/shard_map/all_to_all | solution.py:219
  89.0 1.0 copy-start.3
  134.3 27.1 %all-to-all-start.5 = ((f32[128,1,258]{2,1,0:T(1,128)}), f32[128,1,258]{2,1,0:T(1,128)S(1)}, u32[]{:S(2)}, u32[]{:S(2)}) async-start(f32[128,1,258]{2,1,0:T(1,128)} %broadcast_in_dim.91), calls=%async_computation.5 | async-start | bytes 393216 | tf_op jit(solution)/shard_map/all_to_all | solution.py:26
  163.3 12.8 %all-to-all-start.6 = ((f32[4,1,33024]{2,1,0:T(1,128)}), f32[4,1,33024]{2,1,0:T(1,128)}, u32[]{:S(2)}, u32[]{:S(2)}) async-start(f32[4,1,33024]{2,1,0:T(1,128)} %broadcast_in_dim.93), calls=%async_computation.6 | async-start | bytes 1056768 | tf_op jit(solution)/shard_map/all_to_all | solution.py:26
  181.1 19.1 %copy-start.2 = (f32[512,512]{0,1:T(8,128)}, f32[512,512]{0,1:T(8,128)S(1)}, u32[]{:S(2)}) copy-start(f32[512,512]{0,1:T(8,128)S(1)} %fusion.12) | copy-start | bytes 3145732
  197.2 3.5 %copy-start.7 = (f32[128,128]{1,0:T(8,128)S(1)}, f32[128,128]{1,0:T(8,128)}, u32[]{:S(2)}) copy-start(f32[128,128]{1,0:T(8,128)} %get-tuple-element.108) | copy-start | bytes 196612
  220.0 19.3 %copy-start.1 = (f32[512,512]{1,0:T(8,128)}, f32[512,512]{1,0:T(8,128)S(1)}, u32[]{:S(2)}) copy-start(f32[512,512]{1,0:T(8,128)S(1)} %maximum_dynamic-update-slice_fusion) | copy-start | bytes 3145732
  221.5 37.9 %copy-start.5 = (f32[128,128]{1,0:T(8,128)S(1)}, f32[128,128]{1,0:T(8,128)}, u32[]{:S(2)}) copy-start(f32[128,128]{1,0:T(8,128)} %get-tuple-element.110) | copy-start | bytes 196612
  241.1 20.7 %copy-start.6 = (f32[128,128]{1,0:T(8,128)S(1)}, f32[128,128]{1,0:T(8,128)}, u32[]{:S(2)}) copy-start(f32[128,128]{1,0:T(8,128)} %get-tuple-element.112) | copy-start | bytes 196612
  259.5 5.4 %copy-start.8 = (f32[128,128]{1,0:T(8,128)S(1)}, f32[128,128]{1,0:T(8,128)}, u32[]{:S(2)}) copy-start(f32[128,128]{1,0:T(8,128)} %get-tuple-element.114) | copy-start | bytes 196612
  259.5 5.8 %copy-start.10 = (f32[512]{0:T(512)S(1)}, f32[512]{0:T(512)}, u32[]{:S(2)}) copy-start(f32[512]{0:T(512)} %slice.355) | copy-start | bytes 6148

commit v7 on v6

--- a/solution.py
+++ b/solution.py
@@ -101,20 +101,26 @@
 
 def _eliminate(a_ref, low_ref, inv_ref, m_ref):
     n = a_ref.shape[0]
-    sub = lax.broadcasted_iota(jnp.int32, (n, 1), 0)
-    lane = lax.broadcasted_iota(jnp.int32, (1, n), 1)
+    tile = 16
     rows = lax.broadcasted_iota(jnp.int32, (n, n), 0)
     cols = lax.broadcasted_iota(jnp.int32, (n, n), 1)
+    sub = lax.broadcasted_iota(jnp.int32, (tile, 1), 0)
+    lane = lax.broadcasted_iota(jnp.int32, (1, n), 1)
     m_ref[:, :n] = a_ref[...]
     m_ref[:, n:] = (rows == cols).astype(jnp.float32)
 
     def step(j, carry):
         row = m_ref[pl.ds(j, 1), :]
-        whole = m_ref[...]
-        column = jnp.sum(jnp.where(lane == j, whole[:, :n], 0.0), axis=1, keepdims=True)
         pivot = jnp.sum(jnp.where(lane == j, row[:, :n], 0.0), axis=1, keepdims=True)
-        factor = jnp.where(sub > j, column / pivot, 0.0)
-        m_ref[...] = whole - factor * row
+        for t in range(n // tile):
+
+            @pl.when(t * tile + tile - 1 > j)
+            def _():
+                block = m_ref[t * tile : (t + 1) * tile, :]
+                column = jnp.sum(jnp.where(lane == j, block[:, :n], 0.0), axis=1, keepdims=True)
+                factor = jnp.where(sub + t * tile > j, column / pivot, 0.0)
+                m_ref[t * tile : (t + 1) * tile, :] = block - factor * row
+
         return carry
 
     lax.fori_loop(0, n, step, 0)

time: 271 us -> 438 us (1.62)
  Pallas kernels: 61.1 us -> 229 us
    pallas_call x4, Pallas kernels: 61.1 us -> 229 us  [factor_block(): pl.pallas_call(_eliminate, out_shape=(square, square), in_specs=[pl.Block...]
  transfers between devices with their start and end apart: 7 -> 7, of which waited for: 4 -> 4; matrix products, arithmetic and copies ran while one was open for 6% -> 4% of each run, Pallas kernels for 0% -> 0%
where the time goes in v7:
time: 438 us; the launch traced here: 436 us
  Pallas kernels  229 us (52%)
  waiting for transfers between devices  57.1 us (13%)
  starting transfers between devices  47.9 us (11%)
  blocking collectives  38.9 us (9%)
  local copies, waits for them, and re-layouts  23.6 us (5%)
  matrix products  23.1 us (5%)
  other arithmetic  15.3 us (3%)
    pallas_call x4, Pallas kernels, factor_block(): pl.pallas_call(_eliminate, out_shape=(square, square), in_specs=[pl.Block...  229 us
    all_to_all x4, waiting for transfers between devices, sent_to_all(): lax.all_to_all(jnp.broadcast_to(shard[None], (peers, *shard.shape)), axis...  34.3 us
    all_to_all x4, starting transfers between devices, sent_to_all(): lax.all_to_all(jnp.broadcast_to(shard[None], (peers, *shard.shape)), axis...  34.2 us
    all_to_all x1, blocking collectives, summed_everywhere(): lax.all_to_all(jnp.sum(part, axis=0).reshape(n_cols, width), 'cols', 0, 0...  29.4 us
    all_to_all x1, waiting for transfers between devices, body(): incoming = lax.all_to_all(outgoing, 'mem', 0, 0, tiled=True)  22.9 us
    all_to_all x1, blocking collectives, summed_everywhere(): lax.all_to_all(flat.reshape(n_mem, n_cols * width), 'mem', 0, 0, tiled=True)  9.47 us
  transfers between devices with their start and end apart: 7, of which 4 were waited for; matrix products, arithmetic and copies ran while one was open for 4% of the time, Pallas kernels for 0%

profile of v7, /device:TPU:1, one launch (start us, length us, event | category | flops | bytes accessed | tf_op | source)
XLA Modules:
  0.0 436.0 jit_solution(7803860723980485552)
XLA Ops:
  1.1 4.9 %collective-permute-start = (bf16[1,100,128]{2,1,0:T(8,128)(2,1)S(1)}, bf16[1,100,128]{2,1,0:T(8,128)(2,1)S(1)}, u32[]{:S(2)}, u32[]{:S(2)}) collective-permute-start(bf16[1,100,128]{2,1,0:T(8,128)(2,1)S(1)} %get-tuple-element.119), channel_id=1, source_target_pairs={{0,4},{4,8},{8,12},{12,16},{16,20},{20,24},{24,28},{28,32},{32,36}... | collective-permute-start | bytes 76808 | tf_op jit(solution)/shard_map/ppermute | solution.py:16
  6.1 5.1 %collective-permute-start.1 = (bf16[1,100,128]{2,1,0:T(8,128)(2,1)S(1)}, bf16[1,100,128]{2,1,0:T(8,128)(2,1)S(1)}, u32[]{:S(2)}, u32[]{:S(2)}) collective-permute-start(bf16[1,100,128]{2,1,0:T(8,128)(2,1)S(1)} %get-tuple-element.120), channel_id=1, source_target_pairs={{4,0},{8,4},{12,8},{16,12},{20,16},{24,20},{28,24},{32,28},{36,32}... | collective-permute-start | bytes 76808 | tf_op jit(solution)/shard_map/ppermute | solution.py:19
  15.2 3.3 all-to-all-start
  19.2 3.7 all-to-all-done
  23.5 19.4 %all-to-all-start.2 = ((f32[128,1,1]{2,1,0:T(1,128)}), f32[128,1,1]{2,1,0:T(1,128)S(1)}, u32[]{:S(2)}, u32[]{:S(2)}) async-start(f32[128,1,1]{2,1,0:T(1,128)} %broadcast_in_dim.90), calls=%async_computation.2 | async-start | bytes 131072 | tf_op jit(solution)/shard_map/all_to_all | solution.py:26
  45.7 1.5 pad_maximum_fusion
  47.2 10.7 %all-to-all-done.2 = f32[128,1,1]{2,1,0:T(1,128)S(1)} async-done(((f32[128,1,1]{2,1,0:T(1,128)}), f32[128,1,1]{2,1,0:T(1,128)S(1)}, u32[]{:S(2)}, u32[]{:S(2)}) %all-to-all-start.2) | async-done | bytes 544 | tf_op jit(solution)/shard_map/all_to_all | solution.py:26
  57.9 3.6 all-to-all-start.1
  62.6 1.2 gather_fusion
  64.4 22.9 %all-to-all-done.1 = bf16[4,2112,128]{2,1,0:T(8,128)(2,1)S(1)} async-done(((bf16[4,2112,128]{2,1,0:T(8,128)(2,1)}), bf16[4,2112,128]{2,1,0:T(8,128)(2,1)S(1)}, u32[]{:S(2)}, u32[]{:S(2)}) %all-to-all-start.1) | async-done | bytes 2162720 | tf_op jit(solution)/shard_map/all_to_all | solution.py:225
  91.1 2.4 gather_fusion.1
  93.6 9.5 %all_to_all.47 = f32[4,1,33024]{2,1,0:T(1,128)S(1)} all-to-all(f32[4,1,33024]{2,1,0:T(1,128)S(1)} %bitcast.96), channel_id=1, replica_groups=mesh['cols'=128,'mem'=4] {'mem'}, dimensions={0} | all-to-all | bytes 1056768 | tf_op jit(solution)/shard_map/all_to_all | solution.py:81
  104.0 29.4 %all_to_all.48 = f32[128,1,258]{2,1,0:T(1,128)S(1)} all-to-all(f32[128,1,258]{2,1,0:T(1,128)S(1)} %all_to_all.39), channel_id=1, replica_groups=mesh['cols'=128,'mem'=4] {'cols'}, dimensions={0} | all-to-all | bytes 264192 | tf_op jit(solution)/shard_map/all_to_all | solution.py:82
  134.3 7.2 %all-to-all-start.5 = ((f32[128,1,258]{2,1,0:T(1,128)}), f32[128,1,258]{2,1,0:T(1,128)S(1)}, u32[]{:S(2)}, u32[]{:S(2)}) async-start(f32[128,1,258]{2,1,0:T(1,128)} %broadcast_in_dim.91), calls=%async_computation.5 | async-start | bytes 393216 | tf_op jit(solution)/shard_map/all_to_all | solution.py:26
  141.6 19.9 %all-to-all-done.5 = f32[128,1,258]{2,1,0:T(1,128)S(1)} async-done(((f32[128,1,258]{2,1,0:T(1,128)}), f32[128,1,258]{2,1,0:T(1,128)S(1)}, u32[]{:S(2)}, u32[]{:S(2)}) %all-to-all-start.5) | async-done | bytes 132128 | tf_op jit(solution)/shard_map/all_to_all | solution.py:26
  163.3 4.3 all-to-all-start.6
  170.5 1.3 slice.325
  171.8 2.3 reshape.283
  174.1 1.3 copy.270
  176.7 1.2 slice.355
  178.0 2.4 reduce.25
  182.0 57.1 %shard_map.100 = (f32[128,128]{1,0:T(8,128)}, f32[128,128]{1,0:T(8,128)}) custom-call(f32[128,128]{1,0:T(8,128)} %bitcast_add_fusion.4.a_ref), custom_call_target="tpu_custom_call" | custom-call | tf_op jit(solution)/shard_map/pallas_call | solution.py:138
  240.2 1.3 fusion.39
  244.5 57.2 %shard_map.101 = (f32[128,128]{1,0:T(8,128)}, f32[128,128]{1,0:T(8,128)}) custom-call(f32[128,128]{1,0:T(8,128)} %bitcast_add_fusion.3.a_ref), custom_call_target="tpu_custom_call" | custom-call | tf_op jit(solution)/shard_map/pallas_call | solution.py:138
  301.7 1.2 fusion.47
  303.9 1.4 convolution_subtract_fusion.4
  306.1 57.1 %shard_map.102 = (f32[128,128]{1,0:T(8,128)}, f32[128,128]{1,0:T(8,128)}) custom-call(f32[128,128]{1,0:T(8,128)} %bitcast_add_fusion.2.a_ref), custom_call_target="tpu_custom_call" | custom-call | tf_op jit(solution)/shard_map/pallas_call | solution.py:138
  365.4 1.6 convolution_subtract_fusion.1
  367.6 1.4 broadcast_select_fusion.1
  369.8 57.3 %shard_map.103 = (f32[128,128]{1,0:T(8,128)}, f32[128,128]{1,0:T(8,128)}) custom-call(f32[128,128]{1,0:T(8,128)} %bitcast_add_fusion.1.a_ref), custom_call_target="tpu_custom_call" | custom-call | tf_op jit(solution)/shard_map/pallas_call | solution.py:138
  427.5 2.0 convolution_subtract_fusion
  429.9 2.6 convolution_subtract_fusion.2
  (127 shorter events, 36.7 us)
Async XLA Ops:
  0.0 12.7 %copy-start = (bf16[100,256]{1,0:T(8,128)(2,1)S(1)}, bf16[100,256]{1,0:T(8,128)(2,1)}, u32[]{:S(2)}) copy-start(bf16[100,256]{1,0:T(8,128)(2,1)} %param.27) | copy-start | bytes 153604
  1.1 11.6 %collective-permute-start = (bf16[1,100,128]{2,1,0:T(8,128)(2,1)S(1)}, bf16[1,100,128]{2,1,0:T(8,128)(2,1)S(1)}, u32[]{:S(2)}, u32[]{:S(2)}) collective-permute-start(bf16[1,100,128]{2,1,0:T(8,128)(2,1)S(1)} %get-tuple-element.119), channel_id=1, source_target_pairs={{0,4},{4,8},{8,12},{12,16},{16,20},{20,24},{24,28},{28,32},{32,36}... | collective-permute-start | bytes 76808 | tf_op jit(solution)/shard_map/ppermute | solution.py:16
  6.1 6.6 %collective-permute-start.1 = (bf16[1,100,128]{2,1,0:T(8,128)(2,1)S(1)}, bf16[1,100,128]{2,1,0:T(8,128)(2,1)S(1)}, u32[]{:S(2)}, u32[]{:S(2)}) collective-permute-start(bf16[1,100,128]{2,1,0:T(8,128)(2,1)S(1)} %get-tuple-element.120), channel_id=1, source_target_pairs={{4,0},{8,4},{12,8},{16,12},{20,16},{24,20},{28,24},{32,28},{36,32}... | collective-permute-start | bytes 76808 | tf_op jit(solution)/shard_map/ppermute | solution.py:19
  12.7 1.0 copy-start.4
  12.7 1.0 copy-start.14
  13.7 4.7 %copy-start.13 = (s32[128,4]{0,1:T(4,128)S(1)}, s32[128,4]{0,1:T(4,128)}, u32[]{:S(2)}) copy-start(s32[128,4]{0,1:T(4,128)} %param.31) | copy-start | bytes 6148
  13.8 29.5 %copy-start.9 = (f32[100,16]{0,1:T(8,128)S(1)}, f32[100,16]{0,1:T(8,128)}, u32[]{:S(2)}) copy-start(f32[100,16]{0,1:T(8,128)} %param.30) | copy-start | bytes 19204
  14.6 29.5 %copy-start.11 = (f32[128,16]{0,1:T(8,128)S(1)}, f32[128,16]{0,1:T(8,128)}, u32[]{:S(2)}) copy-start(f32[128,16]{0,1:T(8,128)} %param.34) | copy-start | bytes 24580
  15.2 7.6 %all-to-all-start = ((f32[4,16,100]{2,1,0:T(8,128)}), f32[4,16,100]{2,1,0:T(8,128)S(1)}, u32[]{:S(2)}, u32[]{:S(2)}) async-start(f32[4,16,100]{2,1,0:T(8,128)} %broadcast_in_dim.85), calls=%async_computation | async-start | bytes 65536 | tf_op jit(solution)/shard_map/all_to_all | solution.py:26
  23.5 34.4 %all-to-all-start.2 = ((f32[128,1,1]{2,1,0:T(1,128)}), f32[128,1,1]{2,1,0:T(1,128)S(1)}, u32[]{:S(2)}, u32[]{:S(2)}) async-start(f32[128,1,1]{2,1,0:T(1,128)} %broadcast_in_dim.90), calls=%async_computation.2 | async-start | bytes 131072 | tf_op jit(solution)/shard_map/all_to_all | solution.py:26
  47.2 14.3 %copy-start.15 = (s32[128,1]{0,1:T(1,128)S(1)}, s32[128,1]{0,1:T(1,128)}, u32[]{:S(2)}) copy-start(s32[128,1]{0,1:T(1,128)} %param.32) | copy-start | bytes 1540
  47.2 17.1 %copy-start.12 = (f32[128,16]{0,1:T(8,128)S(1)}, f32[128,16]{0,1:T(8,128)}, u32[]{:S(2)}) copy-start(f32[128,16]{0,1:T(8,128)} %param.33) | copy-start | bytes 24580
  57.9 29.3 %all-to-all-start.1 = ((bf16[4,2112,128]{2,1,0:T(8,128)(2,1)}), bf16[4,2112,128]{2,1,0:T(8,128)(2,1)S(1)}, u32[]{:S(2)}, u32[]{:S(2)}) async-start(bf16[4,2112,128]{2,1,0:T(8,128)(2,1)} %pad_maximum_fusion), calls=%async_computation.1 | async-start | bytes 4325376 | tf_op jit(solution)/shard_map/all_to_all | solution.py:225
  89.0 1.0 copy-start.3
  134.3 27.1 %all-to-all-start.5 = ((f32[128,1,258]{2,1,0:T(1,128)}), f32[128,1,258]{2,1,0:T(1,128)S(1)}, u32[]{:S(2)}, u32[]{:S(2)}) async-start(f32[128,1,258]{2,1,0:T(1,128)} %broadcast_in_dim.91), calls=%async_computation.5 | async-start | bytes 393216 | tf_op jit(solution)/shard_map/all_to_all | solution.py:26
  163.3 12.8 %all-to-all-start.6 = ((f32[4,1,33024]{2,1,0:T(1,128)}), f32[4,1,33024]{2,1,0:T(1,128)}, u32[]{:S(2)}, u32[]{:S(2)}) async-start(f32[4,1,33024]{2,1,0:T(1,128)} %broadcast_in_dim.93), calls=%async_computation.6 | async-start | bytes 1056768 | tf_op jit(solution)/shard_map/all_to_all | solution.py:26
  181.1 61.0 %copy-start.2 = (f32[512,512]{0,1:T(8,128)}, f32[512,512]{0,1:T(8,128)S(1)}, u32[]{:S(2)}) copy-start(f32[512,512]{0,1:T(8,128)S(1)} %fusion.12) | copy-start | bytes 3145732
  239.2 3.5 copy-start.7
  303.9 61.3 %copy-start.1 = (f32[512,512]{1,0:T(8,128)}, f32[512,512]{1,0:T(8,128)S(1)}, u32[]{:S(2)}) copy-start(f32[512,512]{1,0:T(8,128)S(1)} %maximum_dynamic-update-slice_fusion) | copy-start | bytes 3145732
  305.4 121.7 %copy-start.5 = (f32[128,128]{1,0:T(8,128)S(1)}, f32[128,128]{1,0:T(8,128)}, u32[]{:S(2)}) copy-start(f32[128,128]{1,0:T(8,128)} %get-tuple-element.110) | copy-start | bytes 196612
  367.0 62.6 %copy-start.6 = (f32[128,128]{1,0:T(8,128)S(1)}, f32[128,128]{1,0:T(8,128)}, u32[]{:S(2)}) copy-start(f32[128,128]{1,0:T(8,128)} %get-tuple-element.112) | copy-start | bytes 196612
  427.1 5.4 %copy-start.8 = (f32[128,128]{1,0:T(8,128)S(1)}, f32[128,128]{1,0:T(8,128)}, u32[]{:S(2)}) copy-start(f32[128,128]{1,0:T(8,128)} %get-tuple-element.114) | copy-start | bytes 196612
  427.1 5.8 %copy-start.10 = (f32[512]{0:T(512)S(1)}, f32[512]{0:T(512)}, u32[]{:S(2)}) copy-start(f32[512]{0:T(512)} %slice.355) | copy-start | bytes 6148

commit v8 on v6

--- a/solution.py
+++ b/solution.py
@@ -113,11 +113,11 @@
         whole = m_ref[...]
         column = jnp.sum(jnp.where(lane == j, whole[:, :n], 0.0), axis=1, keepdims=True)
         pivot = jnp.sum(jnp.where(lane == j, row[:, :n], 0.0), axis=1, keepdims=True)
-        factor = jnp.where(sub > j, column / pivot, 0.0)
+        factor = jnp.where(sub > j, column * (1.0 / pivot), 0.0)
         m_ref[...] = whole - factor * row
         return carry
 
-    lax.fori_loop(0, n, step, 0)
+    lax.fori_loop(0, n, step, 0, unroll=2)
     whole = m_ref[...]
     diag = jnp.sum(jnp.where(rows == cols, whole[:, :n], 0.0), axis=1, keepdims=True)
     scale = 1.0 / jnp.sqrt(diag)

time: 271 us -> 270 us (level)
  no operation moved by 1% of the time
where the time goes in v8:
time: 270 us; the launch traced here: 268 us
  Pallas kernels  60.4 us (22%)
  waiting for transfers between devices  57.1 us (21%)
  starting transfers between devices  47.9 us (18%)
  blocking collectives  38.9 us (14%)
  local copies, waits for them, and re-layouts  23.6 us (9%)
  matrix products  23.1 us (9%)
  other arithmetic  15.3 us (6%)
    pallas_call x4, Pallas kernels, factor_block(): pl.pallas_call(_eliminate, out_shape=(square, square), in_specs=[pl.Block...  60.4 us
    all_to_all x4, waiting for transfers between devices, sent_to_all(): lax.all_to_all(jnp.broadcast_to(shard[None], (peers, *shard.shape)), axis...  34.3 us
    all_to_all x4, starting transfers between devices, sent_to_all(): lax.all_to_all(jnp.broadcast_to(shard[None], (peers, *shard.shape)), axis...  34.2 us
    all_to_all x1, blocking collectives, summed_everywhere(): lax.all_to_all(jnp.sum(part, axis=0).reshape(n_cols, width), 'cols', 0, 0...  29.4 us
    all_to_all x1, waiting for transfers between devices, body(): incoming = lax.all_to_all(outgoing, 'mem', 0, 0, tiled=True)  22.9 us
    all_to_all x1, blocking collectives, summed_everywhere(): lax.all_to_all(flat.reshape(n_mem, n_cols * width), 'mem', 0, 0, tiled=True)  9.47 us
    dot_general x3, matrix products, factor_inverse(): jnp.dot(chol[begin:finish, :begin], chol_inverse[:begin], precision=top)  6.16 us
  transfers between devices with their start and end apart: 7, of which 4 were waited for; matrix products, arithmetic and copies ran while one was open for 6% of the time, Pallas kernels for 0%

profile of v8, /device:TPU:1, one launch (start us, length us, event | category | flops | bytes accessed | tf_op | source)
XLA Modules:
  0.0 267.6 jit_solution(16315987336291663681)
XLA Ops:
  1.1 4.9 %collective-permute-start = (bf16[1,100,128]{2,1,0:T(8,128)(2,1)S(1)}, bf16[1,100,128]{2,1,0:T(8,128)(2,1)S(1)}, u32[]{:S(2)}, u32[]{:S(2)}) collective-permute-start(bf16[1,100,128]{2,1,0:T(8,128)(2,1)S(1)} %get-tuple-element.119), channel_id=1, source_target_pairs={{0,4},{4,8},{8,12},{12,16},{16,20},{20,24},{24,28},{28,32},{32,36}... | collective-permute-start | bytes 76808 | tf_op jit(solution)/shard_map/ppermute | solution.py:16
  6.1 5.1 %collective-permute-start.1 = (bf16[1,100,128]{2,1,0:T(8,128)(2,1)S(1)}, bf16[1,100,128]{2,1,0:T(8,128)(2,1)S(1)}, u32[]{:S(2)}, u32[]{:S(2)}) collective-permute-start(bf16[1,100,128]{2,1,0:T(8,128)(2,1)S(1)} %get-tuple-element.120), channel_id=1, source_target_pairs={{4,0},{8,4},{12,8},{16,12},{20,16},{24,20},{28,24},{32,28},{36,32}... | collective-permute-start | bytes 76808 | tf_op jit(solution)/shard_map/ppermute | solution.py:19
  15.2 3.3 %all-to-all-start = ((f32[4,16,100]{2,1,0:T(8,128)}), f32[4,16,100]{2,1,0:T(8,128)S(1)}, u32[]{:S(2)}, u32[]{:S(2)}) async-start(f32[4,16,100]{2,1,0:T(8,128)} %broadcast_in_dim.85), calls=%async_computation | async-start | bytes 65536 | tf_op jit(solution)/shard_map/all_to_all | solution.py:26
  19.2 3.7 %all-to-all-done = f32[4,16,100]{2,1,0:T(8,128)S(1)} async-done(((f32[4,16,100]{2,1,0:T(8,128)}), f32[4,16,100]{2,1,0:T(8,128)S(1)}, u32[]{:S(2)}, u32[]{:S(2)}) %all-to-all-start) | async-done | bytes 25632 | tf_op jit(solution)/shard_map/all_to_all | solution.py:26
  23.5 19.4 %all-to-all-start.2 = ((f32[128,1,1]{2,1,0:T(1,128)}), f32[128,1,1]{2,1,0:T(1,128)S(1)}, u32[]{:S(2)}, u32[]{:S(2)}) async-start(f32[128,1,1]{2,1,0:T(1,128)} %broadcast_in_dim.90), calls=%async_computation.2 | async-start | bytes 131072 | tf_op jit(solution)/shard_map/all_to_all | solution.py:26
  45.7 1.5 pad_maximum_fusion
  47.2 10.7 %all-to-all-done.2 = f32[128,1,1]{2,1,0:T(1,128)S(1)} async-done(((f32[128,1,1]{2,1,0:T(1,128)}), f32[128,1,1]{2,1,0:T(1,128)S(1)}, u32[]{:S(2)}, u32[]{:S(2)}) %all-to-all-start.2) | async-done | bytes 544 | tf_op jit(solution)/shard_map/all_to_all | solution.py:26
  57.9 3.6 %all-to-all-start.1 = ((bf16[4,2112,128]{2,1,0:T(8,128)(2,1)}), bf16[4,2112,128]{2,1,0:T(8,128)(2,1)S(1)}, u32[]{:S(2)}, u32[]{:S(2)}) async-start(bf16[4,2112,128]{2,1,0:T(8,128)(2,1)} %pad_maximum_fusion), calls=%async_computation.1 | async-start | bytes 4325376 | tf_op jit(solution)/shard_map/all_to_all | solution.py:219
  62.6 1.2 gather_fusion
  64.4 22.9 %all-to-all-done.1 = bf16[4,2112,128]{2,1,0:T(8,128)(2,1)S(1)} async-done(((bf16[4,2112,128]{2,1,0:T(8,128)(2,1)}), bf16[4,2112,128]{2,1,0:T(8,128)(2,1)S(1)}, u32[]{:S(2)}, u32[]{:S(2)}) %all-to-all-start.1) | async-done | bytes 2162720 | tf_op jit(solution)/shard_map/all_to_all | solution.py:219
  91.1 2.4 gather_fusion.1
  93.6 9.5 %all_to_all.47 = f32[4,1,33024]{2,1,0:T(1,128)S(1)} all-to-all(f32[4,1,33024]{2,1,0:T(1,128)S(1)} %bitcast.96), channel_id=1, replica_groups=mesh['cols'=128,'mem'=4] {'mem'}, dimensions={0} | all-to-all | bytes 1056768 | tf_op jit(solution)/shard_map/all_to_all | solution.py:81
  104.0 29.4 %all_to_all.48 = f32[128,1,258]{2,1,0:T(1,128)S(1)} all-to-all(f32[128,1,258]{2,1,0:T(1,128)S(1)} %all_to_all.39), channel_id=1, replica_groups=mesh['cols'=128,'mem'=4] {'cols'}, dimensions={0} | all-to-all | bytes 264192 | tf_op jit(solution)/shard_map/all_to_all | solution.py:82
  134.3 7.2 %all-to-all-start.5 = ((f32[128,1,258]{2,1,0:T(1,128)}), f32[128,1,258]{2,1,0:T(1,128)S(1)}, u32[]{:S(2)}, u32[]{:S(2)}) async-start(f32[128,1,258]{2,1,0:T(1,128)} %broadcast_in_dim.91), calls=%async_computation.5 | async-start | bytes 393216 | tf_op jit(solution)/shard_map/all_to_all | solution.py:26
  141.6 19.9 %all-to-all-done.5 = f32[128,1,258]{2,1,0:T(1,128)S(1)} async-done(((f32[128,1,258]{2,1,0:T(1,128)}), f32[128,1,258]{2,1,0:T(1,128)S(1)}, u32[]{:S(2)}, u32[]{:S(2)}) %all-to-all-start.5) | async-done | bytes 132128 | tf_op jit(solution)/shard_map/all_to_all | solution.py:26
  163.3 4.3 %all-to-all-start.6 = ((f32[4,1,33024]{2,1,0:T(1,128)}), f32[4,1,33024]{2,1,0:T(1,128)}, u32[]{:S(2)}, u32[]{:S(2)}) async-start(f32[4,1,33024]{2,1,0:T(1,128)} %broadcast_in_dim.93), calls=%async_computation.6 | async-start | bytes 1056768 | tf_op jit(solution)/shard_map/all_to_all | solution.py:26
  170.5 1.3 slice.325
  171.8 2.3 reshape.283
  174.1 1.3 copy.270
  176.7 1.2 slice.355
  178.0 2.4 reduce.25
  182.0 15.0 %shard_map.100 = (f32[128,128]{1,0:T(8,128)}, f32[128,128]{1,0:T(8,128)}) custom-call(f32[128,128]{1,0:T(8,128)} %bitcast_add_fusion.4.a_ref), custom_call_target="tpu_custom_call" | custom-call | tf_op jit(solution)/shard_map/pallas_call | solution.py:132
  198.0 1.3 fusion.39
  202.4 15.0 %shard_map.101 = (f32[128,128]{1,0:T(8,128)}, f32[128,128]{1,0:T(8,128)}) custom-call(f32[128,128]{1,0:T(8,128)} %bitcast_add_fusion.3.a_ref), custom_call_target="tpu_custom_call" | custom-call | tf_op jit(solution)/shard_map/pallas_call | solution.py:132
  217.4 1.2 fusion.47
  219.6 1.4 convolution_subtract_fusion.4
  221.8 15.0 %shard_map.102 = (f32[128,128]{1,0:T(8,128)}, f32[128,128]{1,0:T(8,128)}) custom-call(f32[128,128]{1,0:T(8,128)} %bitcast_add_fusion.2.a_ref), custom_call_target="tpu_custom_call" | custom-call | tf_op jit(solution)/shard_map/pallas_call | solution.py:132
  239.0 1.6 convolution_subtract_fusion.1
  241.3 1.4 broadcast_select_fusion.1
  243.4 15.3 %shard_map.103 = (f32[128,128]{1,0:T(8,128)}, f32[128,128]{1,0:T(8,128)}) custom-call(f32[128,128]{1,0:T(8,128)} %bitcast_add_fusion.1.a_ref), custom_call_target="tpu_custom_call" | custom-call | tf_op jit(solution)/shard_map/pallas_call | solution.py:132
  259.1 2.0 convolution_subtract_fusion
  261.5 2.6 convolution_subtract_fusion.2
  (127 shorter events, 36.7 us)
Async XLA Ops:
  0.0 12.7 %copy-start = (bf16[100,256]{1,0:T(8,128)(2,1)S(1)}, bf16[100,256]{1,0:T(8,128)(2,1)}, u32[]{:S(2)}) copy-start(bf16[100,256]{1,0:T(8,128)(2,1)} %param.27) | copy-start | bytes 153604
  1.1 11.6 %collective-permute-start = (bf16[1,100,128]{2,1,0:T(8,128)(2,1)S(1)}, bf16[1,100,128]{2,1,0:T(8,128)(2,1)S(1)}, u32[]{:S(2)}, u32[]{:S(2)}) collective-permute-start(bf16[1,100,128]{2,1,0:T(8,128)(2,1)S(1)} %get-tuple-element.119), channel_id=1, source_target_pairs={{0,4},{4,8},{8,12},{12,16},{16,20},{20,24},{24,28},{28,32},{32,36}... | collective-permute-start | bytes 76808 | tf_op jit(solution)/shard_map/ppermute | solution.py:16
  6.1 6.6 %collective-permute-start.1 = (bf16[1,100,128]{2,1,0:T(8,128)(2,1)S(1)}, bf16[1,100,128]{2,1,0:T(8,128)(2,1)S(1)}, u32[]{:S(2)}, u32[]{:S(2)}) collective-permute-start(bf16[1,100,128]{2,1,0:T(8,128)(2,1)S(1)} %get-tuple-element.120), channel_id=1, source_target_pairs={{4,0},{8,4},{12,8},{16,12},{20,16},{24,20},{28,24},{32,28},{36,32}... | collective-permute-start | bytes 76808 | tf_op jit(solution)/shard_map/ppermute | solution.py:19
  12.7 1.0 copy-start.4
  12.7 1.0 copy-start.14
  13.7 4.7 %copy-start.13 = (s32[128,4]{0,1:T(4,128)S(1)}, s32[128,4]{0,1:T(4,128)}, u32[]{:S(2)}) copy-start(s32[128,4]{0,1:T(4,128)} %param.31) | copy-start | bytes 6148
  13.8 29.5 %copy-start.9 = (f32[100,16]{0,1:T(8,128)S(1)}, f32[100,16]{0,1:T(8,128)}, u32[]{:S(2)}) copy-start(f32[100,16]{0,1:T(8,128)} %param.30) | copy-start | bytes 19204
  14.6 29.5 %copy-start.11 = (f32[128,16]{0,1:T(8,128)S(1)}, f32[128,16]{0,1:T(8,128)}, u32[]{:S(2)}) copy-start(f32[128,16]{0,1:T(8,128)} %param.34) | copy-start | bytes 24580
  15.2 7.6 %all-to-all-start = ((f32[4,16,100]{2,1,0:T(8,128)}), f32[4,16,100]{2,1,0:T(8,128)S(1)}, u32[]{:S(2)}, u32[]{:S(2)}) async-start(f32[4,16,100]{2,1,0:T(8,128)} %broadcast_in_dim.85), calls=%async_computation | async-start | bytes 65536 | tf_op jit(solution)/shard_map/all_to_all | solution.py:26
  23.5 34.4 %all-to-all-start.2 = ((f32[128,1,1]{2,1,0:T(1,128)}), f32[128,1,1]{2,1,0:T(1,128)S(1)}, u32[]{:S(2)}, u32[]{:S(2)}) async-start(f32[128,1,1]{2,1,0:T(1,128)} %broadcast_in_dim.90), calls=%async_computation.2 | async-start | bytes 131072 | tf_op jit(solution)/shard_map/all_to_all | solution.py:26
  47.2 14.3 %copy-start.15 = (s32[128,1]{0,1:T(1,128)S(1)}, s32[128,1]{0,1:T(1,128)}, u32[]{:S(2)}) copy-start(s32[128,1]{0,1:T(1,128)} %param.32) | copy-start | bytes 1540
  47.2 17.1 %copy-start.12 = (f32[128,16]{0,1:T(8,128)S(1)}, f32[128,16]{0,1:T(8,128)}, u32[]{:S(2)}) copy-start(f32[128,16]{0,1:T(8,128)} %param.33) | copy-start | bytes 24580
  57.9 29.3 %all-to-all-start.1 = ((bf16[4,2112,128]{2,1,0:T(8,128)(2,1)}), bf16[4,2112,128]{2,1,0:T(8,128)(2,1)S(1)}, u32[]{:S(2)}, u32[]{:S(2)}) async-start(bf16[4,2112,128]{2,1,0:T(8,128)(2,1)} %pad_maximum_fusion), calls=%async_computation.1 | async-start | bytes 4325376 | tf_op jit(solution)/shard_map/all_to_all | solution.py:219
  89.0 1.0 copy-start.3
  134.3 27.1 %all-to-all-start.5 = ((f32[128,1,258]{2,1,0:T(1,128)}), f32[128,1,258]{2,1,0:T(1,128)S(1)}, u32[]{:S(2)}, u32[]{:S(2)}) async-start(f32[128,1,258]{2,1,0:T(1,128)} %broadcast_in_dim.91), calls=%async_computation.5 | async-start | bytes 393216 | tf_op jit(solution)/shard_map/all_to_all | solution.py:26
  163.3 12.8 %all-to-all-start.6 = ((f32[4,1,33024]{2,1,0:T(1,128)}), f32[4,1,33024]{2,1,0:T(1,128)}, u32[]{:S(2)}, u32[]{:S(2)}) async-start(f32[4,1,33024]{2,1,0:T(1,128)} %broadcast_in_dim.93), calls=%async_computation.6 | async-start | bytes 1056768 | tf_op jit(solution)/shard_map/all_to_all | solution.py:26
  181.1 18.9 %copy-start.2 = (f32[512,512]{0,1:T(8,128)}, f32[512,512]{0,1:T(8,128)S(1)}, u32[]{:S(2)}) copy-start(f32[512,512]{0,1:T(8,128)S(1)} %fusion.12) | copy-start | bytes 3145732
  197.1 3.5 %copy-start.7 = (f32[128,128]{1,0:T(8,128)S(1)}, f32[128,128]{1,0:T(8,128)}, u32[]{:S(2)}) copy-start(f32[128,128]{1,0:T(8,128)} %get-tuple-element.108) | copy-start | bytes 196612
  219.6 19.1 %copy-start.1 = (f32[512,512]{1,0:T(8,128)}, f32[512,512]{1,0:T(8,128)S(1)}, u32[]{:S(2)}) copy-start(f32[512,512]{1,0:T(8,128)S(1)} %maximum_dynamic-update-slice_fusion) | copy-start | bytes 3145732
  221.2 37.6 %copy-start.5 = (f32[128,128]{1,0:T(8,128)S(1)}, f32[128,128]{1,0:T(8,128)}, u32[]{:S(2)}) copy-start(f32[128,128]{1,0:T(8,128)} %get-tuple-element.110) | copy-start | bytes 196612
  240.6 20.6 %copy-start.6 = (f32[128,128]{1,0:T(8,128)S(1)}, f32[128,128]{1,0:T(8,128)}, u32[]{:S(2)}) copy-start(f32[128,128]{1,0:T(8,128)} %get-tuple-element.112) | copy-start | bytes 196612
  258.7 5.4 %copy-start.8 = (f32[128,128]{1,0:T(8,128)S(1)}, f32[128,128]{1,0:T(8,128)}, u32[]{:S(2)}) copy-start(f32[128,128]{1,0:T(8,128)} %get-tuple-element.114) | copy-start | bytes 196612
  258.7 5.7 %copy-start.10 = (f32[512]{0:T(512)S(1)}, f32[512]{0:T(512)}, u32[]{:S(2)}) copy-start(f32[512]{0:T(512)} %slice.355) | copy-start | bytes 6148

commit v9 on v8

--- a/solution.py
+++ b/solution.py
@@ -105,7 +105,8 @@
     lane = lax.broadcasted_iota(jnp.int32, (1, n), 1)
     rows = lax.broadcasted_iota(jnp.int32, (n, n), 0)
     cols = lax.broadcasted_iota(jnp.int32, (n, n), 1)
-    m_ref[:, :n] = a_ref[...]
+    given = a_ref[...]
+    m_ref[:, :n] = jnp.where(rows >= cols, given, given.T)
     m_ref[:, n:] = (rows == cols).astype(jnp.float32)
 
     def step(j, carry):
@@ -121,22 +122,21 @@
     whole = m_ref[...]
     diag = jnp.sum(jnp.where(rows == cols, whole[:, :n], 0.0), axis=1, keepdims=True)
     scale = 1.0 / jnp.sqrt(diag)
-    low_ref[...] = jnp.where(rows <= cols, whole[:, :n] * scale, 0.0)
+    low_ref[...] = jnp.where(rows <= cols, whole[:, :n] * scale, 0.0).T
     inv_ref[...] = whole[:, n:] * scale
 
 
 def factor_block(block):
     width = block.shape[0]
-    symmetric = jnp.tril(block) + jnp.tril(block, -1).T
     square = jax.ShapeDtypeStruct((width, width), jnp.float32)
-    upper, inverse = pl.pallas_call(
+    lower, inverse = pl.pallas_call(
         _eliminate,
         out_shape=(square, square),
         in_specs=[pl.BlockSpec(memory_space=pltpu.VMEM)],
         out_specs=(pl.BlockSpec(memory_space=pltpu.VMEM), pl.BlockSpec(memory_space=pltpu.VMEM)),
         scratch_shapes=[pltpu.VMEM((width, 2 * width), jnp.float32)],
-    )(symmetric)
-    return upper.T, inverse
+    )(block)
+    return lower, inverse
 
 
 def factor_inverse(gram):

time: 270 us -> 265 us (0.981)
  blocking collectives: 38.9 us -> 65.4 us
  waiting for transfers between devices: 57.1 us -> 37.2 us
  starting transfers between devices: 47.9 us -> 40.5 us
    all_to_all x0 -> x1, blocking collectives: none -> 26.5 us  [sent_to_all(): lax.all_to_all(jnp.broadcast_to(shard[None], (peers, *shard.shape)), axis...]
    all_to_all x4 -> x3, waiting for transfers between devices: 34.3 us -> 14.3 us  [sent_to_all(): lax.all_to_all(jnp.broadcast_to(shard[None], (peers, *shard.shape)), axis...]
    all_to_all x4 -> x3, starting transfers between devices: 34.2 us -> 26.8 us  [sent_to_all(): lax.all_to_all(jnp.broadcast_to(shard[None], (peers, *shard.shape)), axis...]
    add x5 -> x0, other arithmetic: 2.74 us -> none  [factor_block(): symmetric = jnp.tril(block) + jnp.tril(block, -1).T]
  transfers between devices with their start and end apart: 7 -> 6, of which waited for: 4 -> 3; matrix products, arithmetic and copies ran while one was open for 6% -> 6% of each run, Pallas kernels for 0% -> 0%
where the time goes in v9:
time: 265 us; the launch traced here: 263 us
  blocking collectives  65.4 us (25%)
  Pallas kernels  60.9 us (23%)
  starting transfers between devices  40.5 us (15%)
  waiting for transfers between devices  37.2 us (14%)
  matrix products  21.8 us (8%)
  local copies, waits for them, and re-layouts  21.3 us (8%)
  other arithmetic  14.2 us (5%)
    pallas_call x4, Pallas kernels, factor_block(): pl.pallas_call(_eliminate, out_shape=(square, square), in_specs=[pl.Block...  60.9 us
    all_to_all x1, blocking collectives, summed_everywhere(): lax.all_to_all(jnp.sum(part, axis=0).reshape(n_cols, width), 'cols', 0, 0...  29.4 us
    all_to_all x3, starting transfers between devices, sent_to_all(): lax.all_to_all(jnp.broadcast_to(shard[None], (peers, *shard.shape)), axis...  26.8 us
    all_to_all x1, blocking collectives, sent_to_all(): lax.all_to_all(jnp.broadcast_to(shard[None], (peers, *shard.shape)), axis...  26.5 us
    all_to_all x1, waiting for transfers between devices, body(): incoming = lax.all_to_all(outgoing, 'mem', 0, 0, tiled=True)  22.9 us
    all_to_all x3, waiting for transfers between devices, sent_to_all(): lax.all_to_all(jnp.broadcast_to(shard[None], (peers, *shard.shape)), axis...  14.3 us
    all_to_all x1, blocking collectives, summed_everywhere(): lax.all_to_all(flat.reshape(n_mem, n_cols * width), 'mem', 0, 0, tiled=True)  9.47 us
  transfers between devices with their start and end apart: 6, of which 3 were waited for; matrix products, arithmetic and copies ran while one was open for 6% of the time, Pallas kernels for 0%

profile of v9, /device:TPU:1, one launch (start us, length us, event | category | flops | bytes accessed | tf_op | source)
XLA Modules:
  0.0 262.6 jit_solution(5359717345741941438)
XLA Ops:
  0.0 1.1 copy.120
  1.1 4.9 %collective-permute-start = (bf16[1,100,128]{2,1,0:T(8,128)(2,1)S(1)}, bf16[1,100,128]{2,1,0:T(8,128)(2,1)S(1)}, u32[]{:S(2)}, u32[]{:S(2)}) collective-permute-start(bf16[1,100,128]{2,1,0:T(8,128)(2,1)S(1)} %get-tuple-element.121), channel_id=1, source_target_pairs={{0,4},{4,8},{8,12},{12,16},{16,20},{20,24},{24,28},{28,32},{32,36}... | collective-permute-start | bytes 76808 | tf_op jit(solution)/shard_map/ppermute | solution.py:16
  6.1 5.1 %collective-permute-start.1 = (bf16[1,100,128]{2,1,0:T(8,128)(2,1)S(1)}, bf16[1,100,128]{2,1,0:T(8,128)(2,1)S(1)}, u32[]{:S(2)}, u32[]{:S(2)}) collective-permute-start(bf16[1,100,128]{2,1,0:T(8,128)(2,1)S(1)} %get-tuple-element.122), channel_id=1, source_target_pairs={{4,0},{8,4},{12,8},{16,12},{20,16},{24,20},{28,24},{32,28},{36,32}... | collective-permute-start | bytes 76808 | tf_op jit(solution)/shard_map/ppermute | solution.py:19
  15.2 3.3 %all-to-all-start = ((f32[4,16,100]{2,1,0:T(8,128)}), f32[4,16,100]{2,1,0:T(8,128)S(1)}, u32[]{:S(2)}, u32[]{:S(2)}) async-start(f32[4,16,100]{2,1,0:T(8,128)} %broadcast_in_dim.40), calls=%async_computation | async-start | bytes 65536 | tf_op jit(solution)/shard_map/all_to_all | solution.py:26
  19.2 3.7 %all-to-all-done = f32[4,16,100]{2,1,0:T(8,128)S(1)} async-done(((f32[4,16,100]{2,1,0:T(8,128)}), f32[4,16,100]{2,1,0:T(8,128)S(1)}, u32[]{:S(2)}, u32[]{:S(2)}) %all-to-all-start) | async-done | bytes 25632 | tf_op jit(solution)/shard_map/all_to_all | solution.py:26
  23.5 19.4 %all-to-all-start.2 = ((f32[128,1,1]{2,1,0:T(1,128)}), f32[128,1,1]{2,1,0:T(1,128)S(1)}, u32[]{:S(2)}, u32[]{:S(2)}) async-start(f32[128,1,1]{2,1,0:T(1,128)} %broadcast_in_dim.78), calls=%async_computation.2 | async-start | bytes 131072 | tf_op jit(solution)/shard_map/all_to_all | solution.py:26
  45.7 1.5 pad_maximum_fusion
  47.2 10.7 %all-to-all-done.2 = f32[128,1,1]{2,1,0:T(1,128)S(1)} async-done(((f32[128,1,1]{2,1,0:T(1,128)}), f32[128,1,1]{2,1,0:T(1,128)S(1)}, u32[]{:S(2)}, u32[]{:S(2)}) %all-to-all-start.2) | async-done | bytes 544 | tf_op jit(solution)/shard_map/all_to_all | solution.py:26
  57.9 3.6 %all-to-all-start.1 = ((bf16[4,2112,128]{2,1,0:T(8,128)(2,1)}), bf16[4,2112,128]{2,1,0:T(8,128)(2,1)S(1)}, u32[]{:S(2)}, u32[]{:S(2)}) async-start(bf16[4,2112,128]{2,1,0:T(8,128)(2,1)} %pad_maximum_fusion), calls=%async_computation.1 | async-start | bytes 4325376 | tf_op jit(solution)/shard_map/all_to_all | solution.py:219
  62.6 1.2 gather_fusion
  64.4 22.9 %all-to-all-done.1 = bf16[4,2112,128]{2,1,0:T(8,128)(2,1)S(1)} async-done(((bf16[4,2112,128]{2,1,0:T(8,128)(2,1)}), bf16[4,2112,128]{2,1,0:T(8,128)(2,1)S(1)}, u32[]{:S(2)}, u32[]{:S(2)}) %all-to-all-start.1) | async-done | bytes 2162720 | tf_op jit(solution)/shard_map/all_to_all | solution.py:219
  91.6 2.3 gather_fusion.1
  94.0 9.5 %all_to_all.47 = f32[4,1,33024]{2,1,0:T(1,128)S(1)} all-to-all(f32[4,1,33024]{2,1,0:T(1,128)S(1)} %bitcast.84), channel_id=1, replica_groups=mesh['cols'=128,'mem'=4] {'mem'}, dimensions={0} | all-to-all | bytes 1056768 | tf_op jit(solution)/shard_map/all_to_all | solution.py:81
  104.3 29.4 %all_to_all.48 = f32[128,1,258]{2,1,0:T(1,128)S(1)} all-to-all(f32[128,1,258]{2,1,0:T(1,128)S(1)} %all_to_all.39), channel_id=1, replica_groups=mesh['cols'=128,'mem'=4] {'cols'}, dimensions={0} | all-to-all | bytes 264192 | tf_op jit(solution)/shard_map/all_to_all | solution.py:82
  134.0 26.5 %all_to_all.49 = f32[128,1,258]{2,1,0:T(1,128)S(1)} all-to-all(f32[128,1,258]{2,1,0:T(1,128)S(1)} %broadcast_in_dim.79), channel_id=1, replica_groups=mesh['cols'=128,'mem'=4] {'cols'}, dimensions={0} | all-to-all | bytes 264192 | tf_op jit(solution)/shard_map/all_to_all | solution.py:26
  162.3 4.1 %all-to-all-start.6 = ((f32[4,1,33024]{2,1,0:T(1,128)}), f32[4,1,33024]{2,1,0:T(1,128)}, u32[]{:S(2)}, u32[]{:S(2)}) async-start(f32[4,1,33024]{2,1,0:T(1,128)} %broadcast_in_dim.81), calls=%async_computation.6 | async-start | bytes 1056768 | tf_op jit(solution)/shard_map/all_to_all | solution.py:26
  169.1 1.3 slice.325
  170.4 2.3 reshape.283
  172.8 1.3 copy.142
  176.1 2.4 reduce.25
  179.9 15.2 %shard_map.100 = (f32[128,128]{1,0:T(8,128)}, f32[128,128]{1,0:T(8,128)}) custom-call(f32[128,128]{1,0:T(8,128)} %slice.333.a_ref), custom_call_target="tpu_custom_call" | custom-call | tf_op jit(solution)/shard_map/pallas_call | solution.py:132
  195.1 1.2 fusion.37
  196.3 1.5 maximum_select_fusion
  200.0 15.2 %shard_map.101 = (f32[128,128]{1,0:T(8,128)}, f32[128,128]{1,0:T(8,128)}) custom-call(f32[128,128]{1,0:T(8,128)} %slice.339.a_ref), custom_call_target="tpu_custom_call" | custom-call | tf_op jit(solution)/shard_map/pallas_call | solution.py:132
  217.3 1.4 convolution_subtract_fusion.4
  219.3 15.2 %shard_map.102 = (f32[128,128]{1,0:T(8,128)}, f32[128,128]{1,0:T(8,128)}) custom-call(f32[128,128]{1,0:T(8,128)} %slice.346.a_ref), custom_call_target="tpu_custom_call" | custom-call | tf_op jit(solution)/shard_map/pallas_call | solution.py:132
  234.6 1.1 fusion.49
  235.8 1.4 convolution_subtract_fusion.1
  237.9 2.0 convolution_subtract_fusion.5.a_ref
  239.9 15.2 %shard_map.103 = (f32[128,128]{1,0:T(8,128)}, f32[128,128]{1,0:T(8,128)}) custom-call(f32[128,128]{1,0:T(8,128)} %convolution_subtract_fusion.5.a_ref), custom_call_target="tpu_custom_call" | custom-call | tf_op jit(solution)/shard_map/pallas_call | solution.py:132
  255.5 1.4 convolution_subtract_fusion
  257.4 1.7 convolution_subtract_fusion.2
  (111 shorter events, 32.0 us)
Async XLA Ops:
  0.0 12.7 %copy-start = (bf16[100,256]{1,0:T(8,128)(2,1)S(1)}, bf16[100,256]{1,0:T(8,128)(2,1)}, u32[]{:S(2)}) copy-start(bf16[100,256]{1,0:T(8,128)(2,1)} %param.27) | copy-start | bytes 153604
  1.1 11.6 %collective-permute-start = (bf16[1,100,128]{2,1,0:T(8,128)(2,1)S(1)}, bf16[1,100,128]{2,1,0:T(8,128)(2,1)S(1)}, u32[]{:S(2)}, u32[]{:S(2)}) collective-permute-start(bf16[1,100,128]{2,1,0:T(8,128)(2,1)S(1)} %get-tuple-element.121), channel_id=1, source_target_pairs={{0,4},{4,8},{8,12},{12,16},{16,20},{20,24},{24,28},{28,32},{32,36}... | collective-permute-start | bytes 76808 | tf_op jit(solution)/shard_map/ppermute | solution.py:16
  6.1 6.6 %collective-permute-start.1 = (bf16[1,100,128]{2,1,0:T(8,128)(2,1)S(1)}, bf16[1,100,128]{2,1,0:T(8,128)(2,1)S(1)}, u32[]{:S(2)}, u32[]{:S(2)}) collective-permute-start(bf16[1,100,128]{2,1,0:T(8,128)(2,1)S(1)} %get-tuple-element.122), channel_id=1, source_target_pairs={{4,0},{8,4},{12,8},{16,12},{20,16},{24,20},{28,24},{32,28},{36,32}... | collective-permute-start | bytes 76808 | tf_op jit(solution)/shard_map/ppermute | solution.py:19
  12.7 1.0 copy-start.4
  12.7 1.0 copy-start.14
  13.7 4.7 %copy-start.13 = (s32[128,4]{0,1:T(4,128)S(1)}, s32[128,4]{0,1:T(4,128)}, u32[]{:S(2)}) copy-start(s32[128,4]{0,1:T(4,128)} %param.31) | copy-start | bytes 6148
  13.8 29.5 %copy-start.10 = (f32[100,16]{0,1:T(8,128)S(1)}, f32[100,16]{0,1:T(8,128)}, u32[]{:S(2)}) copy-start(f32[100,16]{0,1:T(8,128)} %param.30) | copy-start | bytes 19204
  14.6 29.5 %copy-start.11 = (f32[128,16]{0,1:T(8,128)S(1)}, f32[128,16]{0,1:T(8,128)}, u32[]{:S(2)}) copy-start(f32[128,16]{0,1:T(8,128)} %param.34) | copy-start | bytes 24580
  15.2 7.6 %all-to-all-start = ((f32[4,16,100]{2,1,0:T(8,128)}), f32[4,16,100]{2,1,0:T(8,128)S(1)}, u32[]{:S(2)}, u32[]{:S(2)}) async-start(f32[4,16,100]{2,1,0:T(8,128)} %broadcast_in_dim.40), calls=%async_computation | async-start | bytes 65536 | tf_op jit(solution)/shard_map/all_to_all | solution.py:26
  23.5 34.4 %all-to-all-start.2 = ((f32[128,1,1]{2,1,0:T(1,128)}), f32[128,1,1]{2,1,0:T(1,128)S(1)}, u32[]{:S(2)}, u32[]{:S(2)}) async-start(f32[128,1,1]{2,1,0:T(1,128)} %broadcast_in_dim.78), calls=%async_computation.2 | async-start | bytes 131072 | tf_op jit(solution)/shard_map/all_to_all | solution.py:26
  47.2 14.3 %copy-start.15 = (s32[128,1]{0,1:T(1,128)S(1)}, s32[128,1]{0,1:T(1,128)}, u32[]{:S(2)}) copy-start(s32[128,1]{0,1:T(1,128)} %param.32) | copy-start | bytes 1540
  47.2 17.0 %copy-start.12 = (f32[128,16]{0,1:T(8,128)S(1)}, f32[128,16]{0,1:T(8,128)}, u32[]{:S(2)}) copy-start(f32[128,16]{0,1:T(8,128)} %param.33) | copy-start | bytes 24580
  57.9 29.3 %all-to-all-start.1 = ((bf16[4,2112,128]{2,1,0:T(8,128)(2,1)}), bf16[4,2112,128]{2,1,0:T(8,128)(2,1)S(1)}, u32[]{:S(2)}, u32[]{:S(2)}) async-start(bf16[4,2112,128]{2,1,0:T(8,128)(2,1)} %pad_maximum_fusion), calls=%async_computation.1 | async-start | bytes 4325376 | tf_op jit(solution)/shard_map/all_to_all | solution.py:219
  89.0 1.0 copy-start.3
  162.3 12.5 %all-to-all-start.6 = ((f32[4,1,33024]{2,1,0:T(1,128)}), f32[4,1,33024]{2,1,0:T(1,128)}, u32[]{:S(2)}, u32[]{:S(2)}) async-start(f32[4,1,33024]{2,1,0:T(1,128)} %broadcast_in_dim.81), calls=%async_computation.6 | async-start | bytes 1056768 | tf_op jit(solution)/shard_map/all_to_all | solution.py:26
  179.2 18.7 %copy-start.2 = (f32[512,512]{1,0:T(8,128)}, f32[512,512]{1,0:T(8,128)S(1)}, u32[]{:S(2)}) copy-start(f32[512,512]{1,0:T(8,128)S(1)} %fusion.12) | copy-start | bytes 3145732
  195.1 3.2 %copy-start.7 = (f32[128,128]{1,0:T(8,128)S(1)}, f32[128,128]{1,0:T(8,128)}, u32[]{:S(2)}) copy-start(f32[128,128]{1,0:T(8,128)} %get-tuple-element.108) | copy-start | bytes 196612
  216.4 38.8 %copy-start.5 = (f32[128,128]{1,0:T(8,128)S(1)}, f32[128,128]{1,0:T(8,128)}, u32[]{:S(2)}) copy-start(f32[128,128]{1,0:T(8,128)} %get-tuple-element.110) | copy-start | bytes 196612
  217.3 17.3 %copy-start.1 = (f32[512,512]{1,0:T(8,128)}, f32[512,512]{1,0:T(8,128)S(1)}, u32[]{:S(2)}) copy-start(f32[512,512]{1,0:T(8,128)S(1)} %maximum_dynamic-update-slice_fusion) | copy-start | bytes 3145732
  234.6 2.6 %copy-start.9 = (f32[128,128]{1,0:T(8,128)S(1)}, f32[128,128]{1,0:T(8,128)}, u32[]{:S(2)}) copy-start(f32[128,128]{1,0:T(8,128)} %get-tuple-element.113) | copy-start | bytes 196612
  235.7 21.3 %copy-start.6 = (f32[128,128]{1,0:T(8,128)S(1)}, f32[128,128]{1,0:T(8,128)}, u32[]{:S(2)}) copy-start(f32[128,128]{1,0:T(8,128)} %get-tuple-element.112) | copy-start | bytes 196612
  255.2 3.9 %copy-start.8 = (f32[128,128]{1,0:T(8,128)S(1)}, f32[128,128]{1,0:T(8,128)}, u32[]{:S(2)}) copy-start(f32[128,128]{1,0:T(8,128)} %get-tuple-element.114) | copy-start | bytes 196612

commit v10 on v9

--- a/solution.py
+++ b/solution.py
@@ -99,31 +99,33 @@
     return joined_along(sent_to_all(shard, axis), dim)
 
 
-def _eliminate(a_ref, low_ref, inv_ref, m_ref):
+def _eliminate(a_ref, low_ref, inv_ref, left_ref, right_ref):
     n = a_ref.shape[0]
     sub = lax.broadcasted_iota(jnp.int32, (n, 1), 0)
     lane = lax.broadcasted_iota(jnp.int32, (1, n), 1)
     rows = lax.broadcasted_iota(jnp.int32, (n, n), 0)
     cols = lax.broadcasted_iota(jnp.int32, (n, n), 1)
     given = a_ref[...]
-    m_ref[:, :n] = jnp.where(rows >= cols, given, given.T)
-    m_ref[:, n:] = (rows == cols).astype(jnp.float32)
+    left_ref[...] = jnp.where(rows >= cols, given, given.T)
+    right_ref[...] = (rows == cols).astype(jnp.float32)
 
     def step(j, carry):
-        row = m_ref[pl.ds(j, 1), :]
-        whole = m_ref[...]
-        column = jnp.sum(jnp.where(lane == j, whole[:, :n], 0.0), axis=1, keepdims=True)
-        pivot = jnp.sum(jnp.where(lane == j, row[:, :n], 0.0), axis=1, keepdims=True)
+        row = left_ref[pl.ds(j, 1), :]
+        other = right_ref[pl.ds(j, 1), :]
+        whole = left_ref[...]
+        column = jnp.sum(jnp.where(lane == j, whole, 0.0), axis=1, keepdims=True)
+        pivot = jnp.sum(jnp.where(lane == j, row, 0.0), axis=1, keepdims=True)
         factor = jnp.where(sub > j, column * (1.0 / pivot), 0.0)
-        m_ref[...] = whole - factor * row
+        left_ref[...] = whole - factor * row
+        right_ref[...] = right_ref[...] - factor * other
         return carry
 
     lax.fori_loop(0, n, step, 0, unroll=2)
-    whole = m_ref[...]
-    diag = jnp.sum(jnp.where(rows == cols, whole[:, :n], 0.0), axis=1, keepdims=True)
+    whole = left_ref[...]
+    diag = jnp.sum(jnp.where(rows == cols, whole, 0.0), axis=1, keepdims=True)
     scale = 1.0 / jnp.sqrt(diag)
-    low_ref[...] = jnp.where(rows <= cols, whole[:, :n] * scale, 0.0).T
-    inv_ref[...] = whole[:, n:] * scale
+    low_ref[...] = jnp.where(rows <= cols, whole * scale, 0.0).T
+    inv_ref[...] = right_ref[...] * scale
 
 
 def factor_block(block):
@@ -134,7 +136,7 @@
         out_shape=(square, square),
         in_specs=[pl.BlockSpec(memory_space=pltpu.VMEM)],
         out_specs=(pl.BlockSpec(memory_space=pltpu.VMEM), pl.BlockSpec(memory_space=pltpu.VMEM)),
-        scratch_shapes=[pltpu.VMEM((width, 2 * width), jnp.float32)],
+        scratch_shapes=[pltpu.VMEM((width, width), jnp.float32)] * 2,
     )(block)
     return lower, inverse
 

time: 265 us -> 265 us (level)
  no operation moved by 1% of the time
where the time goes in v10:
time: 265 us; the launch traced here: 262 us
  blocking collectives  65.4 us (25%)
  Pallas kernels  60.7 us (23%)
  starting transfers between devices  40.5 us (15%)
  waiting for transfers between devices  37.2 us (14%)
  matrix products  21.8 us (8%)
  local copies, waits for them, and re-layouts  21.3 us (8%)
  other arithmetic  14.2 us (5%)
    pallas_call x4, Pallas kernels, factor_block(): pl.pallas_call(_eliminate, out_shape=(square, square), in_specs=[pl.Block...  60.7 us
    all_to_all x1, blocking collectives, summed_everywhere(): lax.all_to_all(jnp.sum(part, axis=0).reshape(n_cols, width), 'cols', 0, 0...  29.4 us
    all_to_all x3, starting transfers between devices, sent_to_all(): lax.all_to_all(jnp.broadcast_to(shard[None], (peers, *shard.shape)), axis...  26.8 us
    all_to_all x1, blocking collectives, sent_to_all(): lax.all_to_all(jnp.broadcast_to(shard[None], (peers, *shard.shape)), axis...  26.5 us
    all_to_all x1, waiting for transfers between devices, body(): incoming = lax.all_to_all(outgoing, 'mem', 0, 0, tiled=True)  22.9 us
    all_to_all x3, waiting for transfers between devices, sent_to_all(): lax.all_to_all(jnp.broadcast_to(shard[None], (peers, *shard.shape)), axis...  14.3 us
    all_to_all x1, blocking collectives, summed_everywhere(): lax.all_to_all(flat.reshape(n_mem, n_cols * width), 'mem', 0, 0, tiled=True)  9.47 us
  transfers between devices with their start and end apart: 6, of which 3 were waited for; matrix products, arithmetic and copies ran while one was open for 6% of the time, Pallas kernels for 0%

profile of v10, /device:TPU:1, one launch (start us, length us, event | category | flops | bytes accessed | tf_op | source)
XLA Modules:
  0.0 262.3 jit_solution(16100336562872592095)
XLA Ops:
  0.0 1.1 copy.120
  1.1 4.9 %collective-permute-start = (bf16[1,100,128]{2,1,0:T(8,128)(2,1)S(1)}, bf16[1,100,128]{2,1,0:T(8,128)(2,1)S(1)}, u32[]{:S(2)}, u32[]{:S(2)}) collective-permute-start(bf16[1,100,128]{2,1,0:T(8,128)(2,1)S(1)} %get-tuple-element.121), channel_id=1, source_target_pairs={{0,4},{4,8},{8,12},{12,16},{16,20},{20,24},{24,28},{28,32},{32,36}... | collective-permute-start | bytes 76808 | tf_op jit(solution)/shard_map/ppermute | solution.py:16
  6.1 5.1 %collective-permute-start.1 = (bf16[1,100,128]{2,1,0:T(8,128)(2,1)S(1)}, bf16[1,100,128]{2,1,0:T(8,128)(2,1)S(1)}, u32[]{:S(2)}, u32[]{:S(2)}) collective-permute-start(bf16[1,100,128]{2,1,0:T(8,128)(2,1)S(1)} %get-tuple-element.122), channel_id=1, source_target_pairs={{4,0},{8,4},{12,8},{16,12},{20,16},{24,20},{28,24},{32,28},{36,32}... | collective-permute-start | bytes 76808 | tf_op jit(solution)/shard_map/ppermute | solution.py:19
  15.2 3.3 %all-to-all-start = ((f32[4,16,100]{2,1,0:T(8,128)}), f32[4,16,100]{2,1,0:T(8,128)S(1)}, u32[]{:S(2)}, u32[]{:S(2)}) async-start(f32[4,16,100]{2,1,0:T(8,128)} %broadcast_in_dim.40), calls=%async_computation | async-start | bytes 65536 | tf_op jit(solution)/shard_map/all_to_all | solution.py:26
  19.2 3.7 %all-to-all-done = f32[4,16,100]{2,1,0:T(8,128)S(1)} async-done(((f32[4,16,100]{2,1,0:T(8,128)}), f32[4,16,100]{2,1,0:T(8,128)S(1)}, u32[]{:S(2)}, u32[]{:S(2)}) %all-to-all-start) | async-done | bytes 25632 | tf_op jit(solution)/shard_map/all_to_all | solution.py:26
  23.5 19.4 %all-to-all-start.2 = ((f32[128,1,1]{2,1,0:T(1,128)}), f32[128,1,1]{2,1,0:T(1,128)S(1)}, u32[]{:S(2)}, u32[]{:S(2)}) async-start(f32[128,1,1]{2,1,0:T(1,128)} %broadcast_in_dim.78), calls=%async_computation.2 | async-start | bytes 131072 | tf_op jit(solution)/shard_map/all_to_all | solution.py:26
  45.7 1.5 pad_maximum_fusion
  47.2 10.7 %all-to-all-done.2 = f32[128,1,1]{2,1,0:T(1,128)S(1)} async-done(((f32[128,1,1]{2,1,0:T(1,128)}), f32[128,1,1]{2,1,0:T(1,128)S(1)}, u32[]{:S(2)}, u32[]{:S(2)}) %all-to-all-start.2) | async-done | bytes 544 | tf_op jit(solution)/shard_map/all_to_all | solution.py:26
  57.9 3.6 %all-to-all-start.1 = ((bf16[4,2112,128]{2,1,0:T(8,128)(2,1)}), bf16[4,2112,128]{2,1,0:T(8,128)(2,1)S(1)}, u32[]{:S(2)}, u32[]{:S(2)}) async-start(bf16[4,2112,128]{2,1,0:T(8,128)(2,1)} %pad_maximum_fusion), calls=%async_computation.1 | async-start | bytes 4325376 | tf_op jit(solution)/shard_map/all_to_all | solution.py:221
  62.6 1.2 gather_fusion
  64.4 22.9 %all-to-all-done.1 = bf16[4,2112,128]{2,1,0:T(8,128)(2,1)S(1)} async-done(((bf16[4,2112,128]{2,1,0:T(8,128)(2,1)}), bf16[4,2112,128]{2,1,0:T(8,128)(2,1)S(1)}, u32[]{:S(2)}, u32[]{:S(2)}) %all-to-all-start.1) | async-done | bytes 2162720 | tf_op jit(solution)/shard_map/all_to_all | solution.py:221
  91.6 2.3 gather_fusion.1
  94.0 9.5 %all_to_all.47 = f32[4,1,33024]{2,1,0:T(1,128)S(1)} all-to-all(f32[4,1,33024]{2,1,0:T(1,128)S(1)} %bitcast.84), channel_id=1, replica_groups=mesh['cols'=128,'mem'=4] {'mem'}, dimensions={0} | all-to-all | bytes 1056768 | tf_op jit(solution)/shard_map/all_to_all | solution.py:81
  104.3 29.4 %all_to_all.48 = f32[128,1,258]{2,1,0:T(1,128)S(1)} all-to-all(f32[128,1,258]{2,1,0:T(1,128)S(1)} %all_to_all.39), channel_id=1, replica_groups=mesh['cols'=128,'mem'=4] {'cols'}, dimensions={0} | all-to-all | bytes 264192 | tf_op jit(solution)/shard_map/all_to_all | solution.py:82
  134.0 26.5 %all_to_all.49 = f32[128,1,258]{2,1,0:T(1,128)S(1)} all-to-all(f32[128,1,258]{2,1,0:T(1,128)S(1)} %broadcast_in_dim.79), channel_id=1, replica_groups=mesh['cols'=128,'mem'=4] {'cols'}, dimensions={0} | all-to-all | bytes 264192 | tf_op jit(solution)/shard_map/all_to_all | solution.py:26
  162.3 4.1 %all-to-all-start.6 = ((f32[4,1,33024]{2,1,0:T(1,128)}), f32[4,1,33024]{2,1,0:T(1,128)}, u32[]{:S(2)}, u32[]{:S(2)}) async-start(f32[4,1,33024]{2,1,0:T(1,128)} %broadcast_in_dim.81), calls=%async_computation.6 | async-start | bytes 1056768 | tf_op jit(solution)/shard_map/all_to_all | solution.py:26
  169.1 1.3 slice.325
  170.4 2.3 reshape.283
  172.8 1.3 copy.142
  176.1 2.4 reduce.25
  179.9 15.2 %shard_map.100 = (f32[128,128]{1,0:T(8,128)}, f32[128,128]{1,0:T(8,128)}) custom-call(f32[128,128]{1,0:T(8,128)} %slice.333.a_ref), custom_call_target="tpu_custom_call" | custom-call | tf_op jit(solution)/shard_map/pallas_call | solution.py:134
  195.0 1.2 fusion.37
  196.3 1.5 maximum_select_fusion
  200.0 15.2 %shard_map.101 = (f32[128,128]{1,0:T(8,128)}, f32[128,128]{1,0:T(8,128)}) custom-call(f32[128,128]{1,0:T(8,128)} %slice.339.a_ref), custom_call_target="tpu_custom_call" | custom-call | tf_op jit(solution)/shard_map/pallas_call | solution.py:134
  217.2 1.4 convolution_subtract_fusion.4
  219.2 15.2 %shard_map.102 = (f32[128,128]{1,0:T(8,128)}, f32[128,128]{1,0:T(8,128)}) custom-call(f32[128,128]{1,0:T(8,128)} %slice.346.a_ref), custom_call_target="tpu_custom_call" | custom-call | tf_op jit(solution)/shard_map/pallas_call | solution.py:134
  234.4 1.1 fusion.49
  235.7 1.4 convolution_subtract_fusion.1
  237.7 2.0 convolution_subtract_fusion.5.a_ref
  239.8 15.2 %shard_map.103 = (f32[128,128]{1,0:T(8,128)}, f32[128,128]{1,0:T(8,128)}) custom-call(f32[128,128]{1,0:T(8,128)} %convolution_subtract_fusion.5.a_ref), custom_call_target="tpu_custom_call" | custom-call | tf_op jit(solution)/shard_map/pallas_call | solution.py:134
  255.3 1.4 convolution_subtract_fusion
  257.1 1.7 convolution_subtract_fusion.2
  (111 shorter events, 32.0 us)
Async XLA Ops:
  0.0 12.7 %copy-start = (bf16[100,256]{1,0:T(8,128)(2,1)S(1)}, bf16[100,256]{1,0:T(8,128)(2,1)}, u32[]{:S(2)}) copy-start(bf16[100,256]{1,0:T(8,128)(2,1)} %param.27) | copy-start | bytes 153604
  1.1 11.6 %collective-permute-start = (bf16[1,100,128]{2,1,0:T(8,128)(2,1)S(1)}, bf16[1,100,128]{2,1,0:T(8,128)(2,1)S(1)}, u32[]{:S(2)}, u32[]{:S(2)}) collective-permute-start(bf16[1,100,128]{2,1,0:T(8,128)(2,1)S(1)} %get-tuple-element.121), channel_id=1, source_target_pairs={{0,4},{4,8},{8,12},{12,16},{16,20},{20,24},{24,28},{28,32},{32,36}... | collective-permute-start | bytes 76808 | tf_op jit(solution)/shard_map/ppermute | solution.py:16
  6.1 6.6 %collective-permute-start.1 = (bf16[1,100,128]{2,1,0:T(8,128)(2,1)S(1)}, bf16[1,100,128]{2,1,0:T(8,128)(2,1)S(1)}, u32[]{:S(2)}, u32[]{:S(2)}) collective-permute-start(bf16[1,100,128]{2,1,0:T(8,128)(2,1)S(1)} %get-tuple-element.122), channel_id=1, source_target_pairs={{4,0},{8,4},{12,8},{16,12},{20,16},{24,20},{28,24},{32,28},{36,32}... | collective-permute-start | bytes 76808 | tf_op jit(solution)/shard_map/ppermute | solution.py:19
  12.7 1.0 copy-start.4
  12.7 1.0 copy-start.14
  13.7 4.7 %copy-start.13 = (s32[128,4]{0,1:T(4,128)S(1)}, s32[128,4]{0,1:T(4,128)}, u32[]{:S(2)}) copy-start(s32[128,4]{0,1:T(4,128)} %param.31) | copy-start | bytes 6148
  13.8 29.5 %copy-start.10 = (f32[100,16]{0,1:T(8,128)S(1)}, f32[100,16]{0,1:T(8,128)}, u32[]{:S(2)}) copy-start(f32[100,16]{0,1:T(8,128)} %param.30) | copy-start | bytes 19204
  14.6 29.5 %copy-start.11 = (f32[128,16]{0,1:T(8,128)S(1)}, f32[128,16]{0,1:T(8,128)}, u32[]{:S(2)}) copy-start(f32[128,16]{0,1:T(8,128)} %param.34) | copy-start | bytes 24580
  15.2 7.6 %all-to-all-start = ((f32[4,16,100]{2,1,0:T(8,128)}), f32[4,16,100]{2,1,0:T(8,128)S(1)}, u32[]{:S(2)}, u32[]{:S(2)}) async-start(f32[4,16,100]{2,1,0:T(8,128)} %broadcast_in_dim.40), calls=%async_computation | async-start | bytes 65536 | tf_op jit(solution)/shard_map/all_to_all | solution.py:26
  23.5 34.4 %all-to-all-start.2 = ((f32[128,1,1]{2,1,0:T(1,128)}), f32[128,1,1]{2,1,0:T(1,128)S(1)}, u32[]{:S(2)}, u32[]{:S(2)}) async-start(f32[128,1,1]{2,1,0:T(1,128)} %broadcast_in_dim.78), calls=%async_computation.2 | async-start | bytes 131072 | tf_op jit(solution)/shard_map/all_to_all | solution.py:26
  47.2 14.3 %copy-start.15 = (s32[128,1]{0,1:T(1,128)S(1)}, s32[128,1]{0,1:T(1,128)}, u32[]{:S(2)}) copy-start(s32[128,1]{0,1:T(1,128)} %param.32) | copy-start | bytes 1540
  47.2 17.0 %copy-start.12 = (f32[128,16]{0,1:T(8,128)S(1)}, f32[128,16]{0,1:T(8,128)}, u32[]{:S(2)}) copy-start(f32[128,16]{0,1:T(8,128)} %param.33) | copy-start | bytes 24580
  57.9 29.3 %all-to-all-start.1 = ((bf16[4,2112,128]{2,1,0:T(8,128)(2,1)}), bf16[4,2112,128]{2,1,0:T(8,128)(2,1)S(1)}, u32[]{:S(2)}, u32[]{:S(2)}) async-start(bf16[4,2112,128]{2,1,0:T(8,128)(2,1)} %pad_maximum_fusion), calls=%async_computation.1 | async-start | bytes 4325376 | tf_op jit(solution)/shard_map/all_to_all | solution.py:221
  89.0 1.0 copy-start.3
  162.3 12.5 %all-to-all-start.6 = ((f32[4,1,33024]{2,1,0:T(1,128)}), f32[4,1,33024]{2,1,0:T(1,128)}, u32[]{:S(2)}, u32[]{:S(2)}) async-start(f32[4,1,33024]{2,1,0:T(1,128)} %broadcast_in_dim.81), calls=%async_computation.6 | async-start | bytes 1056768 | tf_op jit(solution)/shard_map/all_to_all | solution.py:26
  179.2 18.6 %copy-start.2 = (f32[512,512]{1,0:T(8,128)}, f32[512,512]{1,0:T(8,128)S(1)}, u32[]{:S(2)}) copy-start(f32[512,512]{1,0:T(8,128)S(1)} %fusion.12) | copy-start | bytes 3145732
  195.0 3.2 %copy-start.7 = (f32[128,128]{1,0:T(8,128)S(1)}, f32[128,128]{1,0:T(8,128)}, u32[]{:S(2)}) copy-start(f32[128,128]{1,0:T(8,128)} %get-tuple-element.108) | copy-start | bytes 196612
  216.2 38.7 %copy-start.5 = (f32[128,128]{1,0:T(8,128)S(1)}, f32[128,128]{1,0:T(8,128)}, u32[]{:S(2)}) copy-start(f32[128,128]{1,0:T(8,128)} %get-tuple-element.110) | copy-start | bytes 196612
  217.1 17.3 %copy-start.1 = (f32[512,512]{1,0:T(8,128)}, f32[512,512]{1,0:T(8,128)S(1)}, u32[]{:S(2)}) copy-start(f32[512,512]{1,0:T(8,128)S(1)} %maximum_dynamic-update-slice_fusion) | copy-start | bytes 3145732
  234.4 2.6 %copy-start.9 = (f32[128,128]{1,0:T(8,128)S(1)}, f32[128,128]{1,0:T(8,128)}, u32[]{:S(2)}) copy-start(f32[128,128]{1,0:T(8,128)} %get-tuple-element.113) | copy-start | bytes 196612
  235.5 21.2 %copy-start.6 = (f32[128,128]{1,0:T(8,128)S(1)}, f32[128,128]{1,0:T(8,128)}, u32[]{:S(2)}) copy-start(f32[128,128]{1,0:T(8,128)} %get-tuple-element.112) | copy-start | bytes 196612
  254.9 3.9 %copy-start.8 = (f32[128,128]{1,0:T(8,128)S(1)}, f32[128,128]{1,0:T(8,128)}, u32[]{:S(2)}) copy-start(f32[128,128]{1,0:T(8,128)} %get-tuple-element.114) | copy-start | bytes 196612
